TPU v7x, 512 devices: a whole 4x4x16 slice. The times are simulated.
512 devices in a mesh: seg: 16 (over z), exp: 32 (over y, x, core).
Axes of the slice: x: 4, y: 4, z: 16, core: 2. Of those that a mesh axis runs over, the one named last changes fastest.
Arguments:
- queries: bfloat16 [16384, 8192], P('seg', 'exp'), may hold values from -6 to 6
- keys: bfloat16 [16384, 8192], P('seg', 'exp'), may hold values from -0.52734375 to 0.52734375
- values: bfloat16 [16384, 8192], P('seg', 'exp'), may hold values from -2000 to 2000
- log_decay: float32 [64, 16384], P('exp', 'seg'), may hold values from -1 to 0
- gain: float32 [8192], P('exp'), may hold values from 0.5 to 1.5
- d_out: bfloat16 [16384, 8192], P('seg', 'exp'), may hold values from -6 to 6
Outputs:
- out: bfloat16 [16384, 8192], P('seg', 'exp')
- d_queries: bfloat16 [16384, 8192], P('seg', 'exp')
- d_keys: bfloat16 [16384, 8192], P('seg', 'exp')
- d_values: bfloat16 [16384, 8192], P('seg', 'exp')
All inputs are finite; a program needn't handle non-finite values.
Results may differ from a plain program's by a relative error of at most 0.0063.
Values sent between devices are 32-bit elements; how exact they have to be, the bound alone decides.
No kernel may reach another device: no remote copies, remote signals or barrier semaphores. Data moves between devices by JAX's collectives and lax.ppermute only.
A program may use at most 64 MiB of HBM per device.

v0:
```python
import jax
import jax.numpy as jnp
from jax import lax
from jax.sharding import PartitionSpec as P

BLK = 512


EPS = 1e-06


def passed_along(value, axis, steps):
    count = lax.axis_size(axis)
    initial, last = (max(0, -steps), min(count, count - steps))
    return lax.ppermute(value, axis, [(source, source + steps) for source in range(initial, last)])


def decay_parts(log_block):
    cumulative = jnp.cumsum(log_block, axis=-1)
    length = log_block.shape[-1]
    spread = cumulative[..., :, None] - cumulative[..., None, :]
    token_place = jnp.arange(length)
    lower = token_place[:, None] >= token_place[None, :]
    mask = jnp.where(lower, jnp.exp(jnp.minimum(spread, 0.0)), 0.0)
    return (cumulative, cumulative[..., -1], mask)


def body(queries, keys, values, log_decay, gain, d_out):
    rows, width = queries.shape
    local_heads = log_decay.shape[0]
    head_width = width // local_heads
    count = rows // BLK
    shape = (count, BLK, local_heads, head_width)
    qblocks = queries.reshape(shape)
    kblocks = keys.reshape(shape)
    vblocks = values.reshape(shape)
    lblocks = log_decay.reshape(local_heads, count, BLK).transpose(1, 0, 2)
    cumulative, totals, mask = decay_parts(lblocks)
    grow = jnp.exp(cumulative).transpose(0, 2, 1)[..., None]
    shrink = jnp.exp(totals[:, None, :] - cumulative.transpose(0, 2, 1))[..., None]
    scores = (
        jnp.einsum("bthe,bshe->bhts", qblocks, kblocks, preferred_element_type=jnp.float32) * mask
    ).astype(jnp.bfloat16)
    inner = jnp.einsum("bhts,bshf->bthf", scores, vblocks, preferred_element_type=jnp.float32)
    key_weighted = (kblocks * shrink).astype(jnp.bfloat16)
    block_state = jnp.einsum(
        "bshe,bshf->bhef", key_weighted, vblocks, preferred_element_type=jnp.float32
    )
    block_fade = jnp.exp(totals)
    seg_fade = block_fade[0]
    seg_state = block_state[0]
    block = 1
    seg_fade = seg_fade * block_fade[block]
    seg_state = block_fade[block][:, None, None] * seg_state + block_state[block]

    def relay_forward(turn, incoming):
        return passed_along(seg_fade[:, None, None] * incoming + seg_state, "seg", 1)

    entering = lax.fori_loop(0, lax.axis_size("seg") - 1, relay_forward, jnp.zeros_like(seg_state))
    held_list = []
    running = entering
    for block in range(count):
        held_list.append(running.astype(jnp.bfloat16))
        running = block_fade[block][:, None, None] * running + block_state[block]
    held = jnp.stack(held_list)
    attended = inner + grow * jnp.einsum(
        "bthe,bhef->bthf", qblocks, held, preferred_element_type=jnp.float32
    )
    attended = attended.reshape(rows, width)
    upstream = d_out.astype(jnp.float32)
    squares, cross = lax.psum(
        (jnp.sum(attended * attended, axis=-1), jnp.sum(gain * upstream * attended, axis=-1)), "exp"
    )
    features = width * lax.axis_size("exp")
    inv_rms = lax.rsqrt(squares / features + EPS)[:, None]
    out = (attended * inv_rms * gain).astype(jnp.bfloat16)
    grad_attended = (
        gain * upstream * inv_rms
        - attended * inv_rms * inv_rms * inv_rms * cross[:, None] / features
    ).astype(jnp.bfloat16)
    grad_blocks = grad_attended.reshape(shape)
    query_weighted = (qblocks * grow).astype(jnp.bfloat16)
    back_terms = jnp.einsum(
        "bthe,bthf->bhef", query_weighted, grad_blocks, preferred_element_type=jnp.float32
    )
    seg_back = back_terms[count - 1]
    block = 0
    seg_back = back_terms[block] + block_fade[block][:, None, None] * seg_back

    def relay_backward(turn, incoming):
        return passed_along(seg_fade[:, None, None] * incoming + seg_back, "seg", -1)

    leaving = lax.fori_loop(0, lax.axis_size("seg") - 1, relay_backward, jnp.zeros_like(seg_back))
    exit_list = [None] * count
    running = leaving
    for block in range(count - 1, -1, -1):
        exit_list[block] = running.astype(jnp.bfloat16)
        running = back_terms[block] + block_fade[block][:, None, None] * running
    exits = jnp.stack(exit_list)
    grad_scores = (
        jnp.einsum("bthf,bshf->bhts", grad_blocks, vblocks, preferred_element_type=jnp.float32)
        * mask
    ).astype(jnp.bfloat16)
    grad_q = jnp.einsum("bhts,bshe->bthe", grad_scores, kblocks, preferred_element_type=jnp.float32)
    grad_q = grad_q + grow * jnp.einsum(
        "bthf,bhef->bthe", grad_blocks, held, preferred_element_type=jnp.float32
    )
    grad_k = jnp.einsum("bhts,bthe->bshe", grad_scores, qblocks, preferred_element_type=jnp.float32)
    grad_k = grad_k + shrink * jnp.einsum(
        "bshf,bhef->bshe", vblocks, exits, preferred_element_type=jnp.float32
    )
    grad_v = jnp.einsum("bhts,bthf->bshf", scores, grad_blocks, preferred_element_type=jnp.float32)
    grad_v = grad_v + shrink * jnp.einsum(
        "bshe,bhef->bshf", kblocks, exits, preferred_element_type=jnp.float32
    )
    return (
        out,
        grad_q.reshape(rows, width).astype(jnp.bfloat16),
        grad_k.reshape(rows, width).astype(jnp.bfloat16),
        grad_v.reshape(rows, width).astype(jnp.bfloat16),
    )


def solution(mesh):
    in_specs = (
        P("seg", "exp"),
        P("seg", "exp"),
        P("seg", "exp"),
        P("exp", "seg"),
        P("exp"),
        P("seg", "exp"),
    )
    out_specs = (P("seg", "exp"), P("seg", "exp"), P("seg", "exp"), P("seg", "exp"))
    return jax.shard_map(body, mesh=mesh, in_specs=in_specs, out_specs=out_specs, check_vma=False)
```

profile of v0, /device:TPU:96, one launch (start us, length us, event | category | flops | bytes accessed | tf_op | source)
XLA Modules:
  0.0 346.3 jit_solution(417789545744979415)
XLA Ops:
  7.9 125.4 %while.20 = (s32[]{:T(128)}, f32[2,128,128]{2,1,0:T(8,128)S(1)}, f32[2]{0:T(128)S(1)}, f32[2,128,128]{2,1,0:T(8,128)S(1)}, s32[]{:T(128)}) while((s32[]{:T(128)}, f32[2,128,128]{2,1,0:T(8,128)S(1)}, f32[2]{0:T(128)S(1)}, f32[2,128,128]{2,1,0:T(8,128)S(1)}, s32[]{:T(128)}) %tuple.42), condition=%wide.region_3.4_spmd, body=%wide.region_2.3_spmd.sunk | while | flops 65538 | bytes 917613 | solution.py:59
  15.8 5.6 %collective-permute-start = (f32[2,128,128]{2,1,0:T(8,128)S(1)}, f32[2,128,128]{2,1,0:T(8,128)S(1)}, u32[]{:S(2)}, u32[]{:S(2)}) collective-permute-start(f32[2,128,128]{2,1,0:T(8,128)S(1)} %multiply_add_fusion.4), channel_id=1, source_target_pairs={{0,32},{32,64},{64,96},{96,128},{128,160},{160,192},{192,224},{224... | collective-permute-start | bytes 393224 | tf_op jit(solution)/shard_map/while/body/eval_jaxpr/ppermute | solution.py:15
  24.0 5.6 %collective-permute-start = (f32[2,128,128]{2,1,0:T(8,128)S(1)}, f32[2,128,128]{2,1,0:T(8,128)S(1)}, u32[]{:S(2)}, u32[]{:S(2)}) collective-permute-start(f32[2,128,128]{2,1,0:T(8,128)S(1)} %multiply_add_fusion.4), channel_id=1, source_target_pairs={{0,32},{32,64},{64,96},{96,128},{128,160},{160,192},{192,224},{224... | collective-permute-start | bytes 393224 | tf_op jit(solution)/shard_map/while/body/eval_jaxpr/ppermute | solution.py:15
  32.2 5.6 %collective-permute-start = (f32[2,128,128]{2,1,0:T(8,128)S(1)}, f32[2,128,128]{2,1,0:T(8,128)S(1)}, u32[]{:S(2)}, u32[]{:S(2)}) collective-permute-start(f32[2,128,128]{2,1,0:T(8,128)S(1)} %multiply_add_fusion.4), channel_id=1, source_target_pairs={{0,32},{32,64},{64,96},{96,128},{128,160},{160,192},{192,224},{224... | collective-permute-start | bytes 393224 | tf_op jit(solution)/shard_map/while/body/eval_jaxpr/ppermute | solution.py:15
  40.4 5.6 %collective-permute-start = (f32[2,128,128]{2,1,0:T(8,128)S(1)}, f32[2,128,128]{2,1,0:T(8,128)S(1)}, u32[]{:S(2)}, u32[]{:S(2)}) collective-permute-start(f32[2,128,128]{2,1,0:T(8,128)S(1)} %multiply_add_fusion.4), channel_id=1, source_target_pairs={{0,32},{32,64},{64,96},{96,128},{128,160},{160,192},{192,224},{224... | collective-permute-start | bytes 393224 | tf_op jit(solution)/shard_map/while/body/eval_jaxpr/ppermute | solution.py:15
  48.5 5.6 %collective-permute-start = (f32[2,128,128]{2,1,0:T(8,128)S(1)}, f32[2,128,128]{2,1,0:T(8,128)S(1)}, u32[]{:S(2)}, u32[]{:S(2)}) collective-permute-start(f32[2,128,128]{2,1,0:T(8,128)S(1)} %multiply_add_fusion.4), channel_id=1, source_target_pairs={{0,32},{32,64},{64,96},{96,128},{128,160},{160,192},{192,224},{224... | collective-permute-start | bytes 393224 | tf_op jit(solution)/shard_map/while/body/eval_jaxpr/ppermute | solution.py:15
  57.7 5.6 %collective-permute-start = (f32[2,128,128]{2,1,0:T(8,128)S(1)}, f32[2,128,128]{2,1,0:T(8,128)S(1)}, u32[]{:S(2)}, u32[]{:S(2)}) collective-permute-start(f32[2,128,128]{2,1,0:T(8,128)S(1)} %multiply_add_fusion.4), channel_id=1, source_target_pairs={{0,32},{32,64},{64,96},{96,128},{128,160},{160,192},{192,224},{224... | collective-permute-start | bytes 393224 | tf_op jit(solution)/shard_map/while/body/eval_jaxpr/ppermute | solution.py:15
  66.4 5.6 %collective-permute-start = (f32[2,128,128]{2,1,0:T(8,128)S(1)}, f32[2,128,128]{2,1,0:T(8,128)S(1)}, u32[]{:S(2)}, u32[]{:S(2)}) collective-permute-start(f32[2,128,128]{2,1,0:T(8,128)S(1)} %multiply_add_fusion.4), channel_id=1, source_target_pairs={{0,32},{32,64},{64,96},{96,128},{128,160},{160,192},{192,224},{224... | collective-permute-start | bytes 393224 | tf_op jit(solution)/shard_map/while/body/eval_jaxpr/ppermute | solution.py:15
  74.6 5.6 %collective-permute-start = (f32[2,128,128]{2,1,0:T(8,128)S(1)}, f32[2,128,128]{2,1,0:T(8,128)S(1)}, u32[]{:S(2)}, u32[]{:S(2)}) collective-permute-start(f32[2,128,128]{2,1,0:T(8,128)S(1)} %multiply_add_fusion.4), channel_id=1, source_target_pairs={{0,32},{32,64},{64,96},{96,128},{128,160},{160,192},{192,224},{224... | collective-permute-start | bytes 393224 | tf_op jit(solution)/shard_map/while/body/eval_jaxpr/ppermute | solution.py:15
  82.8 5.6 %collective-permute-start = (f32[2,128,128]{2,1,0:T(8,128)S(1)}, f32[2,128,128]{2,1,0:T(8,128)S(1)}, u32[]{:S(2)}, u32[]{:S(2)}) collective-permute-start(f32[2,128,128]{2,1,0:T(8,128)S(1)} %multiply_add_fusion.4), channel_id=1, source_target_pairs={{0,32},{32,64},{64,96},{96,128},{128,160},{160,192},{192,224},{224... | collective-permute-start | bytes 393224 | tf_op jit(solution)/shard_map/while/body/eval_jaxpr/ppermute | solution.py:15
  90.9 5.6 %collective-permute-start = (f32[2,128,128]{2,1,0:T(8,128)S(1)}, f32[2,128,128]{2,1,0:T(8,128)S(1)}, u32[]{:S(2)}, u32[]{:S(2)}) collective-permute-start(f32[2,128,128]{2,1,0:T(8,128)S(1)} %multiply_add_fusion.4), channel_id=1, source_target_pairs={{0,32},{32,64},{64,96},{96,128},{128,160},{160,192},{192,224},{224... | collective-permute-start | bytes 393224 | tf_op jit(solution)/shard_map/while/body/eval_jaxpr/ppermute | solution.py:15
  99.1 5.6 %collective-permute-start = (f32[2,128,128]{2,1,0:T(8,128)S(1)}, f32[2,128,128]{2,1,0:T(8,128)S(1)}, u32[]{:S(2)}, u32[]{:S(2)}) collective-permute-start(f32[2,128,128]{2,1,0:T(8,128)S(1)} %multiply_add_fusion.4), channel_id=1, source_target_pairs={{0,32},{32,64},{64,96},{96,128},{128,160},{160,192},{192,224},{224... | collective-permute-start | bytes 393224 | tf_op jit(solution)/shard_map/while/body/eval_jaxpr/ppermute | solution.py:15
  107.9 5.6 %collective-permute-start = (f32[2,128,128]{2,1,0:T(8,128)S(1)}, f32[2,128,128]{2,1,0:T(8,128)S(1)}, u32[]{:S(2)}, u32[]{:S(2)}) collective-permute-start(f32[2,128,128]{2,1,0:T(8,128)S(1)} %multiply_add_fusion.4), channel_id=1, source_target_pairs={{0,32},{32,64},{64,96},{96,128},{128,160},{160,192},{192,224},{224... | collective-permute-start | bytes 393224 | tf_op jit(solution)/shard_map/while/body/eval_jaxpr/ppermute | solution.py:15
  117.0 5.6 %collective-permute-start = (f32[2,128,128]{2,1,0:T(8,128)S(1)}, f32[2,128,128]{2,1,0:T(8,128)S(1)}, u32[]{:S(2)}, u32[]{:S(2)}) collective-permute-start(f32[2,128,128]{2,1,0:T(8,128)S(1)} %multiply_add_fusion.4), channel_id=1, source_target_pairs={{0,32},{32,64},{64,96},{96,128},{128,160},{160,192},{192,224},{224... | collective-permute-start | bytes 393224 | tf_op jit(solution)/shard_map/while/body/eval_jaxpr/ppermute | solution.py:15
  125.2 5.6 %collective-permute-start = (f32[2,128,128]{2,1,0:T(8,128)S(1)}, f32[2,128,128]{2,1,0:T(8,128)S(1)}, u32[]{:S(2)}, u32[]{:S(2)}) collective-permute-start(f32[2,128,128]{2,1,0:T(8,128)S(1)} %multiply_add_fusion.4), channel_id=1, source_target_pairs={{0,32},{32,64},{64,96},{96,128},{128,160},{160,192},{192,224},{224... | collective-permute-start | bytes 393224 | tf_op jit(solution)/shard_map/while/body/eval_jaxpr/ppermute | solution.py:15
  141.7 63.7 %all-reduce = (f32[1024]{0:T(1024)S(1)}, f32[1024]{0:T(1024)S(1)}) all-reduce(f32[1024]{0:T(1024)S(1)} %bitcast.133, f32[1024]{0:T(1024)S(1)} %fusion.11), channel_id=1, replica_groups=mesh['seg'=16,'exp'=32] {'exp'}, use_global_device_ids=true, to_apply=%region_5.6 | all-reduce | flops 2048 | bytes 16384 | tf_op jit(solution)/shard_map/psum | solution.py:71
  211.8 126.6 %while.21 = (s32[]{:T(128)}, f32[2,128,128]{2,1,0:T(8,128)S(1)}, f32[2]{0:T(128)S(1)}, f32[2,128,128]{2,1,0:T(8,128)S(1)}, s32[]{:T(128)}) while((s32[]{:T(128)}, f32[2,128,128]{2,1,0:T(8,128)S(1)}, f32[2]{0:T(128)S(1)}, f32[2,128,128]{2,1,0:T(8,128)S(1)}, s32[]{:T(128)}) %tuple.48), condition=%wide.region_9.10_spmd, body=%wide.region_8.9_spmd.sunk | while | flops 65538 | bytes 917613 | solution.py:93
  213.8 7.4 %collective-permute-done.1 = f32[2,128,128]{2,1,0:T(8,128)S(1)} collective-permute-done((f32[2,128,128]{2,1,0:T(8,128)S(1)}, f32[2,128,128]{2,1,0:T(8,128)S(1)}, u32[]{:S(2)}, u32[]{:S(2)}) %collective-permute-start.1) | collective-permute-done | bytes 131104 | tf_op jit(solution)/shard_map/while/body/eval_jaxpr/ppermute | solution.py:15
  223.2 6.1 %collective-permute-done.1 = f32[2,128,128]{2,1,0:T(8,128)S(1)} collective-permute-done((f32[2,128,128]{2,1,0:T(8,128)S(1)}, f32[2,128,128]{2,1,0:T(8,128)S(1)}, u32[]{:S(2)}, u32[]{:S(2)}) %collective-permute-start.1) | collective-permute-done | bytes 131104 | tf_op jit(solution)/shard_map/while/body/eval_jaxpr/ppermute | solution.py:15
  231.4 6.1 %collective-permute-done.1 = f32[2,128,128]{2,1,0:T(8,128)S(1)} collective-permute-done((f32[2,128,128]{2,1,0:T(8,128)S(1)}, f32[2,128,128]{2,1,0:T(8,128)S(1)}, u32[]{:S(2)}, u32[]{:S(2)}) %collective-permute-start.1) | collective-permute-done | bytes 131104 | tf_op jit(solution)/shard_map/while/body/eval_jaxpr/ppermute | solution.py:15
  239.5 6.1 %collective-permute-done.1 = f32[2,128,128]{2,1,0:T(8,128)S(1)} collective-permute-done((f32[2,128,128]{2,1,0:T(8,128)S(1)}, f32[2,128,128]{2,1,0:T(8,128)S(1)}, u32[]{:S(2)}, u32[]{:S(2)}) %collective-permute-start.1) | collective-permute-done | bytes 131104 | tf_op jit(solution)/shard_map/while/body/eval_jaxpr/ppermute | solution.py:15
  247.7 6.1 %collective-permute-done.1 = f32[2,128,128]{2,1,0:T(8,128)S(1)} collective-permute-done((f32[2,128,128]{2,1,0:T(8,128)S(1)}, f32[2,128,128]{2,1,0:T(8,128)S(1)}, u32[]{:S(2)}, u32[]{:S(2)}) %collective-permute-start.1) | collective-permute-done | bytes 131104 | tf_op jit(solution)/shard_map/while/body/eval_jaxpr/ppermute | solution.py:15
  255.8 6.5 %collective-permute-done.1 = f32[2,128,128]{2,1,0:T(8,128)S(1)} collective-permute-done((f32[2,128,128]{2,1,0:T(8,128)S(1)}, f32[2,128,128]{2,1,0:T(8,128)S(1)}, u32[]{:S(2)}, u32[]{:S(2)}) %collective-permute-start.1) | collective-permute-done | bytes 131104 | tf_op jit(solution)/shard_map/while/body/eval_jaxpr/ppermute | solution.py:15
  264.4 7.4 %collective-permute-done.1 = f32[2,128,128]{2,1,0:T(8,128)S(1)} collective-permute-done((f32[2,128,128]{2,1,0:T(8,128)S(1)}, f32[2,128,128]{2,1,0:T(8,128)S(1)}, u32[]{:S(2)}, u32[]{:S(2)}) %collective-permute-start.1) | collective-permute-done | bytes 131104 | tf_op jit(solution)/shard_map/while/body/eval_jaxpr/ppermute | solution.py:15
  273.8 6.5 %collective-permute-done.1 = f32[2,128,128]{2,1,0:T(8,128)S(1)} collective-permute-done((f32[2,128,128]{2,1,0:T(8,128)S(1)}, f32[2,128,128]{2,1,0:T(8,128)S(1)}, u32[]{:S(2)}, u32[]{:S(2)}) %collective-permute-start.1) | collective-permute-done | bytes 131104 | tf_op jit(solution)/shard_map/while/body/eval_jaxpr/ppermute | solution.py:15
  282.4 6.1 %collective-permute-done.1 = f32[2,128,128]{2,1,0:T(8,128)S(1)} collective-permute-done((f32[2,128,128]{2,1,0:T(8,128)S(1)}, f32[2,128,128]{2,1,0:T(8,128)S(1)}, u32[]{:S(2)}, u32[]{:S(2)}) %collective-permute-start.1) | collective-permute-done | bytes 131104 | tf_op jit(solution)/shard_map/while/body/eval_jaxpr/ppermute | solution.py:15
  290.5 6.1 %collective-permute-done.1 = f32[2,128,128]{2,1,0:T(8,128)S(1)} collective-permute-done((f32[2,128,128]{2,1,0:T(8,128)S(1)}, f32[2,128,128]{2,1,0:T(8,128)S(1)}, u32[]{:S(2)}, u32[]{:S(2)}) %collective-permute-start.1) | collective-permute-done | bytes 131104 | tf_op jit(solution)/shard_map/while/body/eval_jaxpr/ppermute | solution.py:15
  298.7 6.1 %collective-permute-done.1 = f32[2,128,128]{2,1,0:T(8,128)S(1)} collective-permute-done((f32[2,128,128]{2,1,0:T(8,128)S(1)}, f32[2,128,128]{2,1,0:T(8,128)S(1)}, u32[]{:S(2)}, u32[]{:S(2)}) %collective-permute-start.1) | collective-permute-done | bytes 131104 | tf_op jit(solution)/shard_map/while/body/eval_jaxpr/ppermute | solution.py:15
  306.8 6.1 %collective-permute-done.1 = f32[2,128,128]{2,1,0:T(8,128)S(1)} collective-permute-done((f32[2,128,128]{2,1,0:T(8,128)S(1)}, f32[2,128,128]{2,1,0:T(8,128)S(1)}, u32[]{:S(2)}, u32[]{:S(2)}) %collective-permute-start.1) | collective-permute-done | bytes 131104 | tf_op jit(solution)/shard_map/while/body/eval_jaxpr/ppermute | solution.py:15
  315.0 7.1 %collective-permute-done.1 = f32[2,128,128]{2,1,0:T(8,128)S(1)} collective-permute-done((f32[2,128,128]{2,1,0:T(8,128)S(1)}, f32[2,128,128]{2,1,0:T(8,128)S(1)}, u32[]{:S(2)}, u32[]{:S(2)}) %collective-permute-start.1) | collective-permute-done | bytes 131104 | tf_op jit(solution)/shard_map/while/body/eval_jaxpr/ppermute | solution.py:15
  324.0 6.1 %collective-permute-done.1 = f32[2,128,128]{2,1,0:T(8,128)S(1)} collective-permute-done((f32[2,128,128]{2,1,0:T(8,128)S(1)}, f32[2,128,128]{2,1,0:T(8,128)S(1)}, u32[]{:S(2)}, u32[]{:S(2)}) %collective-permute-start.1) | collective-permute-done | bytes 131104 | tf_op jit(solution)/shard_map/while/body/eval_jaxpr/ppermute | solution.py:15
  332.2 6.1 %collective-permute-done.1 = f32[2,128,128]{2,1,0:T(8,128)S(1)} collective-permute-done((f32[2,128,128]{2,1,0:T(8,128)S(1)}, f32[2,128,128]{2,1,0:T(8,128)S(1)}, u32[]{:S(2)}, u32[]{:S(2)}) %collective-permute-start.1) | collective-permute-done | bytes 131104 | tf_op jit(solution)/shard_map/while/body/eval_jaxpr/ppermute | solution.py:15
  (130 shorter events, 106.7 us)
Async XLA Ops:
  6.8 129.9 %copy-start.2 = (bf16[2,512,2,128]{3,2,1,0:T(2,128)(2,1)}, bf16[2,512,2,128]{3,2,1,0:T(2,128)(2,1)S(1)}, u32[]{:S(2)}) copy-start(bf16[2,512,2,128]{3,2,1,0:T(2,128)(2,1)S(1)} %reshape.82) | copy-start | bytes 1572868
  8.0 7.8 %collective-permute-start = (f32[2,128,128]{2,1,0:T(8,128)S(1)}, f32[2,128,128]{2,1,0:T(8,128)S(1)}, u32[]{:S(2)}, u32[]{:S(2)}) collective-permute-start(f32[2,128,128]{2,1,0:T(8,128)S(1)} %multiply_add_fusion.4), channel_id=1, source_target_pairs={{0,32},{32,64},{64,96},{96,128},{128,160},{160,192},{192,224},{224... | collective-permute-start | bytes 393224 | tf_op jit(solution)/shard_map/while/body/eval_jaxpr/ppermute | solution.py:15
  15.8 8.1 %collective-permute-start = (f32[2,128,128]{2,1,0:T(8,128)S(1)}, f32[2,128,128]{2,1,0:T(8,128)S(1)}, u32[]{:S(2)}, u32[]{:S(2)}) collective-permute-start(f32[2,128,128]{2,1,0:T(8,128)S(1)} %multiply_add_fusion.4), channel_id=1, source_target_pairs={{0,32},{32,64},{64,96},{96,128},{128,160},{160,192},{192,224},{224... | collective-permute-start | bytes 393224 | tf_op jit(solution)/shard_map/while/body/eval_jaxpr/ppermute | solution.py:15
  24.0 8.1 %collective-permute-start = (f32[2,128,128]{2,1,0:T(8,128)S(1)}, f32[2,128,128]{2,1,0:T(8,128)S(1)}, u32[]{:S(2)}, u32[]{:S(2)}) collective-permute-start(f32[2,128,128]{2,1,0:T(8,128)S(1)} %multiply_add_fusion.4), channel_id=1, source_target_pairs={{0,32},{32,64},{64,96},{96,128},{128,160},{160,192},{192,224},{224... | collective-permute-start | bytes 393224 | tf_op jit(solution)/shard_map/while/body/eval_jaxpr/ppermute | solution.py:15
  32.2 8.1 %collective-permute-start = (f32[2,128,128]{2,1,0:T(8,128)S(1)}, f32[2,128,128]{2,1,0:T(8,128)S(1)}, u32[]{:S(2)}, u32[]{:S(2)}) collective-permute-start(f32[2,128,128]{2,1,0:T(8,128)S(1)} %multiply_add_fusion.4), channel_id=1, source_target_pairs={{0,32},{32,64},{64,96},{96,128},{128,160},{160,192},{192,224},{224... | collective-permute-start | bytes 393224 | tf_op jit(solution)/shard_map/while/body/eval_jaxpr/ppermute | solution.py:15
  40.4 8.1 %collective-permute-start = (f32[2,128,128]{2,1,0:T(8,128)S(1)}, f32[2,128,128]{2,1,0:T(8,128)S(1)}, u32[]{:S(2)}, u32[]{:S(2)}) collective-permute-start(f32[2,128,128]{2,1,0:T(8,128)S(1)} %multiply_add_fusion.4), channel_id=1, source_target_pairs={{0,32},{32,64},{64,96},{96,128},{128,160},{160,192},{192,224},{224... | collective-permute-start | bytes 393224 | tf_op jit(solution)/shard_map/while/body/eval_jaxpr/ppermute | solution.py:15
  48.5 9.1 %collective-permute-start = (f32[2,128,128]{2,1,0:T(8,128)S(1)}, f32[2,128,128]{2,1,0:T(8,128)S(1)}, u32[]{:S(2)}, u32[]{:S(2)}) collective-permute-start(f32[2,128,128]{2,1,0:T(8,128)S(1)} %multiply_add_fusion.4), channel_id=1, source_target_pairs={{0,32},{32,64},{64,96},{96,128},{128,160},{160,192},{192,224},{224... | collective-permute-start | bytes 393224 | tf_op jit(solution)/shard_map/while/body/eval_jaxpr/ppermute | solution.py:15
  57.7 8.6 %collective-permute-start = (f32[2,128,128]{2,1,0:T(8,128)S(1)}, f32[2,128,128]{2,1,0:T(8,128)S(1)}, u32[]{:S(2)}, u32[]{:S(2)}) collective-permute-start(f32[2,128,128]{2,1,0:T(8,128)S(1)} %multiply_add_fusion.4), channel_id=1, source_target_pairs={{0,32},{32,64},{64,96},{96,128},{128,160},{160,192},{192,224},{224... | collective-permute-start | bytes 393224 | tf_op jit(solution)/shard_map/while/body/eval_jaxpr/ppermute | solution.py:15
  66.4 8.1 %collective-permute-start = (f32[2,128,128]{2,1,0:T(8,128)S(1)}, f32[2,128,128]{2,1,0:T(8,128)S(1)}, u32[]{:S(2)}, u32[]{:S(2)}) collective-permute-start(f32[2,128,128]{2,1,0:T(8,128)S(1)} %multiply_add_fusion.4), channel_id=1, source_target_pairs={{0,32},{32,64},{64,96},{96,128},{128,160},{160,192},{192,224},{224... | collective-permute-start | bytes 393224 | tf_op jit(solution)/shard_map/while/body/eval_jaxpr/ppermute | solution.py:15
  74.6 8.1 %collective-permute-start = (f32[2,128,128]{2,1,0:T(8,128)S(1)}, f32[2,128,128]{2,1,0:T(8,128)S(1)}, u32[]{:S(2)}, u32[]{:S(2)}) collective-permute-start(f32[2,128,128]{2,1,0:T(8,128)S(1)} %multiply_add_fusion.4), channel_id=1, source_target_pairs={{0,32},{32,64},{64,96},{96,128},{128,160},{160,192},{192,224},{224... | collective-permute-start | bytes 393224 | tf_op jit(solution)/shard_map/while/body/eval_jaxpr/ppermute | solution.py:15
  82.8 8.1 %collective-permute-start = (f32[2,128,128]{2,1,0:T(8,128)S(1)}, f32[2,128,128]{2,1,0:T(8,128)S(1)}, u32[]{:S(2)}, u32[]{:S(2)}) collective-permute-start(f32[2,128,128]{2,1,0:T(8,128)S(1)} %multiply_add_fusion.4), channel_id=1, source_target_pairs={{0,32},{32,64},{64,96},{96,128},{128,160},{160,192},{192,224},{224... | collective-permute-start | bytes 393224 | tf_op jit(solution)/shard_map/while/body/eval_jaxpr/ppermute | solution.py:15
  90.9 8.1 %collective-permute-start = (f32[2,128,128]{2,1,0:T(8,128)S(1)}, f32[2,128,128]{2,1,0:T(8,128)S(1)}, u32[]{:S(2)}, u32[]{:S(2)}) collective-permute-start(f32[2,128,128]{2,1,0:T(8,128)S(1)} %multiply_add_fusion.4), channel_id=1, source_target_pairs={{0,32},{32,64},{64,96},{96,128},{128,160},{160,192},{192,224},{224... | collective-permute-start | bytes 393224 | tf_op jit(solution)/shard_map/while/body/eval_jaxpr/ppermute | solution.py:15
  99.1 8.7 %collective-permute-start = (f32[2,128,128]{2,1,0:T(8,128)S(1)}, f32[2,128,128]{2,1,0:T(8,128)S(1)}, u32[]{:S(2)}, u32[]{:S(2)}) collective-permute-start(f32[2,128,128]{2,1,0:T(8,128)S(1)} %multiply_add_fusion.4), channel_id=1, source_target_pairs={{0,32},{32,64},{64,96},{96,128},{128,160},{160,192},{192,224},{224... | collective-permute-start | bytes 393224 | tf_op jit(solution)/shard_map/while/body/eval_jaxpr/ppermute | solution.py:15
  107.9 9.0 %collective-permute-start = (f32[2,128,128]{2,1,0:T(8,128)S(1)}, f32[2,128,128]{2,1,0:T(8,128)S(1)}, u32[]{:S(2)}, u32[]{:S(2)}) collective-permute-start(f32[2,128,128]{2,1,0:T(8,128)S(1)} %multiply_add_fusion.4), channel_id=1, source_target_pairs={{0,32},{32,64},{64,96},{96,128},{128,160},{160,192},{192,224},{224... | collective-permute-start | bytes 393224 | tf_op jit(solution)/shard_map/while/body/eval_jaxpr/ppermute | solution.py:15
  117.0 8.1 %collective-permute-start = (f32[2,128,128]{2,1,0:T(8,128)S(1)}, f32[2,128,128]{2,1,0:T(8,128)S(1)}, u32[]{:S(2)}, u32[]{:S(2)}) collective-permute-start(f32[2,128,128]{2,1,0:T(8,128)S(1)} %multiply_add_fusion.4), channel_id=1, source_target_pairs={{0,32},{32,64},{64,96},{96,128},{128,160},{160,192},{192,224},{224... | collective-permute-start | bytes 393224 | tf_op jit(solution)/shard_map/while/body/eval_jaxpr/ppermute | solution.py:15
  125.2 8.1 %collective-permute-start = (f32[2,128,128]{2,1,0:T(8,128)S(1)}, f32[2,128,128]{2,1,0:T(8,128)S(1)}, u32[]{:S(2)}, u32[]{:S(2)}) collective-permute-start(f32[2,128,128]{2,1,0:T(8,128)S(1)} %multiply_add_fusion.4), channel_id=1, source_target_pairs={{0,32},{32,64},{64,96},{96,128},{128,160},{160,192},{192,224},{224... | collective-permute-start | bytes 393224 | tf_op jit(solution)/shard_map/while/body/eval_jaxpr/ppermute | solution.py:15
  211.4 127.1 %copy-start.6 = (f32[2,512,2,128]{3,1,2,0:T(8,128)S(1)}, f32[2,512,2,128]{3,1,2,0:T(8,128)}, u32[]{:S(2)}) copy-start(f32[2,512,2,128]{3,1,2,0:T(8,128)} %convolution_bitcast_fusion) | copy-start | bytes 3145732
  211.9 9.3 %collective-permute-start.1 = (f32[2,128,128]{2,1,0:T(8,128)S(1)}, f32[2,128,128]{2,1,0:T(8,128)S(1)}, u32[]{:S(2)}, u32[]{:S(2)}) collective-permute-start(f32[2,128,128]{2,1,0:T(8,128)S(1)} %multiply_add_fusion.5), channel_id=1, source_target_pairs={{32,0},{64,32},{96,64},{128,96},{160,128},{192,160},{224,192},{256... | collective-permute-start | bytes 393224 | tf_op jit(solution)/shard_map/while/body/eval_jaxpr/ppermute | solution.py:15
  221.3 8.1 %collective-permute-start.1 = (f32[2,128,128]{2,1,0:T(8,128)S(1)}, f32[2,128,128]{2,1,0:T(8,128)S(1)}, u32[]{:S(2)}, u32[]{:S(2)}) collective-permute-start(f32[2,128,128]{2,1,0:T(8,128)S(1)} %multiply_add_fusion.5), channel_id=1, source_target_pairs={{32,0},{64,32},{96,64},{128,96},{160,128},{192,160},{224,192},{256... | collective-permute-start | bytes 393224 | tf_op jit(solution)/shard_map/while/body/eval_jaxpr/ppermute | solution.py:15
  229.4 8.1 %collective-permute-start.1 = (f32[2,128,128]{2,1,0:T(8,128)S(1)}, f32[2,128,128]{2,1,0:T(8,128)S(1)}, u32[]{:S(2)}, u32[]{:S(2)}) collective-permute-start(f32[2,128,128]{2,1,0:T(8,128)S(1)} %multiply_add_fusion.5), channel_id=1, source_target_pairs={{32,0},{64,32},{96,64},{128,96},{160,128},{192,160},{224,192},{256... | collective-permute-start | bytes 393224 | tf_op jit(solution)/shard_map/while/body/eval_jaxpr/ppermute | solution.py:15
  237.6 8.1 %collective-permute-start.1 = (f32[2,128,128]{2,1,0:T(8,128)S(1)}, f32[2,128,128]{2,1,0:T(8,128)S(1)}, u32[]{:S(2)}, u32[]{:S(2)}) collective-permute-start(f32[2,128,128]{2,1,0:T(8,128)S(1)} %multiply_add_fusion.5), channel_id=1, source_target_pairs={{32,0},{64,32},{96,64},{128,96},{160,128},{192,160},{224,192},{256... | collective-permute-start | bytes 393224 | tf_op jit(solution)/shard_map/while/body/eval_jaxpr/ppermute | solution.py:15
  245.7 8.1 %collective-permute-start.1 = (f32[2,128,128]{2,1,0:T(8,128)S(1)}, f32[2,128,128]{2,1,0:T(8,128)S(1)}, u32[]{:S(2)}, u32[]{:S(2)}) collective-permute-start(f32[2,128,128]{2,1,0:T(8,128)S(1)} %multiply_add_fusion.5), channel_id=1, source_target_pairs={{32,0},{64,32},{96,64},{128,96},{160,128},{192,160},{224,192},{256... | collective-permute-start | bytes 393224 | tf_op jit(solution)/shard_map/while/body/eval_jaxpr/ppermute | solution.py:15
  253.9 8.5 %collective-permute-start.1 = (f32[2,128,128]{2,1,0:T(8,128)S(1)}, f32[2,128,128]{2,1,0:T(8,128)S(1)}, u32[]{:S(2)}, u32[]{:S(2)}) collective-permute-start(f32[2,128,128]{2,1,0:T(8,128)S(1)} %multiply_add_fusion.5), channel_id=1, source_target_pairs={{32,0},{64,32},{96,64},{128,96},{160,128},{192,160},{224,192},{256... | collective-permute-start | bytes 393224 | tf_op jit(solution)/shard_map/while/body/eval_jaxpr/ppermute | solution.py:15
  262.4 9.3 %collective-permute-start.1 = (f32[2,128,128]{2,1,0:T(8,128)S(1)}, f32[2,128,128]{2,1,0:T(8,128)S(1)}, u32[]{:S(2)}, u32[]{:S(2)}) collective-permute-start(f32[2,128,128]{2,1,0:T(8,128)S(1)} %multiply_add_fusion.5), channel_id=1, source_target_pairs={{32,0},{64,32},{96,64},{128,96},{160,128},{192,160},{224,192},{256... | collective-permute-start | bytes 393224 | tf_op jit(solution)/shard_map/while/body/eval_jaxpr/ppermute | solution.py:15
  271.9 8.5 %collective-permute-start.1 = (f32[2,128,128]{2,1,0:T(8,128)S(1)}, f32[2,128,128]{2,1,0:T(8,128)S(1)}, u32[]{:S(2)}, u32[]{:S(2)}) collective-permute-start(f32[2,128,128]{2,1,0:T(8,128)S(1)} %multiply_add_fusion.5), channel_id=1, source_target_pairs={{32,0},{64,32},{96,64},{128,96},{160,128},{192,160},{224,192},{256... | collective-permute-start | bytes 393224 | tf_op jit(solution)/shard_map/while/body/eval_jaxpr/ppermute | solution.py:15
  280.4 8.1 %collective-permute-start.1 = (f32[2,128,128]{2,1,0:T(8,128)S(1)}, f32[2,128,128]{2,1,0:T(8,128)S(1)}, u32[]{:S(2)}, u32[]{:S(2)}) collective-permute-start(f32[2,128,128]{2,1,0:T(8,128)S(1)} %multiply_add_fusion.5), channel_id=1, source_target_pairs={{32,0},{64,32},{96,64},{128,96},{160,128},{192,160},{224,192},{256... | collective-permute-start | bytes 393224 | tf_op jit(solution)/shard_map/while/body/eval_jaxpr/ppermute | solution.py:15
  288.6 8.1 %collective-permute-start.1 = (f32[2,128,128]{2,1,0:T(8,128)S(1)}, f32[2,128,128]{2,1,0:T(8,128)S(1)}, u32[]{:S(2)}, u32[]{:S(2)}) collective-permute-start(f32[2,128,128]{2,1,0:T(8,128)S(1)} %multiply_add_fusion.5), channel_id=1, source_target_pairs={{32,0},{64,32},{96,64},{128,96},{160,128},{192,160},{224,192},{256... | collective-permute-start | bytes 393224 | tf_op jit(solution)/shard_map/while/body/eval_jaxpr/ppermute | solution.py:15
  296.7 8.1 %collective-permute-start.1 = (f32[2,128,128]{2,1,0:T(8,128)S(1)}, f32[2,128,128]{2,1,0:T(8,128)S(1)}, u32[]{:S(2)}, u32[]{:S(2)}) collective-permute-start(f32[2,128,128]{2,1,0:T(8,128)S(1)} %multiply_add_fusion.5), channel_id=1, source_target_pairs={{32,0},{64,32},{96,64},{128,96},{160,128},{192,160},{224,192},{256... | collective-permute-start | bytes 393224 | tf_op jit(solution)/shard_map/while/body/eval_jaxpr/ppermute | solution.py:15
  304.9 8.1 %collective-permute-start.1 = (f32[2,128,128]{2,1,0:T(8,128)S(1)}, f32[2,128,128]{2,1,0:T(8,128)S(1)}, u32[]{:S(2)}, u32[]{:S(2)}) collective-permute-start(f32[2,128,128]{2,1,0:T(8,128)S(1)} %multiply_add_fusion.5), channel_id=1, source_target_pairs={{32,0},{64,32},{96,64},{128,96},{160,128},{192,160},{224,192},{256... | collective-permute-start | bytes 393224 | tf_op jit(solution)/shard_map/while/body/eval_jaxpr/ppermute | solution.py:15
  313.0 9.0 %collective-permute-start.1 = (f32[2,128,128]{2,1,0:T(8,128)S(1)}, f32[2,128,128]{2,1,0:T(8,128)S(1)}, u32[]{:S(2)}, u32[]{:S(2)}) collective-permute-start(f32[2,128,128]{2,1,0:T(8,128)S(1)} %multiply_add_fusion.5), channel_id=1, source_target_pairs={{32,0},{64,32},{96,64},{128,96},{160,128},{192,160},{224,192},{256... | collective-permute-start | bytes 393224 | tf_op jit(solution)/shard_map/while/body/eval_jaxpr/ppermute | solution.py:15
  322.1 8.1 %collective-permute-start.1 = (f32[2,128,128]{2,1,0:T(8,128)S(1)}, f32[2,128,128]{2,1,0:T(8,128)S(1)}, u32[]{:S(2)}, u32[]{:S(2)}) collective-permute-start(f32[2,128,128]{2,1,0:T(8,128)S(1)} %multiply_add_fusion.5), channel_id=1, source_target_pairs={{32,0},{64,32},{96,64},{128,96},{160,128},{192,160},{224,192},{256... | collective-permute-start | bytes 393224 | tf_op jit(solution)/shard_map/while/body/eval_jaxpr/ppermute | solution.py:15
  330.3 8.1 %collective-permute-start.1 = (f32[2,128,128]{2,1,0:T(8,128)S(1)}, f32[2,128,128]{2,1,0:T(8,128)S(1)}, u32[]{:S(2)}, u32[]{:S(2)}) collective-permute-start(f32[2,128,128]{2,1,0:T(8,128)S(1)} %multiply_add_fusion.5), channel_id=1, source_target_pairs={{32,0},{64,32},{96,64},{128,96},{160,128},{192,160},{224,192},{256... | collective-permute-start | bytes 393224 | tf_op jit(solution)/shard_map/while/body/eval_jaxpr/ppermute | solution.py:15
  (8 other events, 266.5 us)
where the time goes:
time: 348 us; the launch traced here: 346 us
  waiting for transfers between devices  137 us (39%)
  starting transfers between devices  112 us (32%)
  blocking collectives  63.7 us (18%)
  matrix products  12.2 us (4%)
  local copies, waits for them, and re-layouts  10.9 us (3%)
  other arithmetic  8.96 us (3%)
    ppermute x30, waiting for transfers between devices, passed_along(): lax.ppermute(value, axis, [(source, source + steps) for source in range(i...  137 us
    ppermute x30, starting transfers between devices, passed_along(): lax.ppermute(value, axis, [(source, source + steps) for source in range(i...  112 us
    psum x1, blocking collectives, body(): lax.psum((jnp.sum(attended * attended, axis=-1), jnp.sum(gain * upstream...  63.7 us
  transfers between devices with their start and end apart: 30, of which 30 were waited for; matrix products, arithmetic and copies ran while one was open for 0% of the time, Pallas kernels for 0%

commit v1 on v0

--- a/solution.py
+++ b/solution.py
@@ -7,12 +7,6 @@
 
 
 EPS = 1e-06
-
-
-def passed_along(value, axis, steps):
-    count = lax.axis_size(axis)
-    initial, last = (max(0, -steps), min(count, count - steps))
-    return lax.ppermute(value, axis, [(source, source + steps) for source in range(initial, last)])
 
 
 def decay_parts(log_block):
@@ -47,16 +41,30 @@
         "bshe,bshf->bhef", key_weighted, vblocks, preferred_element_type=jnp.float32
     )
     block_fade = jnp.exp(totals)
-    seg_fade = block_fade[0]
+    seg_count = lax.axis_size("seg")
+    here = lax.axis_index("seg")
     seg_state = block_state[0]
-    block = 1
-    seg_fade = seg_fade * block_fade[block]
-    seg_state = block_fade[block][:, None, None] * seg_state + block_state[block]
-
-    def relay_forward(turn, incoming):
-        return passed_along(seg_fade[:, None, None] * incoming + seg_state, "seg", 1)
-
-    entering = lax.fori_loop(0, lax.axis_size("seg") - 1, relay_forward, jnp.zeros_like(seg_state))
+    for block in range(1, count):
+        seg_state = block_fade[block][:, None, None] * seg_state + block_state[block]
+    seg_log = jnp.sum(log_decay, axis=-1)
+    log_rows = jnp.broadcast_to(seg_log[:, None, None], (local_heads, 8, head_width))
+    gathered = lax.all_gather(jnp.concatenate((seg_state, log_rows), axis=1), "seg")
+    all_states = gathered[:, :, :head_width, :]
+    all_logs = gathered[:, :, head_width, 0]
+    places = jnp.arange(seg_count)
+    between_fwd = (places[:, None] < places[None, :]) & (places[None, :] < here)
+    between_bwd = (places[:, None] > places[None, :]) & (places[None, :] > here)
+    weight_fwd = jnp.where(
+        (places < here)[:, None],
+        jnp.exp(jnp.sum(jnp.where(between_fwd[:, :, None], all_logs[None, :, :], 0.0), axis=1)),
+        0.0,
+    )
+    weight_bwd = jnp.where(
+        (places > here)[:, None],
+        jnp.exp(jnp.sum(jnp.where(between_bwd[:, :, None], all_logs[None, :, :], 0.0), axis=1)),
+        0.0,
+    )
+    entering = jnp.sum(weight_fwd[:, :, None, None] * all_states, axis=0)
     held_list = []
     running = entering
     for block in range(count):
@@ -68,9 +76,11 @@
     )
     attended = attended.reshape(rows, width)
     upstream = d_out.astype(jnp.float32)
-    squares, cross = lax.psum(
-        (jnp.sum(attended * attended, axis=-1), jnp.sum(gain * upstream * attended, axis=-1)), "exp"
+    partial = jnp.stack(
+        (jnp.sum(attended * attended, axis=-1), jnp.sum(gain * upstream * attended, axis=-1))
     )
+    totals_exp = jnp.sum(lax.all_gather(jnp.concatenate((partial, jnp.zeros((6, partial.shape[1]), partial.dtype))), "exp"), axis=0)[:2]
+    squares, cross = totals_exp[0], totals_exp[1]
     features = width * lax.axis_size("exp")
     inv_rms = lax.rsqrt(squares / features + EPS)[:, None]
     out = (attended * inv_rms * gain).astype(jnp.bfloat16)
@@ -84,13 +94,10 @@
         "bthe,bthf->bhef", query_weighted, grad_blocks, preferred_element_type=jnp.float32
     )
     seg_back = back_terms[count - 1]
-    block = 0
-    seg_back = back_terms[block] + block_fade[block][:, None, None] * seg_back
-
-    def relay_backward(turn, incoming):
-        return passed_along(seg_fade[:, None, None] * incoming + seg_back, "seg", -1)
-
-    leaving = lax.fori_loop(0, lax.axis_size("seg") - 1, relay_backward, jnp.zeros_like(seg_back))
+    for block in range(count - 2, -1, -1):
+        seg_back = back_terms[block] + block_fade[block][:, None, None] * seg_back
+    all_backs = lax.all_gather(seg_back, "seg")
+    leaving = jnp.sum(weight_bwd[:, :, None, None] * all_backs, axis=0)
     exit_list = [None] * count
     running = leaving
     for block in range(count - 1, -1, -1):

time: 348 us -> 252 us (0.72)
  the two profiles are of different devices: /device:TPU:96 before, /device:TPU:6 now
where the time goes in v1:
time: 252 us; the launch traced here: 251 us
  waiting for transfers between devices  185 us (73%)
  local copies, waits for them, and re-layouts  20.9 us (8%)
  other arithmetic  16.2 us (6%)
  matrix products  14.9 us (6%)
  between operations  14.2 us (6%)
    all_gather x1, waiting for transfers between devices, body(): lax.all_gather(jnp.concatenate((seg_state, log_rows), axis=1), 'seg')  72.5 us
    all_gather x1, waiting for transfers between devices, body(): all_backs = lax.all_gather(seg_back, 'seg')  57.9 us
    all_gather x1, waiting for transfers between devices, body(): lax.all_gather(jnp.concatenate((partial, jnp.zeros((6, partial.shape[1]),...  54.5 us
    unnamed x48, local copies, waits for them, and re-layouts  5.25 us
  transfers between devices with their start and end apart: 3, of which 3 were waited for; matrix products, arithmetic and copies ran while one was open for 8% of the time, Pallas kernels for 0%

profile of v1, /device:TPU:6, one launch (start us, length us, event | category | flops | bytes accessed | tf_op | source)
XLA Modules:
  0.0 251.4 jit_solution(9528865667513007123)
XLA Ops:
  7.9 0.8 reduce_sum.76
  8.8 1.2 reduce-window.6
  11.4 1.2 reshape.222
  12.7 1.4 reshape.226
  14.0 0.9 fusion.13
  17.3 2.5 %multiply_convert_fusion.1 = bf16[2,2,512,512]{3,2,1,0:T(8,128)(2,1)S(1)} fusion(bf16[2,512,2,128]{1,3,2,0:T(8,128)(2,1)S(1)} %copy.118, f32[2,2,512]{2,1,0:T(2,128)S(1)} %reduce_window_sum.24, pred[512,512]{1,0:T(8,128)(4,1)S(1)} %iota_compare_fusion, bf16[2,512,2,128]{3,2,1,0:T(2,128)(2,1)} %copy-done.6), kind=kOutput, calls=%fused_computation.1 | convolution fusion | flops 273678336 | bytes 3416064 | tf_op jit(solution)/shard_map/bthe,bshe->bhts/dot_general | solution.py:36
  19.9 1.8 convolution_bitcast_fusion.3
  21.7 72.5 %all-gather.8.cloned.1.call-done = f32[32,136,128]{2,1,0:T(8,128)} async-done(((f32[2,136,128]{2,1,0:T(8,128)}), f32[32,136,128]{2,1,0:T(8,128)}) %all-gather.8.cloned.1.call-update) | async-done | bytes 2228240 | tf_op jit(solution)/shard_map/all_gather | solution.py:51
  94.2 0.9 slice.64
  95.9 1.9 fusion
  98.0 1.3 multiply_reduce_fusion.1
  99.3 1.5 copy.109
  100.9 1.3 fusion.12
  103.1 54.5 %all-gather.10.cloned.1.call-done = f32[256,1024]{1,0:T(8,128)} async-done(((f32[8,1024]{1,0:T(8,128)}), f32[256,1024]{1,0:T(8,128)}) %all-gather.10.cloned.1.call-update) | async-done | bytes 1048592 | tf_op jit(solution)/shard_map/all_gather | solution.py:82
  157.5 1.3 bitcast_reduce_fusion
  158.9 2.4 subtract_convert_fusion
  161.3 2.0 reshape.228
  163.3 1.3 copy.124
  164.9 1.4 slice_add_fusion
  166.3 1.2 exponential_select_fusion.1
  167.5 1.3 copy.120
  168.9 2.6 %multiply_convert_fusion = bf16[2,2,512,512]{3,2,1,0:T(8,128)(2,1)S(1)} fusion(bf16[2,512,2,128]{1,3,2,0:T(8,128)(2,1)S(1)} %copy.124, f32[2,2,512]{2,1,0:T(2,128)} %copy-done.13, pred[512,512]{1,0:T(8,128)(4,1)} %copy-done.12, bf16[2,512,2,128]{3,2,1,0:T(2,128)(2,1)} %copy-done.4), kind=kOutput, calls=%fused_computation | convolution fusion | flops 273678336 | bytes 3416064 | tf_op jit(solution)/shard_map/bthf,bshf->bhts/dot_general | solution.py:108
  171.5 1.3 copy-done
  173.6 1.1 fusion.9
  174.7 2.0 copy.115
  176.7 1.9 copy.172
  178.7 1.9 convolution_bitcast_fusion
  180.5 0.9 convolution_bitcast_fusion.1
  181.5 57.9 %all-gather.6.cloned.1.call-done = f32[16,2,128,128]{3,2,1,0:T(8,128)} async-done(((f32[1,2,128,128]{3,2,1,0:T(8,128)}), f32[16,2,128,128]{3,2,1,0:T(8,128)}) %all-gather.6.cloned.1.call-update) | async-done | bytes 2097168 | tf_op jit(solution)/shard_map/all_gather | solution.py:99
  239.3 1.8 multiply_reduce_fusion
  242.2 0.9 copy.170
  244.0 0.9 copy.171
  (87 shorter events, 9.4 us)
Async XLA Ops:
  7.2 87.0 %all-gather.8.cloned.1.call-start = ((), (), s32[]{:S(2)}) async-start(), calls=%async_computation.1 | async-start | bytes 2367488 | tf_op jit(solution)/shard_map/all_gather | solution.py:51
  10.6 6.7 %copy-start.13 = (f32[2,2,512]{2,1,0:T(2,128)}, f32[2,2,512]{2,1,0:T(2,128)S(1)}, u32[]{:S(2)}) copy-start(f32[2,2,512]{2,1,0:T(2,128)S(1)} %reduce_window_sum.24) | copy-start | bytes 24580
  11.3 3.6 %copy-start.15 = (f32[2]{0:T(128)}, f32[2]{0:T(128)S(1)}, u32[]{:S(2)}) copy-start(f32[2]{0:T(128)S(1)} %get-tuple-element.13) | copy-start | bytes 28
  11.4 4.5 %copy-start.11 = (bf16[1024,256]{1,0:T(8,128)(2,1)S(1)}, bf16[1024,256]{1,0:T(8,128)(2,1)}, u32[]{:S(2)}) copy-start(bf16[1024,256]{1,0:T(8,128)(2,1)} %param.6) | copy-start | bytes 1572868
  12.7 3.4 %copy-start.6 = (bf16[2,512,2,128]{3,2,1,0:T(2,128)(2,1)}, bf16[2,512,2,128]{3,2,1,0:T(2,128)(2,1)S(1)}, u32[]{:S(2)}) copy-start(bf16[2,512,2,128]{3,2,1,0:T(2,128)(2,1)S(1)} %reshape.222) | copy-start | bytes 1572868
  14.0 5.8 %copy-start.4 = (bf16[2,512,2,128]{3,2,1,0:T(2,128)(2,1)}, bf16[2,512,2,128]{3,2,1,0:T(2,128)(2,1)S(1)}, u32[]{:S(2)}) copy-start(bf16[2,512,2,128]{3,2,1,0:T(2,128)(2,1)S(1)} %reshape.226) | copy-start | bytes 1572868
  15.8 141.7 %all-gather.10.cloned.1.call-start = ((), (), s32[]{:S(2)}) async-start(), calls=%async_computation.2 | async-start | bytes 1081344 | tf_op jit(solution)/shard_map/all_gather | solution.py:82
  16.5 81.5 %copy-start.2 = (bf16[2,512,2,128]{1,3,2,0:T(8,128)(2,1)}, bf16[2,512,2,128]{1,3,2,0:T(8,128)(2,1)S(1)}, u32[]{:S(2)}) copy-start(bf16[2,512,2,128]{1,3,2,0:T(8,128)(2,1)S(1)} %copy.118) | copy-start | bytes 1572868
  17.1 2.7 %copy-start.19 = (pred[16]{0:T(512)(128)(4,1)}, pred[16]{0:T(512)(128)(4,1)S(1)}, u32[]{:S(2)}) copy-start(pred[16]{0:T(512)(128)(4,1)S(1)} %get-tuple-element.16) | copy-start | bytes 52
  17.2 2.6 %copy-start.12 = (pred[512,512]{1,0:T(8,128)(4,1)}, pred[512,512]{1,0:T(8,128)(4,1)S(1)}, u32[]{:S(2)}) copy-start(pred[512,512]{1,0:T(8,128)(4,1)S(1)} %iota_compare_fusion) | copy-start | bytes 786436
  21.7 76.2 %copy-start.17 = (f32[2]{0:T(128)S(1)}, f32[2]{0:T(128)}, u32[]{:S(2)}) copy-start(f32[2]{0:T(128)} %get-tuple-element.12) | copy-start | bytes 28
  95.9 2.0 copy-start.9
  97.9 2.9 %copy-start.18 = (f32[256]{0:T(256)S(1)}, f32[256]{0:T(256)}, u32[]{:S(2)}) copy-start(f32[256]{0:T(256)} %param.10) | copy-start | bytes 3076
  99.3 2.8 %copy-start.20 = (f32[8]{0:T(128)S(1)}, f32[8]{0:T(128)}, u32[]{:S(2)}) copy-start(f32[8]{0:T(128)} %pad.4.clone) | copy-start | bytes 100
  102.8 136.5 %all-gather.6.cloned.1.call-start = ((), (), s32[]{:S(2)}) async-start(), calls=%async_computation | async-start | bytes 2228224 | tf_op jit(solution)/shard_map/all_gather | solution.py:99
  161.3 3.3 %copy-start.3 = (bf16[2,512,2,128]{1,3,2,0:T(8,128)(2,1)S(1)}, bf16[2,512,2,128]{1,3,2,0:T(8,128)(2,1)}, u32[]{:S(2)}) copy-start(bf16[2,512,2,128]{1,3,2,0:T(8,128)(2,1)} %copy-done.2) | copy-start | bytes 1572868
  168.9 3.9 %copy-start.7 = (bf16[2,512,2,128]{3,2,1,0:T(2,128)(2,1)S(1)}, bf16[2,512,2,128]{3,2,1,0:T(2,128)(2,1)}, u32[]{:S(2)}) copy-start(bf16[2,512,2,128]{3,2,1,0:T(2,128)(2,1)} %copy-done.6) | copy-start | bytes 1572868
  171.5 1.3 copy-start
  178.6 1.9 copy-start.1
  180.5 58.8 %copy-start.14 = (f32[16,2]{1,0:T(8,128)S(1)}, f32[16,2]{1,0:T(8,128)}, u32[]{:S(2)}) copy-start(f32[16,2]{1,0:T(8,128)} %copy.120) | copy-start | bytes 388
  180.5 60.6 %copy-start.16 = (f32[2]{0:T(128)S(1)}, f32[2]{0:T(128)}, u32[]{:S(2)}) copy-start(f32[2]{0:T(128)} %copy-done.15) | copy-start | bytes 28
  181.4 59.8 %copy-start.8 = (bf16[2,512,2,128]{3,2,1,0:T(2,128)(2,1)S(1)}, bf16[2,512,2,128]{3,2,1,0:T(2,128)(2,1)}, u32[]{:S(2)}) copy-start(bf16[2,512,2,128]{3,2,1,0:T(2,128)(2,1)} %copy-done.6) | copy-start | bytes 1572868
  181.4 59.8 %copy-start.10 = (f32[2,512,2,128]{3,1,2,0:T(8,128)S(1)}, f32[2,512,2,128]{3,1,2,0:T(8,128)}, u32[]{:S(2)}) copy-start(f32[2,512,2,128]{3,1,2,0:T(8,128)} %convolution_bitcast_fusion) | copy-start | bytes 3145732
  241.3 1.8 copy-start.5
Sparse Core Ops, SparseCore 0:
  15.9 78.1 all-gather.7
  103.0 54.5 all-gather.9
  166.4 72.8 all-gather.5

commit v2 on v1

--- a/solution.py
+++ b/solution.py
@@ -4,6 +4,7 @@
 from jax.sharding import PartitionSpec as P
 
 BLK = 512
+EXP_PARTS = ("exp_y", "exp_x", "exp_core")
 
 
 EPS = 1e-06
@@ -79,9 +80,11 @@
     partial = jnp.stack(
         (jnp.sum(attended * attended, axis=-1), jnp.sum(gain * upstream * attended, axis=-1))
     )
-    totals_exp = jnp.sum(lax.all_gather(jnp.concatenate((partial, jnp.zeros((6, partial.shape[1]), partial.dtype))), "exp"), axis=0)[:2]
+    totals_exp = partial
+    for axis in EXP_PARTS[::-1]:
+        totals_exp = lax.psum(totals_exp, axis)
     squares, cross = totals_exp[0], totals_exp[1]
-    features = width * lax.axis_size("exp")
+    features = width * lax.axis_size(EXP_PARTS)
     inv_rms = lax.rsqrt(squares / features + EPS)[:, None]
     out = (attended * inv_rms * gain).astype(jnp.bfloat16)
     grad_attended = (
@@ -129,13 +132,9 @@
 
 
 def solution(mesh):
-    in_specs = (
-        P("seg", "exp"),
-        P("seg", "exp"),
-        P("seg", "exp"),
-        P("exp", "seg"),
-        P("exp"),
-        P("seg", "exp"),
-    )
-    out_specs = (P("seg", "exp"), P("seg", "exp"), P("seg", "exp"), P("seg", "exp"))
-    return jax.shard_map(body, mesh=mesh, in_specs=in_specs, out_specs=out_specs, check_vma=False)
+    parts = mesh.devices.reshape(mesh.devices.shape[0], 4, -1, 2)
+    split = jax.sharding.Mesh(parts, ("seg",) + EXP_PARTS)
+    rows_heads = P("seg", EXP_PARTS)
+    in_specs = (rows_heads, rows_heads, rows_heads, P(EXP_PARTS, "seg"), P(EXP_PARTS), rows_heads)
+    out_specs = (rows_heads, rows_heads, rows_heads, rows_heads)
+    return jax.shard_map(body, mesh=split, in_specs=in_specs, out_specs=out_specs, check_vma=False)

time: 252 us -> 212 us (0.84)
  waiting for transfers between devices: 185 us -> 127 us
  blocking collectives: 0 us -> 20.8 us
    all_gather x1 -> x0, waiting for transfers between devices: 54.5 us -> none  [body(): lax.all_gather(jnp.concatenate((partial, jnp.zeros((6, partial.shape[1]),...]
    psum x0 -> x3, blocking collectives: none -> 20.8 us  [body(): totals_exp = lax.psum(totals_exp, axis)]
    all_gather x1, waiting for transfers between devices: 57.9 us -> 53.6 us  [body(): all_backs = lax.all_gather(seg_back, 'seg')]
    unnamed x48 -> x46, local copies, waits for them, and re-layouts: 5.25 us -> 5.24 us
  transfers between devices with their start and end apart: 3 -> 2, of which waited for: 3 -> 2; matrix products, arithmetic and copies ran while one was open for 8% -> 9% of each run, Pallas kernels for 0% -> 0%
where the time goes in v2:
time: 212 us
  waiting for transfers between devices  127 us (60%)
  blocking collectives  20.8 us (10%)
  local copies, waits for them, and re-layouts  20.3 us (10%)
  matrix products  15 us (7%)
  between operations  14.5 us (7%)
  other arithmetic  14.4 us (7%)
    all_gather x1, waiting for transfers between devices, body(): lax.all_gather(jnp.concatenate((seg_state, log_rows), axis=1), 'seg')  73.1 us
    all_gather x1, waiting for transfers between devices, body(): all_backs = lax.all_gather(seg_back, 'seg')  53.6 us
    psum x3, blocking collectives, body(): totals_exp = lax.psum(totals_exp, axis)  20.8 us
    unnamed x46, local copies, waits for them, and re-layouts  5.24 us
  transfers between devices with their start and end apart: 2, of which 2 were waited for; matrix products, arithmetic and copies ran while one was open for 9% of the time, Pallas kernels for 0%

profile of v2, /device:TPU:6, one launch (start us, length us, event | category | flops | bytes accessed | tf_op | source)
XLA Modules:
  0.0 211.8 jit_solution(14159423612587468207)
XLA Ops:
  8.8 1.2 reduce-window.6
  11.5 1.2 reshape.222
  12.7 1.4 reshape.226
  14.1 0.9 fusion.13
  16.7 2.6 %multiply_convert_fusion.1 = bf16[2,2,512,512]{3,2,1,0:T(8,128)(2,1)S(1)} fusion(bf16[2,512,2,128]{1,3,2,0:T(8,128)(2,1)S(1)} %copy.118, f32[2,2,512]{2,1,0:T(2,128)S(1)} %reduce_window_sum.24, pred[512,512]{1,0:T(8,128)(4,1)S(1)} %iota_compare_fusion, bf16[2,512,2,128]{3,2,1,0:T(2,128)(2,1)} %copy-done.6), kind=kOutput, calls=%fused_computation.1 | convolution fusion | flops 273678336 | bytes 3416064 | tf_op jit(solution)/shard_map/bthe,bshe->bhts/dot_general | solution.py:37
  19.3 1.8 convolution_bitcast_fusion.3
  21.2 73.1 %all-gather.6.cloned.1.call-done = f32[32,136,128]{2,1,0:T(8,128)} async-done(((f32[2,136,128]{2,1,0:T(8,128)}), f32[32,136,128]{2,1,0:T(8,128)}) %all-gather.6.cloned.1.call-update) | async-done | bytes 2228240 | tf_op jit(solution)/shard_map/all_gather | solution.py:52
  94.2 0.9 slice.61
  96.0 1.9 fusion
  98.1 1.4 multiply_reduce_fusion.1
  99.4 1.5 copy.109
  101.0 1.3 fusion.12
  102.3 2.5 %psum.21 = f32[2,1024]{1,0:T(2,128)S(1)} all-reduce(f32[2,1024]{1,0:T(2,128)S(1)} %pad_maximum_fusion.7), channel_id=1, replica_groups=mesh['seg'=16,'exp_y'=4,'exp_x'=4,'exp_core'=2] {'exp_core'}, use_global_device_ids=true, to_apply=%region_7.8 | all-reduce | flops 2048 | bytes 16384 | tf_op jit(solution)/shard_map/psum | solution.py:85
  104.8 7.6 %psum.22 = f32[2,1024]{1,0:T(2,128)S(1)} all-reduce(f32[2,1024]{1,0:T(2,128)S(1)} %psum.21), channel_id=1, replica_groups=mesh['seg'=16,'exp_y'=4,'exp_x'=4,'exp_core'=2] {'exp_x'}, use_global_device_ids=true, to_apply=%region_8.9 | all-reduce | flops 2048 | bytes 16384 | tf_op jit(solution)/shard_map/psum | solution.py:85
  112.3 10.8 %psum.23 = f32[2,1024]{1,0:T(2,128)S(1)} all-reduce(f32[2,1024]{1,0:T(2,128)S(1)} %psum.22), channel_id=1, replica_groups=mesh['seg'=16,'exp_y'=4,'exp_x'=4,'exp_core'=2] {'exp_y'}, use_global_device_ids=true, to_apply=%region_9.10 | all-reduce | flops 2048 | bytes 16384 | tf_op jit(solution)/shard_map/psum | solution.py:85
  123.1 2.4 %subtract_convert_fusion = (bf16[1024,256]{1,0:T(8,128)(2,1)}, bf16[1024,256]{1,0:T(8,128)(2,1)}) fusion(bf16[1024,256]{1,0:T(8,128)(2,1)} %param.11, f32[128,8,2,128]{3,2,1,0:T(2,128)S(1)} %bitcast.120, f32[1024]{0:T(1024)S(1)} %bitcast.131, f32[1024]{0:T(1024)S(1)} %bitcast.132, f32[256]{0:T(256)S(1)} %copy-done.18), kind=kLoop, calls=%fused_computation.29 | loop fusion | flops 3145728 | bytes 2630656 | tf_op jit(solution)/shard_map/convert_element_type | solution.py:93
  125.6 2.0 reshape.228
  127.6 1.3 copy.124
  129.2 1.4 slice_add_fusion
  130.7 1.2 exponential_select_fusion.1
  131.9 1.4 copy.120
  133.2 2.6 %multiply_convert_fusion = bf16[2,2,512,512]{3,2,1,0:T(8,128)(2,1)S(1)} fusion(bf16[2,512,2,128]{1,3,2,0:T(8,128)(2,1)S(1)} %copy.124, f32[2,2,512]{2,1,0:T(2,128)} %copy-done.13, pred[512,512]{1,0:T(8,128)(4,1)} %copy-done.12, bf16[2,512,2,128]{3,2,1,0:T(2,128)(2,1)} %copy-done.4), kind=kOutput, calls=%fused_computation | convolution fusion | flops 273678336 | bytes 3416064 | tf_op jit(solution)/shard_map/bthf,bshf->bhts/dot_general | solution.py:111
  135.9 1.3 copy-done
  138.0 1.1 fusion.9
  139.1 2.0 copy.115
  141.1 1.9 copy.172
  143.0 1.9 convolution_bitcast_fusion
  144.9 0.9 convolution_bitcast_fusion.1
  145.8 53.6 %all-gather.4.cloned.1.call-done = f32[16,2,128,128]{3,2,1,0:T(8,128)} async-done(((f32[1,2,128,128]{3,2,1,0:T(8,128)}), f32[16,2,128,128]{3,2,1,0:T(8,128)}) %all-gather.4.cloned.1.call-update) | async-done | bytes 2097168 | tf_op jit(solution)/shard_map/all_gather | solution.py:102
  199.4 1.8 multiply_reduce_fusion
  202.2 0.9 copy.170
  204.1 0.9 copy.171
  (82 shorter events, 8.7 us)
Async XLA Ops:
  7.2 87.1 %all-gather.6.cloned.1.call-start = ((), (), s32[]{:S(2)}) async-start(), calls=%async_computation.1 | async-start | bytes 2367488 | tf_op jit(solution)/shard_map/all_gather | solution.py:52
  10.6 6.1 %copy-start.13 = (f32[2,2,512]{2,1,0:T(2,128)}, f32[2,2,512]{2,1,0:T(2,128)S(1)}, u32[]{:S(2)}) copy-start(f32[2,2,512]{2,1,0:T(2,128)S(1)} %reduce_window_sum.24) | copy-start | bytes 24580
  11.4 3.6 %copy-start.15 = (f32[2]{0:T(128)}, f32[2]{0:T(128)S(1)}, u32[]{:S(2)}) copy-start(f32[2]{0:T(128)S(1)} %get-tuple-element.13) | copy-start | bytes 28
  11.5 4.5 %copy-start.11 = (bf16[1024,256]{1,0:T(8,128)(2,1)S(1)}, bf16[1024,256]{1,0:T(8,128)(2,1)}, u32[]{:S(2)}) copy-start(bf16[1024,256]{1,0:T(8,128)(2,1)} %param.6) | copy-start | bytes 1572868
  12.7 3.4 %copy-start.6 = (bf16[2,512,2,128]{3,2,1,0:T(2,128)(2,1)}, bf16[2,512,2,128]{3,2,1,0:T(2,128)(2,1)S(1)}, u32[]{:S(2)}) copy-start(bf16[2,512,2,128]{3,2,1,0:T(2,128)(2,1)S(1)} %reshape.222) | copy-start | bytes 1572868
  14.1 5.2 %copy-start.4 = (bf16[2,512,2,128]{3,2,1,0:T(2,128)(2,1)}, bf16[2,512,2,128]{3,2,1,0:T(2,128)(2,1)S(1)}, u32[]{:S(2)}) copy-start(bf16[2,512,2,128]{3,2,1,0:T(2,128)(2,1)S(1)} %reshape.226) | copy-start | bytes 1572868
  15.9 183.5 %all-gather.4.cloned.1.call-start = ((), (), s32[]{:S(2)}) async-start(), calls=%async_computation | async-start | bytes 2228224 | tf_op jit(solution)/shard_map/all_gather | solution.py:102
  16.5 81.5 %copy-start.2 = (bf16[2,512,2,128]{1,3,2,0:T(8,128)(2,1)}, bf16[2,512,2,128]{1,3,2,0:T(8,128)(2,1)S(1)}, u32[]{:S(2)}) copy-start(bf16[2,512,2,128]{1,3,2,0:T(8,128)(2,1)S(1)} %copy.118) | copy-start | bytes 1572868
  16.6 2.8 %copy-start.19 = (pred[16]{0:T(512)(128)(4,1)}, pred[16]{0:T(512)(128)(4,1)S(1)}, u32[]{:S(2)}) copy-start(pred[16]{0:T(512)(128)(4,1)S(1)} %get-tuple-element.16) | copy-start | bytes 52
  16.7 2.7 %copy-start.12 = (pred[512,512]{1,0:T(8,128)(4,1)}, pred[512,512]{1,0:T(8,128)(4,1)S(1)}, u32[]{:S(2)}) copy-start(pred[512,512]{1,0:T(8,128)(4,1)S(1)} %iota_compare_fusion) | copy-start | bytes 786436
  21.2 76.8 %copy-start.17 = (f32[2]{0:T(128)S(1)}, f32[2]{0:T(128)}, u32[]{:S(2)}) copy-start(f32[2]{0:T(128)} %get-tuple-element.12) | copy-start | bytes 28
  96.0 2.0 copy-start.9
  98.1 2.9 %copy-start.18 = (f32[256]{0:T(256)S(1)}, f32[256]{0:T(256)}, u32[]{:S(2)}) copy-start(f32[256]{0:T(256)} %param.10) | copy-start | bytes 3076
  125.6 3.3 %copy-start.3 = (bf16[2,512,2,128]{1,3,2,0:T(8,128)(2,1)S(1)}, bf16[2,512,2,128]{1,3,2,0:T(8,128)(2,1)}, u32[]{:S(2)}) copy-start(bf16[2,512,2,128]{1,3,2,0:T(8,128)(2,1)} %copy-done.2) | copy-start | bytes 1572868
  133.2 3.9 %copy-start.7 = (bf16[2,512,2,128]{3,2,1,0:T(2,128)(2,1)S(1)}, bf16[2,512,2,128]{3,2,1,0:T(2,128)(2,1)}, u32[]{:S(2)}) copy-start(bf16[2,512,2,128]{3,2,1,0:T(2,128)(2,1)} %copy-done.6) | copy-start | bytes 1572868
  135.9 1.3 copy-start
  143.0 1.9 copy-start.1
  144.9 54.5 %copy-start.14 = (f32[16,2]{1,0:T(8,128)S(1)}, f32[16,2]{1,0:T(8,128)}, u32[]{:S(2)}) copy-start(f32[16,2]{1,0:T(8,128)} %copy.120) | copy-start | bytes 388
  144.9 56.3 %copy-start.16 = (f32[2]{0:T(128)S(1)}, f32[2]{0:T(128)}, u32[]{:S(2)}) copy-start(f32[2]{0:T(128)} %copy-done.15) | copy-start | bytes 28
  145.8 55.5 %copy-start.8 = (bf16[2,512,2,128]{3,2,1,0:T(2,128)(2,1)S(1)}, bf16[2,512,2,128]{3,2,1,0:T(2,128)(2,1)}, u32[]{:S(2)}) copy-start(bf16[2,512,2,128]{3,2,1,0:T(2,128)(2,1)} %copy-done.6) | copy-start | bytes 1572868
  145.8 55.5 %copy-start.10 = (f32[2,512,2,128]{3,1,2,0:T(8,128)S(1)}, f32[2,512,2,128]{3,1,2,0:T(8,128)}, u32[]{:S(2)}) copy-start(f32[2,512,2,128]{3,1,2,0:T(8,128)} %convolution_bitcast_fusion) | copy-start | bytes 3145732
  201.3 1.8 copy-start.5
Sparse Core Ops, SparseCore 0:
  16.0 78.1 all-gather.5
  130.8 68.5 all-gather.3

commit v3 on v2

--- a/solution.py
+++ b/solution.py
@@ -5,6 +5,7 @@
 
 BLK = 512
 EXP_PARTS = ("exp_y", "exp_x", "exp_core")
+SEG_PARTS = ("seg_hi", "seg_lo")
 
 
 EPS = 1e-06
@@ -18,6 +19,12 @@
     lower = token_place[:, None] >= token_place[None, :]
     mask = jnp.where(lower, jnp.exp(jnp.minimum(spread, 0.0)), 0.0)
     return (cumulative, cumulative[..., -1], mask)
+
+
+def fade_weights(order, valid, logs, limit, extra=0.0):
+    between = order & limit
+    summed = jnp.sum(jnp.where(between[:, :, None], logs[None, :, :], 0.0), axis=1) + extra
+    return jnp.where(valid[:, None], jnp.exp(summed), 0.0)
 
 
 def body(queries, keys, values, log_decay, gain, d_out):
@@ -42,30 +49,32 @@
         "bshe,bshf->bhef", key_weighted, vblocks, preferred_element_type=jnp.float32
     )
     block_fade = jnp.exp(totals)
-    seg_count = lax.axis_size("seg")
-    here = lax.axis_index("seg")
     seg_state = block_state[0]
     for block in range(1, count):
         seg_state = block_fade[block][:, None, None] * seg_state + block_state[block]
+    low = lax.axis_index("seg_lo")
+    high = lax.axis_index("seg_hi")
+    low_places = jnp.arange(lax.axis_size("seg_lo"))
+    high_places = jnp.arange(lax.axis_size("seg_hi"))
     seg_log = jnp.sum(log_decay, axis=-1)
     log_rows = jnp.broadcast_to(seg_log[:, None, None], (local_heads, 8, head_width))
-    gathered = lax.all_gather(jnp.concatenate((seg_state, log_rows), axis=1), "seg")
-    all_states = gathered[:, :, :head_width, :]
-    all_logs = gathered[:, :, head_width, 0]
-    places = jnp.arange(seg_count)
-    between_fwd = (places[:, None] < places[None, :]) & (places[None, :] < here)
-    between_bwd = (places[:, None] > places[None, :]) & (places[None, :] > here)
-    weight_fwd = jnp.where(
-        (places < here)[:, None],
-        jnp.exp(jnp.sum(jnp.where(between_fwd[:, :, None], all_logs[None, :, :], 0.0), axis=1)),
-        0.0,
+    first = lax.all_gather(jnp.concatenate((seg_state, log_rows), axis=1), "seg_lo")
+    low_states = first[:, :, :head_width, :]
+    low_logs = first[:, :, head_width, 0]
+    inside = fade_weights(low_places[:, None] < low_places[None, :], low_places < low, low_logs, low_places[None, :] < low)
+    within = jnp.sum(inside[:, :, None, None] * low_states, axis=0)
+    to_end = fade_weights(low_places[:, None] < low_places[None, :], low_places >= 0, low_logs, True)
+    group_state = jnp.sum(to_end[:, :, None, None] * low_states, axis=0)
+    group_log = jnp.sum(low_logs, axis=0)
+    group_rows = jnp.broadcast_to(group_log[:, None, None], (local_heads, 8, head_width))
+    second = lax.all_gather(jnp.concatenate((group_state, group_rows), axis=1), "seg_hi")
+    high_states = second[:, :, :head_width, :]
+    high_logs = second[:, :, head_width, 0]
+    before_here = jnp.sum(jnp.where((low_places < low)[:, None], low_logs, 0.0), axis=0)
+    outside = fade_weights(
+        high_places[:, None] < high_places[None, :], high_places < high, high_logs, high_places[None, :] < high, before_here
     )
-    weight_bwd = jnp.where(
-        (places > here)[:, None],
-        jnp.exp(jnp.sum(jnp.where(between_bwd[:, :, None], all_logs[None, :, :], 0.0), axis=1)),
-        0.0,
-    )
-    entering = jnp.sum(weight_fwd[:, :, None, None] * all_states, axis=0)
+    entering = within + jnp.sum(outside[:, :, None, None] * high_states, axis=0)
     held_list = []
     running = entering
     for block in range(count):
@@ -99,8 +108,17 @@
     seg_back = back_terms[count - 1]
     for block in range(count - 2, -1, -1):
         seg_back = back_terms[block] + block_fade[block][:, None, None] * seg_back
-    all_backs = lax.all_gather(seg_back, "seg")
-    leaving = jnp.sum(weight_bwd[:, :, None, None] * all_backs, axis=0)
+    third = lax.all_gather(seg_back, "seg_lo")
+    inside_back = fade_weights(low_places[:, None] > low_places[None, :], low_places > low, low_logs, low_places[None, :] > low)
+    within_back = jnp.sum(inside_back[:, :, None, None] * third, axis=0)
+    to_start = fade_weights(low_places[:, None] > low_places[None, :], low_places >= 0, low_logs, True)
+    group_back = jnp.sum(to_start[:, :, None, None] * third, axis=0)
+    fourth = lax.all_gather(group_back, "seg_hi")
+    after_here = jnp.sum(jnp.where((low_places > low)[:, None], low_logs, 0.0), axis=0)
+    outside_back = fade_weights(
+        high_places[:, None] > high_places[None, :], high_places > high, high_logs, high_places[None, :] > high, after_here
+    )
+    leaving = within_back + jnp.sum(outside_back[:, :, None, None] * fourth, axis=0)
     exit_list = [None] * count
     running = leaving
     for block in range(count - 1, -1, -1):
@@ -132,9 +150,9 @@
 
 
 def solution(mesh):
-    parts = mesh.devices.reshape(mesh.devices.shape[0], 4, -1, 2)
-    split = jax.sharding.Mesh(parts, ("seg",) + EXP_PARTS)
-    rows_heads = P("seg", EXP_PARTS)
-    in_specs = (rows_heads, rows_heads, rows_heads, P(EXP_PARTS, "seg"), P(EXP_PARTS), rows_heads)
+    parts = mesh.devices.reshape(4, -1, 4, mesh.devices.shape[1] // 8, 2)
+    split = jax.sharding.Mesh(parts, SEG_PARTS + EXP_PARTS)
+    rows_heads = P(SEG_PARTS, EXP_PARTS)
+    in_specs = (rows_heads, rows_heads, rows_heads, P(EXP_PARTS, SEG_PARTS), P(EXP_PARTS), rows_heads)
     out_specs = (rows_heads, rows_heads, rows_heads, rows_heads)
     return jax.shard_map(body, mesh=split, in_specs=in_specs, out_specs=out_specs, check_vma=False)

time: 212 us -> 155 us (0.73)
  waiting for transfers between devices: 127 us -> 0 us
  blocking collectives: 20.8 us -> 113 us
  between operations: 14.5 us -> 1.14 us
  matrix products: 15 us -> 9.9 us
  local copies, waits for them, and re-layouts: 20.3 us -> 17.2 us
    all_gather x2 -> x0, waiting for transfers between devices: 127 us -> none  [the longest x1 73.1 us: body(): lax.all_gather(jnp.concatenate((seg_state, log_rows), axis=1), 'seg')]
    all_gather x0 -> x4, blocking collectives: none -> 92.3 us  [the longest x1 32.9 us: body(): lax.all_gather(jnp.concatenate((group_state, group_rows), axis=1), 'seg_hi')]
    reduce_sum x3 -> x8, other arithmetic: 4.37 us -> 4.15 us  [the longest x1 1.22 us: body(): group_back = jnp.sum(to_start[:, :, None, None] * third, axis=0)]
  transfers between devices with their start and end apart: 2 -> 0, of which waited for: 2 -> 0; matrix products, arithmetic and copies ran while one was open for 9% -> 0% of each run, Pallas kernels for 0% -> 0%
where the time goes in v3:
time: 155 us; the launch traced here: 154 us
  blocking collectives  113 us (73%)
  local copies, waits for them, and re-layouts  17.2 us (11%)
  other arithmetic  12.3 us (8%)
  matrix products  9.9 us (6%)
    all_gather x1, blocking collectives, body(): lax.all_gather(jnp.concatenate((group_state, group_rows), axis=1), 'seg_hi')  32.9 us
    all_gather x1, blocking collectives, body(): fourth = lax.all_gather(group_back, 'seg_hi')  25.2 us
    psum x3, blocking collectives, body(): totals_exp = lax.psum(totals_exp, axis)  20.9 us
    all_gather x1, blocking collectives, body(): lax.all_gather(jnp.concatenate((seg_state, log_rows), axis=1), 'seg_lo')  17.4 us
    all_gather x1, blocking collectives, body(): third = lax.all_gather(seg_back, 'seg_lo')  16.7 us
    unnamed x46, local copies, waits for them, and re-layouts  3.6 us
    reshape x2, local copies, waits for them, and re-layouts, body(): grad_blocks = grad_attended.reshape(shape)  3.32 us

profile of v3, /device:TPU:6, one launch (start us, length us, event | category | flops | bytes accessed | tf_op | source)
XLA Modules:
  0.0 153.8 jit_solution(9403425347393937954)
XLA Ops:
  0.6 0.7 reshape.401
  1.4 1.2 reduce-window.6
  3.5 1.2 reshape.400
  4.7 1.4 reshape.404
  6.1 0.9 fusion.12
  7.3 17.4 %all-gather = f32[8,136,128]{2,1,0:T(8,128)S(1)} all-gather(f32[2,136,128]{2,1,0:T(8,128)S(1)} %pad_maximum_fusion), channel_id=2, replica_groups=mesh['seg_hi'=4,'seg_lo'=4,'exp_y'=4,'exp_x'=4,'exp_core'=2] {'seg_lo'}, dimensions={0}, use_global_device_ids=true | all-gather | bytes 696320 | tf_op jit(solution)/shard_map/all_gather | solution.py:61
  26.2 32.9 %all-gather.1 = f32[8,136,128]{2,1,0:T(8,128)S(1)} all-gather(f32[2,136,128]{2,1,0:T(8,128)S(1)} %pad_maximum_fusion.1), channel_id=3, replica_groups=mesh['seg_hi'=4,'seg_lo'=4,'exp_y'=4,'exp_x'=4,'exp_core'=2] {'seg_hi'}, dimensions={0}, use_global_device_ids=true | all-gather | bytes 696320 | tf_op jit(solution)/shard_map/all_gather | solution.py:70
  61.6 1.4 multiply_convert_fusion.1
  63.1 0.8 convolution_bitcast_fusion.3
  64.0 1.4 multiply_reduce_fusion
  65.3 1.5 copy.128
  66.9 1.3 fusion.11
  68.2 2.5 %psum.21 = f32[2,1024]{1,0:T(2,128)S(1)} all-reduce(f32[2,1024]{1,0:T(2,128)S(1)} %pad_maximum_fusion.8), channel_id=1, replica_groups=mesh['seg_hi'=4,'seg_lo'=4,'exp_y'=4,'exp_x'=4,'exp_core'=2] {'exp_core'}, use_global_device_ids=true, to_apply=%region_13.14 | all-reduce | flops 2048 | bytes 16384 | tf_op jit(solution)/shard_map/psum | solution.py:94
  70.7 7.6 %psum.22 = f32[2,1024]{1,0:T(2,128)S(1)} all-reduce(f32[2,1024]{1,0:T(2,128)S(1)} %psum.21), channel_id=1, replica_groups=mesh['seg_hi'=4,'seg_lo'=4,'exp_y'=4,'exp_x'=4,'exp_core'=2] {'exp_x'}, use_global_device_ids=true, to_apply=%region_14.15 | all-reduce | flops 2048 | bytes 16384 | tf_op jit(solution)/shard_map/psum | solution.py:94
  78.2 10.8 %psum.23 = f32[2,1024]{1,0:T(2,128)S(1)} all-reduce(f32[2,1024]{1,0:T(2,128)S(1)} %psum.22), channel_id=1, replica_groups=mesh['seg_hi'=4,'seg_lo'=4,'exp_y'=4,'exp_x'=4,'exp_core'=2] {'exp_y'}, use_global_device_ids=true, to_apply=%region_15.16 | all-reduce | flops 2048 | bytes 16384 | tf_op jit(solution)/shard_map/psum | solution.py:94
  89.1 2.4 %subtract_convert_fusion = (bf16[1024,256]{1,0:T(8,128)(2,1)}, bf16[1024,256]{1,0:T(8,128)(2,1)}) fusion(bf16[1024,256]{1,0:T(8,128)(2,1)} %param.11, f32[128,8,2,128]{3,2,1,0:T(2,128)S(1)} %bitcast.125, f32[1024]{0:T(1024)S(1)} %bitcast.139, f32[1024]{0:T(1024)S(1)} %bitcast.140, f32[256]{0:T(256)S(1)} %copy-done.18), kind=kLoop, calls=%fused_computation.26 | loop fusion | flops 3145728 | bytes 2630656 | tf_op jit(solution)/shard_map/convert_element_type | solution.py:102
  91.5 2.0 %reshape.406 = bf16[2,512,2,128]{3,2,1,0:T(2,128)(2,1)} reshape(bf16[1024,256]{1,0:T(8,128)(2,1)} %get-tuple-element.16) | data formatting | bytes 1048576 | tf_op jit(solution)/shard_map/reshape | solution.py:103
  93.6 1.3 copy.145
  95.3 16.7 %all_gather.26 = f32[4,2,128,128]{3,2,1,0:T(8,128)} all-gather(f32[1,2,128,128]{3,2,1,0:T(8,128)S(1)} %slice_add_fusion), channel_id=1, replica_groups=mesh['seg_hi'=4,'seg_lo'=4,'exp_y'=4,'exp_x'=4,'exp_core'=2] {'seg_lo'}, dimensions={0}, use_global_device_ids=true | all-gather | bytes 655360 | tf_op jit(solution)/shard_map/all_gather | solution.py:111
  113.3 1.2 multiply_reduce_fusion.2
  114.6 25.2 %all-gather.2 = f32[8,128,128]{2,1,0:T(8,128)} all-gather(f32[2,128,128]{2,1,0:T(8,128)S(1)} %get-tuple-element.6), channel_id=4, replica_groups=mesh['seg_hi'=4,'seg_lo'=4,'exp_y'=4,'exp_x'=4,'exp_core'=2] {'seg_hi'}, dimensions={0}, use_global_device_ids=true | all-gather | bytes 655360 | tf_op jit(solution)/shard_map/all_gather | solution.py:116
  139.8 1.3 exponential_select_fusion.1
  141.1 1.3 copy.140
  142.4 1.2 multiply_reduce_fusion.1
  143.6 0.7 fusion.27
  144.4 0.9 convolution_bitcast_fusion
  146.3 0.9 copy.192
  147.2 1.4 multiply_convert_fusion
  148.6 0.9 convolution_bitcast_fusion.1
  150.5 0.9 copy.193
  151.3 0.8 convolution_bitcast_fusion.2
  152.9 0.9 copy.194
  (98 shorter events, 9.5 us)
Async XLA Ops:
  3.2 58.4 %copy-start.14 = (f32[2,2,512]{2,1,0:T(2,128)}, f32[2,2,512]{2,1,0:T(2,128)S(1)}, u32[]{:S(2)}) copy-start(f32[2,2,512]{2,1,0:T(2,128)S(1)} %reduce_window_sum.24) | copy-start | bytes 24580
  3.5 3.6 %copy-start.16 = (f32[2,1024]{1,0:T(2,128)S(1)}, f32[2,1024]{1,0:T(2,128)}, u32[]{:S(2)}) copy-start(f32[2,1024]{1,0:T(2,128)} %param.9) | copy-start | bytes 24580
  4.7 56.9 %copy-start.2 = (bf16[2,512,2,128]{3,2,1,0:T(2,128)(2,1)}, bf16[2,512,2,128]{3,2,1,0:T(2,128)(2,1)S(1)}, u32[]{:S(2)}) copy-start(bf16[2,512,2,128]{3,2,1,0:T(2,128)(2,1)S(1)} %reshape.400) | copy-start | bytes 1572868
  6.0 20.2 %copy-start.4 = (bf16[2,512,2,128]{3,2,1,0:T(2,128)(2,1)}, bf16[2,512,2,128]{3,2,1,0:T(2,128)(2,1)S(1)}, u32[]{:S(2)}) copy-start(bf16[2,512,2,128]{3,2,1,0:T(2,128)(2,1)S(1)} %reshape.404) | copy-start | bytes 1572868
  7.0 53.8 %copy-start.17 = (f32[2]{0:T(128)}, f32[2]{0:T(128)S(1)}, u32[]{:S(2)}) copy-start(f32[2]{0:T(128)S(1)} %get-tuple-element.24) | copy-start | bytes 28
  7.3 53.6 %copy-start.11 = (bf16[1024,256]{1,0:T(8,128)(2,1)S(1)}, bf16[1024,256]{1,0:T(8,128)(2,1)}, u32[]{:S(2)}) copy-start(bf16[1024,256]{1,0:T(8,128)(2,1)} %param.6) | copy-start | bytes 1572868
  59.2 0.5 copy-start.19
  60.8 3.1 %copy-start.7 = (bf16[1,2,128,128]{3,2,1,0:T(8,128)(2,1)}, bf16[1,2,128,128]{3,2,1,0:T(8,128)(2,1)S(1)}, u32[]{:S(2)}) copy-start(bf16[1,2,128,128]{3,2,1,0:T(8,128)(2,1)S(1)} %bitcast_convert_fusion.1) | copy-start | bytes 196612
  60.9 3.0 %copy-start.9 = (bf16[1,2,128,128]{3,2,1,0:T(8,128)(2,1)}, bf16[1,2,128,128]{3,2,1,0:T(8,128)(2,1)S(1)}, u32[]{:S(2)}) copy-start(bf16[1,2,128,128]{3,2,1,0:T(8,128)(2,1)S(1)} %fusion.29) | copy-start | bytes 196612
  61.5 2.5 %copy-start = (bf16[2,512,2,128]{1,3,2,0:T(8,128)(2,1)}, bf16[2,512,2,128]{1,3,2,0:T(8,128)(2,1)S(1)}, u32[]{:S(2)}) copy-start(bf16[2,512,2,128]{1,3,2,0:T(8,128)(2,1)S(1)} %copy.137) | copy-start | bytes 1572868
  61.6 1.5 copy-start.12
  61.6 1.5 copy-start.5
  63.9 2.9 %copy-start.18 = (f32[256]{0:T(256)S(1)}, f32[256]{0:T(256)}, u32[]{:S(2)}) copy-start(f32[256]{0:T(256)} %param.10) | copy-start | bytes 3076
  91.5 3.3 %copy-start.1 = (bf16[2,512,2,128]{1,3,2,0:T(8,128)(2,1)S(1)}, bf16[2,512,2,128]{1,3,2,0:T(8,128)(2,1)}, u32[]{:S(2)}) copy-start(bf16[2,512,2,128]{1,3,2,0:T(8,128)(2,1)} %copy-done) | copy-start | bytes 1572868
  144.3 1.0 copy-start.3
  145.4 1.8 %copy-start.6 = (bf16[2,512,2,128]{3,2,1,0:T(2,128)(2,1)S(1)}, bf16[2,512,2,128]{3,2,1,0:T(2,128)(2,1)}, u32[]{:S(2)}) copy-start(bf16[2,512,2,128]{3,2,1,0:T(2,128)(2,1)} %copy-done.4) | copy-start | bytes 1572868
  145.4 1.8 %copy-start.13 = (pred[512,512]{1,0:T(8,128)(4,1)S(1)}, pred[512,512]{1,0:T(8,128)(4,1)}, u32[]{:S(2)}) copy-start(pred[512,512]{1,0:T(8,128)(4,1)} %copy-done.12) | copy-start | bytes 786436
  145.4 1.8 %copy-start.15 = (f32[2,2,512]{2,1,0:T(2,128)S(1)}, f32[2,2,512]{2,1,0:T(2,128)}, u32[]{:S(2)}) copy-start(f32[2,2,512]{2,1,0:T(2,128)} %copy-done.14) | copy-start | bytes 24580
  151.3 0.8 copy-start.8
  151.3 0.9 copy-start.10

commit v4 on v3

--- a/solution.py
+++ b/solution.py
@@ -89,9 +89,9 @@
     partial = jnp.stack(
         (jnp.sum(attended * attended, axis=-1), jnp.sum(gain * upstream * attended, axis=-1))
     )
-    totals_exp = partial
-    for axis in EXP_PARTS[::-1]:
-        totals_exp = lax.psum(totals_exp, axis)
+    totals_exp = lax.psum(partial, EXP_PARTS[-1])
+    for axis in EXP_PARTS[-2::-1]:
+        totals_exp = jnp.sum(lax.all_gather(totals_exp, axis), axis=0)
     squares, cross = totals_exp[0], totals_exp[1]
     features = width * lax.axis_size(EXP_PARTS)
     inv_rms = lax.rsqrt(squares / features + EPS)[:, None]

time: 155 us -> 159 us (1.026)
  blocking collectives: 113 us -> 118 us
    all_gather x0 -> x2, blocking collectives: none -> 24.3 us  [body(): totals_exp = jnp.sum(lax.all_gather(totals_exp, axis), axis=0)]
    psum x3 -> x1, blocking collectives: 20.9 us -> 2.5 us  [body(): totals_exp = lax.psum(partial, EXP_PARTS[-1])]
    all_gather x1, blocking collectives: 25.2 us -> 23.5 us  [body(): fourth = lax.all_gather(group_back, 'seg_hi')]
where the time goes in v4:
time: 159 us; the launch traced here: 158 us
  blocking collectives  118 us (74%)
  local copies, waits for them, and re-layouts  17.2 us (11%)
  other arithmetic  12.3 us (8%)
  matrix products  9.91 us (6%)
    all_gather x1, blocking collectives, body(): lax.all_gather(jnp.concatenate((group_state, group_rows), axis=1), 'seg_hi')  32.9 us
    all_gather x2, blocking collectives, body(): totals_exp = jnp.sum(lax.all_gather(totals_exp, axis), axis=0)  24.3 us
    all_gather x1, blocking collectives, body(): fourth = lax.all_gather(group_back, 'seg_hi')  23.5 us
    all_gather x1, blocking collectives, body(): lax.all_gather(jnp.concatenate((seg_state, log_rows), axis=1), 'seg_lo')  17.4 us
    all_gather x1, blocking collectives, body(): third = lax.all_gather(seg_back, 'seg_lo')  17.2 us
    unnamed x46, local copies, waits for them, and re-layouts  3.6 us
    reshape x2, local copies, waits for them, and re-layouts, body(): grad_blocks = grad_attended.reshape(shape)  3.32 us

profile of v4, /device:TPU:6, one launch (start us, length us, event | category | flops | bytes accessed | tf_op | source)
XLA Modules:
  0.0 158.5 jit_solution(7248070411868868633)
XLA Ops:
  0.6 0.7 reshape.401
  1.4 1.2 reduce-window.6
  3.5 1.2 reshape.400
  4.7 1.4 reshape.404
  6.1 0.9 fusion.12
  7.3 17.4 %all-gather = f32[8,136,128]{2,1,0:T(8,128)S(1)} all-gather(f32[2,136,128]{2,1,0:T(8,128)S(1)} %pad_maximum_fusion), channel_id=2, replica_groups=mesh['seg_hi'=4,'seg_lo'=4,'exp_y'=4,'exp_x'=4,'exp_core'=2] {'seg_lo'}, dimensions={0}, use_global_device_ids=true | all-gather | bytes 696320 | tf_op jit(solution)/shard_map/all_gather | solution.py:61
  26.2 32.9 %all-gather.1 = f32[8,136,128]{2,1,0:T(8,128)S(1)} all-gather(f32[2,136,128]{2,1,0:T(8,128)S(1)} %pad_maximum_fusion.1), channel_id=3, replica_groups=mesh['seg_hi'=4,'seg_lo'=4,'exp_y'=4,'exp_x'=4,'exp_core'=2] {'seg_hi'}, dimensions={0}, use_global_device_ids=true | all-gather | bytes 696320 | tf_op jit(solution)/shard_map/all_gather | solution.py:70
  61.6 1.4 multiply_convert_fusion.1
  63.1 0.8 convolution_bitcast_fusion.3
  64.0 1.4 multiply_reduce_fusion
  65.3 1.5 copy.128
  66.9 1.3 fusion.11
  68.2 2.5 %psum.7 = f32[1,2,1024]{2,1,0:T(2,128)S(1)} all-reduce(f32[1,2,1024]{2,1,0:T(2,128)S(1)} %maximum_bitcast_fusion), channel_id=1, replica_groups=mesh['seg_hi'=4,'seg_lo'=4,'exp_y'=4,'exp_x'=4,'exp_core'=2] {'exp_core'}, use_global_device_ids=true, to_apply=%region_13.14 | all-reduce | flops 2048 | bytes 16384 | tf_op jit(solution)/shard_map/psum | solution.py:92
  70.7 11.9 %all_gather.39 = f32[4,2,1024]{2,1,0:T(2,128)S(1)} all-gather(f32[1,2,1024]{2,1,0:T(2,128)S(1)} %psum.7), channel_id=1, replica_groups=mesh['seg_hi'=4,'seg_lo'=4,'exp_y'=4,'exp_x'=4,'exp_core'=2] {'exp_x'}, dimensions={0}, use_global_device_ids=true | all-gather | bytes 40960 | tf_op jit(solution)/shard_map/all_gather | solution.py:94
  82.6 12.4 %all-gather.4 = f32[4,2,1024]{2,1,0:T(2,128)S(1)} all-gather(f32[1,2,1024]{2,1,0:T(2,128)S(1)} %bitcast.140), channel_id=4, replica_groups=mesh['seg_hi'=4,'seg_lo'=4,'exp_y'=4,'exp_x'=4,'exp_core'=2] {'exp_y'}, dimensions={0}, use_global_device_ids=true | all-gather | bytes 40960 | tf_op jit(solution)/shard_map/all_gather | solution.py:94
  95.0 2.4 %subtract_convert_fusion = (bf16[1024,256]{1,0:T(8,128)(2,1)}, bf16[1024,256]{1,0:T(8,128)(2,1)}) fusion(bf16[1024,256]{1,0:T(8,128)(2,1)} %param.11, f32[128,8,2,128]{3,2,1,0:T(2,128)S(1)} %bitcast.128, f32[1024]{0:T(1024)S(1)} %bitcast.143, f32[1024]{0:T(1024)S(1)} %bitcast.144, f32[256]{0:T(256)S(1)} %copy-done.18), kind=kLoop, calls=%fused_computation.26 | loop fusion | flops 3145728 | bytes 2630656 | tf_op jit(solution)/shard_map/convert_element_type | solution.py:102
  97.5 2.0 %reshape.406 = bf16[2,512,2,128]{3,2,1,0:T(2,128)(2,1)} reshape(bf16[1024,256]{1,0:T(8,128)(2,1)} %get-tuple-element.16) | data formatting | bytes 1048576 | tf_op jit(solution)/shard_map/reshape | solution.py:103
  99.5 1.3 copy.145
  101.2 17.2 %all_gather.42 = f32[4,2,128,128]{3,2,1,0:T(8,128)} all-gather(f32[1,2,128,128]{3,2,1,0:T(8,128)S(1)} %slice_add_fusion), channel_id=1, replica_groups=mesh['seg_hi'=4,'seg_lo'=4,'exp_y'=4,'exp_x'=4,'exp_core'=2] {'seg_lo'}, dimensions={0}, use_global_device_ids=true | all-gather | bytes 655360 | tf_op jit(solution)/shard_map/all_gather | solution.py:111
  119.8 1.2 multiply_reduce_fusion.2
  121.0 23.5 %all-gather.3 = f32[8,128,128]{2,1,0:T(8,128)} all-gather(f32[2,128,128]{2,1,0:T(8,128)S(1)} %get-tuple-element.6), channel_id=5, replica_groups=mesh['seg_hi'=4,'seg_lo'=4,'exp_y'=4,'exp_x'=4,'exp_core'=2] {'seg_hi'}, dimensions={0}, use_global_device_ids=true | all-gather | bytes 655360 | tf_op jit(solution)/shard_map/all_gather | solution.py:116
  144.5 1.3 exponential_select_fusion.1
  145.8 1.3 copy.140
  147.1 1.2 multiply_reduce_fusion.1
  148.3 0.7 fusion.27
  149.0 0.9 convolution_bitcast_fusion
  151.0 0.9 copy.192
  151.9 1.4 multiply_convert_fusion
  153.3 0.9 convolution_bitcast_fusion.1
  155.2 0.9 copy.193
  156.0 0.8 convolution_bitcast_fusion.2
  157.6 0.9 copy.194
  (100 shorter events, 9.5 us)
Async XLA Ops:
  3.2 58.4 %copy-start.14 = (f32[2,2,512]{2,1,0:T(2,128)}, f32[2,2,512]{2,1,0:T(2,128)S(1)}, u32[]{:S(2)}) copy-start(f32[2,2,512]{2,1,0:T(2,128)S(1)} %reduce_window_sum.24) | copy-start | bytes 24580
  3.5 3.6 %copy-start.16 = (f32[2,1024]{1,0:T(2,128)S(1)}, f32[2,1024]{1,0:T(2,128)}, u32[]{:S(2)}) copy-start(f32[2,1024]{1,0:T(2,128)} %param.9) | copy-start | bytes 24580
  4.7 56.9 %copy-start.2 = (bf16[2,512,2,128]{3,2,1,0:T(2,128)(2,1)}, bf16[2,512,2,128]{3,2,1,0:T(2,128)(2,1)S(1)}, u32[]{:S(2)}) copy-start(bf16[2,512,2,128]{3,2,1,0:T(2,128)(2,1)S(1)} %reshape.400) | copy-start | bytes 1572868
  6.0 20.2 %copy-start.4 = (bf16[2,512,2,128]{3,2,1,0:T(2,128)(2,1)}, bf16[2,512,2,128]{3,2,1,0:T(2,128)(2,1)S(1)}, u32[]{:S(2)}) copy-start(bf16[2,512,2,128]{3,2,1,0:T(2,128)(2,1)S(1)} %reshape.404) | copy-start | bytes 1572868
  7.0 53.8 %copy-start.17 = (f32[2]{0:T(128)}, f32[2]{0:T(128)S(1)}, u32[]{:S(2)}) copy-start(f32[2]{0:T(128)S(1)} %get-tuple-element.24) | copy-start | bytes 28
  7.3 53.6 %copy-start.11 = (bf16[1024,256]{1,0:T(8,128)(2,1)S(1)}, bf16[1024,256]{1,0:T(8,128)(2,1)}, u32[]{:S(2)}) copy-start(bf16[1024,256]{1,0:T(8,128)(2,1)} %param.6) | copy-start | bytes 1572868
  59.2 0.5 copy-start.19
  60.8 3.1 %copy-start.7 = (bf16[1,2,128,128]{3,2,1,0:T(8,128)(2,1)}, bf16[1,2,128,128]{3,2,1,0:T(8,128)(2,1)S(1)}, u32[]{:S(2)}) copy-start(bf16[1,2,128,128]{3,2,1,0:T(8,128)(2,1)S(1)} %bitcast_convert_fusion.1) | copy-start | bytes 196612
  60.9 3.0 %copy-start.9 = (bf16[1,2,128,128]{3,2,1,0:T(8,128)(2,1)}, bf16[1,2,128,128]{3,2,1,0:T(8,128)(2,1)S(1)}, u32[]{:S(2)}) copy-start(bf16[1,2,128,128]{3,2,1,0:T(8,128)(2,1)S(1)} %fusion.29) | copy-start | bytes 196612
  61.5 2.5 %copy-start = (bf16[2,512,2,128]{1,3,2,0:T(8,128)(2,1)}, bf16[2,512,2,128]{1,3,2,0:T(8,128)(2,1)S(1)}, u32[]{:S(2)}) copy-start(bf16[2,512,2,128]{1,3,2,0:T(8,128)(2,1)S(1)} %copy.137) | copy-start | bytes 1572868
  61.6 1.5 copy-start.12
  61.6 1.5 copy-start.5
  63.9 2.9 %copy-start.18 = (f32[256]{0:T(256)S(1)}, f32[256]{0:T(256)}, u32[]{:S(2)}) copy-start(f32[256]{0:T(256)} %param.10) | copy-start | bytes 3076
  97.5 3.3 %copy-start.1 = (bf16[2,512,2,128]{1,3,2,0:T(8,128)(2,1)S(1)}, bf16[2,512,2,128]{1,3,2,0:T(8,128)(2,1)}, u32[]{:S(2)}) copy-start(bf16[2,512,2,128]{1,3,2,0:T(8,128)(2,1)} %copy-done) | copy-start | bytes 1572868
  149.0 1.0 copy-start.3
  150.0 1.8 %copy-start.6 = (bf16[2,512,2,128]{3,2,1,0:T(2,128)(2,1)S(1)}, bf16[2,512,2,128]{3,2,1,0:T(2,128)(2,1)}, u32[]{:S(2)}) copy-start(bf16[2,512,2,128]{3,2,1,0:T(2,128)(2,1)} %copy-done.4) | copy-start | bytes 1572868
  150.0 1.8 %copy-start.13 = (pred[512,512]{1,0:T(8,128)(4,1)S(1)}, pred[512,512]{1,0:T(8,128)(4,1)}, u32[]{:S(2)}) copy-start(pred[512,512]{1,0:T(8,128)(4,1)} %copy-done.12) | copy-start | bytes 786436
  150.0 1.8 %copy-start.15 = (f32[2,2,512]{2,1,0:T(2,128)S(1)}, f32[2,2,512]{2,1,0:T(2,128)}, u32[]{:S(2)}) copy-start(f32[2,2,512]{2,1,0:T(2,128)} %copy-done.14) | copy-start | bytes 24580
  156.0 0.8 copy-start.8
  156.0 0.9 copy-start.10

commit v5 on v3

v5 whole, which is shorter than its diff:
```python
import jax
import jax.numpy as jnp
from jax import lax
from jax.sharding import PartitionSpec as P

BLK = 512
EXP_PARTS = ("exp_y", "exp_x", "exp_core")
SEG_PARTS = ("seg_hi", "seg_lo")


EPS = 1e-06


def fade_weights(order, valid, logs, limit, extra=0.0):
    between = order & limit
    summed = jnp.sum(jnp.where(between[:, :, None], logs[None, :, :], 0.0), axis=1) + extra
    return jnp.where(valid[:, None], jnp.exp(summed), 0.0)


def mm(a, b):
    return lax.dot_general(a, b, (((1,), (0,)), ((), ())), preferred_element_type=jnp.float32)


def mm_t(a, b):
    return lax.dot_general(a, b, (((1,), (1,)), ((), ())), preferred_element_type=jnp.float32)


def tm(a, b):
    return lax.dot_general(a, b, (((0,), (0,)), ((), ())), preferred_element_type=jnp.float32)


def body(queries, keys, values, log_decay, gain, d_out):
    rows, width = queries.shape
    local_heads = log_decay.shape[0]
    head_width = width // local_heads
    count = rows // BLK
    pairs = [(block, head) for block in range(count) for head in range(local_heads)]
    place = jnp.arange(BLK)
    lower = place[:, None] >= place[None, :]

    def tile(array, block, head):
        return array[block * BLK:(block + 1) * BLK, head * head_width:(head + 1) * head_width]

    q, k, v, up, mask, grow, shrink, scores = {}, {}, {}, {}, {}, {}, {}, {}
    block_state, block_fade = {}, {}
    for block, head in pairs:
        key = (block, head)
        q[key] = tile(queries, block, head)
        k[key] = tile(keys, block, head)
        v[key] = tile(values, block, head)
        up[key] = tile(d_out, block, head).astype(jnp.float32)
        cumulative = jnp.cumsum(log_decay[head, block * BLK:(block + 1) * BLK])
        total = cumulative[-1]
        spread = cumulative[:, None] - cumulative[None, :]
        mask[key] = jnp.where(lower, jnp.exp(jnp.minimum(spread, 0.0)), 0.0)
        grow[key] = jnp.exp(cumulative)[:, None]
        shrink[key] = jnp.exp(total - cumulative)[:, None]
        block_fade[key] = jnp.exp(total)
        scores[key] = (mm_t(q[key], k[key]) * mask[key]).astype(jnp.bfloat16)
        key_weighted = (k[key] * shrink[key]).astype(jnp.bfloat16)
        block_state[key] = tm(key_weighted, v[key])
    fades = [jnp.stack([block_fade[(block, head)] for head in range(local_heads)]) for block in range(count)]
    states = [jnp.stack([block_state[(block, head)] for head in range(local_heads)]) for block in range(count)]
    seg_state = states[0]
    for block in range(1, count):
        seg_state = fades[block][:, None, None] * seg_state + states[block]
    low = lax.axis_index("seg_lo")
    high = lax.axis_index("seg_hi")
    low_places = jnp.arange(lax.axis_size("seg_lo"))
    high_places = jnp.arange(lax.axis_size("seg_hi"))
    seg_log = jnp.sum(log_decay, axis=-1)
    log_rows = jnp.broadcast_to(seg_log[:, None, None], (local_heads, 8, head_width))
    first = lax.all_gather(jnp.concatenate((seg_state, log_rows), axis=1), "seg_lo")
    low_states = first[:, :, :head_width, :]
    low_logs = first[:, :, head_width, 0]
    inside = fade_weights(low_places[:, None] < low_places[None, :], low_places < low, low_logs, low_places[None, :] < low)
    within = jnp.sum(inside[:, :, None, None] * low_states, axis=0)
    to_end = fade_weights(low_places[:, None] < low_places[None, :], low_places >= 0, low_logs, True)
    group_state = jnp.sum(to_end[:, :, None, None] * low_states, axis=0)
    group_log = jnp.sum(low_logs, axis=0)
    group_rows = jnp.broadcast_to(group_log[:, None, None], (local_heads, 8, head_width))
    second = lax.all_gather(jnp.concatenate((group_state, group_rows), axis=1), "seg_hi")
    high_states = second[:, :, :head_width, :]
    high_logs = second[:, :, head_width, 0]
    before_here = jnp.sum(jnp.where((low_places < low)[:, None], low_logs, 0.0), axis=0)
    outside = fade_weights(
        high_places[:, None] < high_places[None, :], high_places < high, high_logs, high_places[None, :] < high, before_here
    )
    running = within + jnp.sum(outside[:, :, None, None] * high_states, axis=0)
    held, attended = {}, {}
    for block in range(count):
        for head in range(local_heads):
            held[(block, head)] = running[head].astype(jnp.bfloat16)
        running = fades[block][:, None, None] * running + states[block]
    squares, cross = [], []
    for block in range(count):
        square_sum, cross_sum = 0.0, 0.0
        for head in range(local_heads):
            key = (block, head)
            inner = mm(scores[key], v[key])
            attended[key] = inner + grow[key] * mm(q[key], held[key])
            gain_here = gain[head * head_width:(head + 1) * head_width]
            square_sum = square_sum + jnp.sum(attended[key] * attended[key], axis=-1)
            cross_sum = cross_sum + jnp.sum(gain_here * up[key] * attended[key], axis=-1)
        squares.append(square_sum)
        cross.append(cross_sum)
    partial = jnp.stack((jnp.concatenate(squares), jnp.concatenate(cross)))
    totals_exp = partial
    for axis in EXP_PARTS[::-1]:
        totals_exp = lax.psum(totals_exp, axis)
    features = width * lax.axis_size(EXP_PARTS)
    outs, grads, back_terms = {}, {}, {}
    for block, head in pairs:
        key = (block, head)
        rows_here = slice(block * BLK, (block + 1) * BLK)
        inv_rms = lax.rsqrt(totals_exp[0, rows_here] / features + EPS)[:, None]
        cross_here = totals_exp[1, rows_here][:, None]
        gain_here = gain[head * head_width:(head + 1) * head_width]
        outs[key] = (attended[key] * inv_rms * gain_here).astype(jnp.bfloat16)
        grads[key] = (
            gain_here * up[key] * inv_rms
            - attended[key] * inv_rms * inv_rms * inv_rms * cross_here / features
        ).astype(jnp.bfloat16)
        query_weighted = (q[key] * grow[key]).astype(jnp.bfloat16)
        back_terms[key] = tm(query_weighted, grads[key])
    backs = [jnp.stack([back_terms[(block, head)] for head in range(local_heads)]) for block in range(count)]
    seg_back = backs[count - 1]
    for block in range(count - 2, -1, -1):
        seg_back = backs[block] + fades[block][:, None, None] * seg_back
    third = lax.all_gather(seg_back, "seg_lo")
    inside_back = fade_weights(low_places[:, None] > low_places[None, :], low_places > low, low_logs, low_places[None, :] > low)
    within_back = jnp.sum(inside_back[:, :, None, None] * third, axis=0)
    to_start = fade_weights(low_places[:, None] > low_places[None, :], low_places >= 0, low_logs, True)
    group_back = jnp.sum(to_start[:, :, None, None] * third, axis=0)
    fourth = lax.all_gather(group_back, "seg_hi")
    after_here = jnp.sum(jnp.where((low_places > low)[:, None], low_logs, 0.0), axis=0)
    outside_back = fade_weights(
        high_places[:, None] > high_places[None, :], high_places > high, high_logs, high_places[None, :] > high, after_here
    )
    running = within_back + jnp.sum(outside_back[:, :, None, None] * fourth, axis=0)
    exits = {}
    for block in range(count - 1, -1, -1):
        for head in range(local_heads):
            exits[(block, head)] = running[head].astype(jnp.bfloat16)
        running = backs[block] + fades[block][:, None, None] * running
    grad_q, grad_k, grad_v = {}, {}, {}
    for block, head in pairs:
        key = (block, head)
        grad_scores = (mm_t(grads[key], v[key]) * mask[key]).astype(jnp.bfloat16)
        grad_q[key] = (mm(grad_scores, k[key]) + grow[key] * mm_t(grads[key], held[key])).astype(jnp.bfloat16)
        grad_k[key] = (tm(grad_scores, q[key]) + shrink[key] * mm_t(v[key], exits[key])).astype(jnp.bfloat16)
        grad_v[key] = (tm(scores[key], grads[key]) + shrink[key] * mm(k[key], exits[key])).astype(jnp.bfloat16)

    def whole(parts):
        return jnp.concatenate(
            [jnp.concatenate([parts[(block, head)] for head in range(local_heads)], axis=1) for block in range(count)],
            axis=0,
        )

    return whole(outs), whole(grad_q), whole(grad_k), whole(grad_v)


def solution(mesh):
    parts = mesh.devices.reshape(4, -1, 4, mesh.devices.shape[1] // 8, 2)
    split = jax.sharding.Mesh(parts, SEG_PARTS + EXP_PARTS)
    rows_heads = P(SEG_PARTS, EXP_PARTS)
    in_specs = (rows_heads, rows_heads, rows_heads, P(EXP_PARTS, SEG_PARTS), P(EXP_PARTS), rows_heads)
    out_specs = (rows_heads, rows_heads, rows_heads, rows_heads)
    return jax.shard_map(body, mesh=split, in_specs=in_specs, out_specs=out_specs, check_vma=False)
```

time: 155 us -> 189 us (1.22); the launches traced: 154 us -> 185 us
  local copies, waits for them, and re-layouts: 17.2 us -> 38.2 us
  matrix products: 9.9 us -> 18.7 us
  between operations: 1.14 us -> 4.4 us
  blocking collectives: 113 us -> 110 us
    unnamed x46 -> x156, local copies, waits for them, and re-layouts: 3.6 us -> 27.8 us
    dot_general x12 -> x48, matrix products: 9.9 us -> 18.7 us  [the longest x16 7.86 us: mm(): lax.dot_general(a, b, (((1,), (0,)), ((), ())), preferred_element_type=jn...]
    reshape x9 -> x0, local copies, waits for them, and re-layouts: 7.14 us -> none  [the longest x2 3.32 us: body(): grad_blocks = grad_attended.reshape(shape)]
    slice x2 -> x8, local copies, waits for them, and re-layouts: 0.23 us -> 4.66 us  [the longest x4 2.35 us: body(): total = cumulative[-1]]
    exp x1 -> x8, other arithmetic: 0.08 us -> 2.9 us  [the longest x4 2.6 us: body(): shrink[key] = jnp.exp(total - cumulative)[:, None]]
    all_gather x1, blocking collectives: 25.2 us -> 22.6 us  [body(): fourth = lax.all_gather(group_back, 'seg_hi')]
where the time goes in v5:
time: 189 us; the launch traced here: 185 us
  blocking collectives  110 us (58%)
  local copies, waits for them, and re-layouts  38.2 us (20%)
  matrix products  18.7 us (10%)
  other arithmetic  13.7 us (7%)
  between operations  4.4 us (2%)
    all_gather x1, blocking collectives, body(): lax.all_gather(jnp.concatenate((group_state, group_rows), axis=1), 'seg_hi')  32.9 us
    unnamed x156, local copies, waits for them, and re-layouts  27.8 us
    all_gather x1, blocking collectives, body(): fourth = lax.all_gather(group_back, 'seg_hi')  22.6 us
    psum x3, blocking collectives, body(): totals_exp = lax.psum(totals_exp, axis)  20.9 us
    all_gather x1, blocking collectives, body(): lax.all_gather(jnp.concatenate((seg_state, log_rows), axis=1), 'seg_lo')  17.3 us
    all_gather x1, blocking collectives, body(): third = lax.all_gather(seg_back, 'seg_lo')  16 us
    dot_general x16, matrix products, mm(): lax.dot_general(a, b, (((1,), (0,)), ((), ())), preferred_element_type=jn...  7.86 us
    dot_general x16, matrix products, tm(): lax.dot_general(a, b, (((0,), (0,)), ((), ())), preferred_element_type=jn...  6.78 us

profile of v5, /device:TPU:6, one launch (start us, length us, event | category | flops | bytes accessed | tf_op | source)
XLA Modules:
  0.0 184.8 jit_solution(16080258136791420082)
XLA Ops:
  0.6 0.8 fusion.115
  3.9 1.3 convolution_bitcast_fusion.4
  7.1 1.3 convolution_bitcast_fusion.5
  10.2 1.2 convolution_bitcast_fusion.2
  16.3 17.3 %all-gather = f32[8,136,128]{2,1,0:T(8,128)S(1)} all-gather(f32[2,136,128]{2,1,0:T(8,128)S(1)} %pad_maximum_fusion), channel_id=2, replica_groups=mesh['seg_hi'=4,'seg_lo'=4,'exp_y'=4,'exp_x'=4,'exp_core'=2] {'seg_lo'}, dimensions={0}, use_global_device_ids=true | all-gather | bytes 696320 | tf_op jit(solution)/shard_map/all_gather | solution.py:73
  34.6 1.3 select_reduce_fusion.6
  36.3 32.9 %all-gather.1 = f32[8,136,128]{2,1,0:T(8,128)S(1)} all-gather(f32[2,136,128]{2,1,0:T(8,128)S(1)} %pad_maximum_fusion.1), channel_id=3, replica_groups=mesh['seg_hi'=4,'seg_lo'=4,'exp_y'=4,'exp_x'=4,'exp_core'=2] {'seg_hi'}, dimensions={0}, use_global_device_ids=true | all-gather | bytes 696320 | tf_op jit(solution)/shard_map/all_gather | solution.py:82
  75.0 0.8 fusion.113
  76.0 1.0 copy.96
  77.7 1.5 multiply_reduce_fusion.11
  81.5 0.8 copy-done.5
  82.2 1.0 fusion.85
  83.4 1.1 copy.95
  85.1 1.9 %multiply_reduce_fusion.12 = (f32[512]{0:T(512)S(1)}, f32[512]{0:T(512)S(1)}, f32[512]{0:T(512)S(1)}, f32[512]{0:T(512)S(1)}, f32[512,128]{0,1:T(8,128)}) fusion(bf16[512,128]{0,1:T(8,128)(2,1)S(1)} %copy.93, f32[128]{0:T(128)S(1)} %copy-done.59, f32[512,128]{0,1:T(8,128)S(1)} %fusion.23, bf16[512,128]{0,1:T(8,128)(2,1)S(1)} %copy.95, ...), kind=kOutput, calls=%fused_computation.117 | convolution fusion | flops 17692672 | bytes 1223168 | tf_op jit(solution)/shard_map/dot_general | solution.py:21
  89.1 2.5 %psum.21 = f32[2,1024]{1,0:T(2,128)S(1)} all-reduce(f32[2,1024]{1,0:T(2,128)S(1)} %pad_maximum_fusion.3), channel_id=1, replica_groups=mesh['seg_hi'=4,'seg_lo'=4,'exp_y'=4,'exp_x'=4,'exp_core'=2] {'exp_core'}, use_global_device_ids=true, to_apply=%region_25.26 | all-reduce | flops 2048 | bytes 16384 | tf_op jit(solution)/shard_map/psum | solution.py:110
  91.6 7.6 %psum.22 = f32[2,1024]{1,0:T(2,128)S(1)} all-reduce(f32[2,1024]{1,0:T(2,128)S(1)} %psum.21), channel_id=1, replica_groups=mesh['seg_hi'=4,'seg_lo'=4,'exp_y'=4,'exp_x'=4,'exp_core'=2] {'exp_x'}, use_global_device_ids=true, to_apply=%region_26.27 | all-reduce | flops 2048 | bytes 16384 | tf_op jit(solution)/shard_map/psum | solution.py:110
  99.2 10.9 %psum.23 = f32[2,1024]{1,0:T(2,128)S(1)} all-reduce(f32[2,1024]{1,0:T(2,128)S(1)} %psum.22), channel_id=1, replica_groups=mesh['seg_hi'=4,'seg_lo'=4,'exp_y'=4,'exp_x'=4,'exp_core'=2] {'exp_y'}, use_global_device_ids=true, to_apply=%region_27.28 | all-reduce | flops 2048 | bytes 16384 | tf_op jit(solution)/shard_map/psum | solution.py:110
  110.8 2.5 %subtract_convert_fusion.1 = (bf16[512,128]{0,1:T(8,128)(2,1)S(1)}, bf16[512,128]{0,1:T(8,128)(2,1)}, bf16[512,128]{0,1:T(8,128)(2,1)}, bf16[512,128]{0,1:T(8,12...) fusion(bf16[512,128]{0,1:T(8,128)(2,1)} %copy-done.19, ...), kind=kLoop, calls=%fused_computation.99 | loop fusion | flops 3145728 | bytes 2630656 | tf_op jit(solution)/shard_map/convert_element_type | solution.py:123
  114.1 0.8 copy-done.9
  115.2 0.8 copy-done.13
  116.6 16.0 %all_gather.26 = f32[4,2,128,128]{3,2,1,0:T(8,128)S(1)} all-gather(f32[1,2,128,128]{3,2,1,0:T(8,128)S(1)} %maximum_add_fusion.2), channel_id=1, replica_groups=mesh['seg_hi'=4,'seg_lo'=4,'exp_y'=4,'exp_x'=4,'exp_core'=2] {'seg_lo'}, dimensions={0}, use_global_device_ids=true | all-gather | bytes 655360 | tf_op jit(solution)/shard_map/all_gather | solution.py:130
  132.7 1.3 copy.81
  135.2 1.3 copy.83
  136.6 1.5 multiply_reduce_fusion.1
  138.1 22.6 %all-gather.2 = f32[8,128,128]{2,1,0:T(8,128)S(1)} all-gather(f32[2,128,128]{2,1,0:T(8,128)S(1)} %get-tuple-element.22), channel_id=4, replica_groups=mesh['seg_hi'=4,'seg_lo'=4,'exp_y'=4,'exp_x'=4,'exp_core'=2] {'seg_hi'}, dimensions={0}, use_global_device_ids=true | all-gather | bytes 655360 | tf_op jit(solution)/shard_map/all_gather | solution.py:135
  162.1 1.3 copy.82
  163.4 0.8 multiply_reduce_fusion
  169.8 1.0 copy.87
  176.7 0.8 copy-done.7
  177.8 1.0 copy.86
  182.7 1.0 copy.85
  183.8 1.0 copy.84
  (261 shorter events, 41.5 us)
Async XLA Ops:
  0.6 9.6 %copy-start.1 = (bf16[1024,256]{1,0:T(8,128)(2,1)S(1)}, bf16[1024,256]{1,0:T(8,128)(2,1)}, u32[]{:S(2)}) copy-start(bf16[1024,256]{1,0:T(8,128)(2,1)} %param.8) | copy-start | bytes 1572868
  2.1 71.6 %copy-start.47 = (f32[512]{0:T(512)}, f32[512]{0:T(512)S(1)}, u32[]{:S(2)}) copy-start(f32[512]{0:T(512)S(1)} %get-tuple-element.41) | copy-start | bytes 6148
  5.2 8.2 %copy-start.2 = (bf16[1024,256]{1,0:T(8,128)(2,1)S(1)}, bf16[1024,256]{1,0:T(8,128)(2,1)}, u32[]{:S(2)}) copy-start(bf16[1024,256]{1,0:T(8,128)(2,1)} %param.7) | copy-start | bytes 1572868
  7.1 1.3 copy-start.39
  9.0 63.8 %copy-start.49 = (f32[512]{0:T(512)}, f32[512]{0:T(512)S(1)}, u32[]{:S(2)}) copy-start(f32[512]{0:T(512)S(1)} %get-tuple-element.47) | copy-start | bytes 6148
  10.2 1.2 copy-start.37
  70.7 2.1 %copy-start = (bf16[1024,256]{1,0:T(8,128)(2,1)S(1)}, bf16[1024,256]{1,0:T(8,128)(2,1)}, u32[]{:S(2)}) copy-start(bf16[1024,256]{1,0:T(8,128)(2,1)} %param.6) | copy-start | bytes 1572868
  72.8 4.8 %copy-start.20 = (bf16[2,128,128]{2,1,0:T(8,128)(2,1)}, bf16[2,128,128]{2,1,0:T(8,128)(2,1)S(1)}, u32[]{:S(2)}) copy-start(bf16[2,128,128]{2,1,0:T(8,128)(2,1)S(1)} %get-tuple-element.68) | copy-start | bytes 196612
  74.0 1.0 copy-start.27
  76.0 1.0 copy-start.68
  77.0 2.2 %copy-start.17 = (bf16[512,128]{0,1:T(8,128)(2,1)}, bf16[512,128]{0,1:T(8,128)(2,1)S(1)}, u32[]{:S(2)}) copy-start(bf16[512,128]{0,1:T(8,128)(2,1)S(1)} %copy.96) | copy-start | bytes 393220
  77.6 1.6 copy-start.57
  77.6 1.6 copy-start.55
  79.5 1.1 copy-start.3
  79.5 0.9 copy-start.23
  82.2 1.0 copy-start.33
  83.4 1.1 copy-start.18
  84.4 2.6 %copy-start.19 = (bf16[512,128]{0,1:T(8,128)(2,1)}, bf16[512,128]{0,1:T(8,128)(2,1)S(1)}, u32[]{:S(2)}) copy-start(bf16[512,128]{0,1:T(8,128)(2,1)S(1)} %copy.95) | copy-start | bytes 393220
  85.1 1.9 %copy-start.46 = (f32[512]{0:T(512)S(1)}, f32[512]{0:T(512)}, u32[]{:S(2)}) copy-start(f32[512]{0:T(512)} %get-tuple-element.24) | copy-start | bytes 6148
  114.0 0.9 copy-start.9
  138.1 22.7 %copy-start.70 = (pred[4]{0:T(512)(128)(4,1)S(1)}, pred[4]{0:T(512)(128)(4,1)}, u32[]{:S(2)}) copy-start(pred[4]{0:T(512)(128)(4,1)} %copy-done.69) | copy-start | bytes 16
  163.4 0.9 copy-start.28
  163.4 0.9 copy-start.64
  164.2 1.1 copy-start.6
  164.4 9.4 %copy-start.25 = (bf16[2,128,128]{2,1,0:T(8,128)(2,1)}, bf16[2,128,128]{2,1,0:T(8,128)(2,1)S(1)}, u32[]{:S(2)}) copy-start(bf16[2,128,128]{2,1,0:T(8,128)(2,1)S(1)} %get-tuple-element.67) | copy-start | bytes 196612
  165.0 0.9 copy-start.14
  167.6 1.0 copy-start.4
  181.0 1.1 copy-start.8
  182.6 1.0 copy-start.29
  182.7 1.0 copy-start.30
  182.7 1.0 copy-start.31
  182.7 1.1 copy-start.32
  (39 other events, 28.1 us)

commit v6 on v2

--- a/solution.py
+++ b/solution.py
@@ -5,6 +5,7 @@
 
 BLK = 512
 EXP_PARTS = ("exp_y", "exp_x", "exp_core")
+SEG_PARTS = ("seg_hi", "seg_mid", "seg_lo")
 
 
 EPS = 1e-06
@@ -18,6 +19,12 @@
     lower = token_place[:, None] >= token_place[None, :]
     mask = jnp.where(lower, jnp.exp(jnp.minimum(spread, 0.0)), 0.0)
     return (cumulative, cumulative[..., -1], mask)
+
+
+def fade_weights(order, valid, logs, limit, extra=0.0):
+    between = order & limit
+    summed = jnp.sum(jnp.where(between[:, :, None], logs[None, :, :], 0.0), axis=1) + extra
+    return jnp.where(valid[:, None], jnp.exp(summed), 0.0)
 
 
 def body(queries, keys, values, log_decay, gain, d_out):
@@ -42,30 +49,30 @@
         "bshe,bshf->bhef", key_weighted, vblocks, preferred_element_type=jnp.float32
     )
     block_fade = jnp.exp(totals)
-    seg_count = lax.axis_size("seg")
-    here = lax.axis_index("seg")
     seg_state = block_state[0]
     for block in range(1, count):
         seg_state = block_fade[block][:, None, None] * seg_state + block_state[block]
     seg_log = jnp.sum(log_decay, axis=-1)
-    log_rows = jnp.broadcast_to(seg_log[:, None, None], (local_heads, 8, head_width))
-    gathered = lax.all_gather(jnp.concatenate((seg_state, log_rows), axis=1), "seg")
-    all_states = gathered[:, :, :head_width, :]
-    all_logs = gathered[:, :, head_width, 0]
-    places = jnp.arange(seg_count)
-    between_fwd = (places[:, None] < places[None, :]) & (places[None, :] < here)
-    between_bwd = (places[:, None] > places[None, :]) & (places[None, :] > here)
-    weight_fwd = jnp.where(
-        (places < here)[:, None],
-        jnp.exp(jnp.sum(jnp.where(between_fwd[:, :, None], all_logs[None, :, :], 0.0), axis=1)),
-        0.0,
-    )
-    weight_bwd = jnp.where(
-        (places > here)[:, None],
-        jnp.exp(jnp.sum(jnp.where(between_bwd[:, :, None], all_logs[None, :, :], 0.0), axis=1)),
-        0.0,
-    )
-    entering = jnp.sum(weight_fwd[:, :, None, None] * all_states, axis=0)
+    level_logs = []
+    level_here = []
+    entering = jnp.zeros_like(seg_state)
+    offset = jnp.zeros_like(seg_log)
+    unit_state, unit_log = seg_state, seg_log
+    for axis in SEG_PARTS[::-1]:
+        here = lax.axis_index(axis)
+        places = jnp.arange(lax.axis_size(axis))
+        log_rows = jnp.broadcast_to(unit_log[:, None, None], (local_heads, 8, head_width))
+        gathered = lax.all_gather(jnp.concatenate((unit_state, log_rows), axis=1), axis)
+        states = gathered[:, :, :head_width, :]
+        logs = gathered[:, :, head_width, 0]
+        level_logs.append(logs)
+        level_here.append(here)
+        inside = fade_weights(places[:, None] < places[None, :], places < here, logs, places[None, :] < here, offset)
+        entering = entering + jnp.sum(inside[:, :, None, None] * states, axis=0)
+        offset = offset + jnp.sum(jnp.where((places < here)[:, None], logs, 0.0), axis=0)
+        to_end = fade_weights(places[:, None] < places[None, :], places >= 0, logs, True)
+        unit_state = jnp.sum(to_end[:, :, None, None] * states, axis=0)
+        unit_log = jnp.sum(logs, axis=0)
     held_list = []
     running = entering
     for block in range(count):
@@ -99,8 +106,17 @@
     seg_back = back_terms[count - 1]
     for block in range(count - 2, -1, -1):
         seg_back = back_terms[block] + block_fade[block][:, None, None] * seg_back
-    all_backs = lax.all_gather(seg_back, "seg")
-    leaving = jnp.sum(weight_bwd[:, :, None, None] * all_backs, axis=0)
+    leaving = jnp.zeros_like(seg_back)
+    offset = jnp.zeros_like(seg_log)
+    unit_back = seg_back
+    for axis, logs, here in zip(SEG_PARTS[::-1], level_logs, level_here):
+        places = jnp.arange(lax.axis_size(axis))
+        backs = lax.all_gather(unit_back, axis)
+        inside = fade_weights(places[:, None] > places[None, :], places > here, logs, places[None, :] > here, offset)
+        leaving = leaving + jnp.sum(inside[:, :, None, None] * backs, axis=0)
+        offset = offset + jnp.sum(jnp.where((places > here)[:, None], logs, 0.0), axis=0)
+        to_start = fade_weights(places[:, None] > places[None, :], places >= 0, logs, True)
+        unit_back = jnp.sum(to_start[:, :, None, None] * backs, axis=0)
     exit_list = [None] * count
     running = leaving
     for block in range(count - 1, -1, -1):
@@ -132,9 +148,9 @@
 
 
 def solution(mesh):
-    parts = mesh.devices.reshape(mesh.devices.shape[0], 4, -1, 2)
-    split = jax.sharding.Mesh(parts, ("seg",) + EXP_PARTS)
-    rows_heads = P("seg", EXP_PARTS)
-    in_specs = (rows_heads, rows_heads, rows_heads, P(EXP_PARTS, "seg"), P(EXP_PARTS), rows_heads)
+    parts = mesh.devices.reshape(2, 2, -1, 4, mesh.devices.shape[1] // 8, 2)
+    split = jax.sharding.Mesh(parts, SEG_PARTS + EXP_PARTS)
+    rows_heads = P(SEG_PARTS, EXP_PARTS)
+    in_specs = (rows_heads, rows_heads, rows_heads, P(EXP_PARTS, SEG_PARTS), P(EXP_PARTS), rows_heads)
     out_specs = (rows_heads, rows_heads, rows_heads, rows_heads)
     return jax.shard_map(body, mesh=split, in_specs=in_specs, out_specs=out_specs, check_vma=False)

time: 212 us -> 171 us (0.81)
  waiting for transfers between devices: 127 us -> 0 us
  blocking collectives: 20.8 us -> 126 us
  between operations: 14.5 us -> 1.17 us
  matrix products: 15 us -> 10.7 us
    all_gather x2 -> x0, waiting for transfers between devices: 127 us -> none  [the longest x1 73.1 us: body(): lax.all_gather(jnp.concatenate((seg_state, log_rows), axis=1), 'seg')]
    all_gather x0 -> x6, blocking collectives: none -> 105 us  [the longest x3 59.6 us: body(): lax.all_gather(jnp.concatenate((unit_state, log_rows), axis=1), axis)]
    exp x0 -> x6, local copies, waits for them, and re-layouts: none -> 3.39 us  [fade_weights(): return jnp.where(valid[:, None], jnp.exp(summed), 0.0)]
    unnamed x46 -> x42, local copies, waits for them, and re-layouts: 5.24 us -> 3.6 us
    reduce_sum x3 -> x11, other arithmetic: 4.37 us -> 5.27 us  [the longest x3 2.11 us: body(): leaving = leaving + jnp.sum(inside[:, :, None, None] * backs, axis=0)]
  transfers between devices with their start and end apart: 2 -> 0, of which waited for: 2 -> 0; matrix products, arithmetic and copies ran while one was open for 9% -> 0% of each run, Pallas kernels for 0% -> 0%
where the time goes in v6:
time: 171 us; the launch traced here: 170 us
  blocking collectives  126 us (74%)
  local copies, waits for them, and re-layouts  19.2 us (11%)
  other arithmetic  13 us (8%)
  matrix products  10.7 us (6%)
    all_gather x3, blocking collectives, body(): lax.all_gather(jnp.concatenate((unit_state, log_rows), axis=1), axis)  59.6 us
    all_gather x3, blocking collectives, body(): backs = lax.all_gather(unit_back, axis)  45.8 us
    psum x3, blocking collectives, body(): totals_exp = lax.psum(totals_exp, axis)  20.9 us
    unnamed x42, local copies, waits for them, and re-layouts  3.6 us

profile of v6, /device:TPU:6, one launch (start us, length us, event | category | flops | bytes accessed | tf_op | source)
XLA Modules:
  0.0 170.3 jit_solution(18080962183282470933)
XLA Ops:
  1.4 1.2 reduce-window.6
  3.8 1.2 reshape.596
  5.0 1.4 reshape.600
  6.4 0.9 fusion.12
  7.9 17.3 %all-gather = f32[8,136,128]{2,1,0:T(8,128)S(1)} all-gather(f32[2,136,128]{2,1,0:T(8,128)S(1)} %pad_maximum_fusion), channel_id=2, replica_groups=mesh['seg_hi'=2,'seg_mid'=2,'seg_lo'=4,'exp_y'=4,'exp_x'=4,'exp_core'=2]..., dimensions={0}, use_global_device_ids=true | all-gather | bytes 696320 | tf_op jit(solution)/shard_map/all_gather | solution.py:65
  27.3 18.1 %all-gather.1 = f32[4,136,128]{2,1,0:T(8,128)S(1)} all-gather(f32[2,136,128]{2,1,0:T(8,128)S(1)} %pad_maximum_fusion.1), channel_id=3, replica_groups=mesh['seg_hi'=2,'seg_mid'=2,'seg_lo'=4,'exp_y'=4,'exp_x'=4,'exp_core'=2]..., dimensions={0}, use_global_device_ids=true | all-gather | bytes 417792 | tf_op jit(solution)/shard_map/all_gather | solution.py:65
  47.1 24.2 %all-gather.2 = f32[4,136,128]{2,1,0:T(8,128)S(1)} all-gather(f32[2,136,128]{2,1,0:T(8,128)S(1)} %pad_maximum_fusion.2), channel_id=4, replica_groups=mesh['seg_hi'=2,'seg_mid'=2,'seg_lo'=4,'exp_y'=4,'exp_x'=4,'exp_core'=2]..., dimensions={0}, use_global_device_ids=true | all-gather | bytes 417792 | tf_op jit(solution)/shard_map/all_gather | solution.py:65
  73.1 2.3 %multiply_convert_fusion.1 = bf16[2,2,512,512]{3,2,1,0:T(8,128)(2,1)S(1)} fusion(bf16[2,512,2,128]{1,3,2,0:T(8,128)(2,1)S(1)} %copy.159, f32[2,2,512]{2,1,0:T(2,128)} %copy-done.10, pred[512,512]{1,0:T(8,128)(4,1)S(1)} %iota_compare_fusion, bf16[2,512,2,128]{3,2,1,0:T(2,128)(2,1)S(1)} %reshape.596), kind=kOutput, calls=%fused_computation.1 | convolution fusion | flops 273678336 | bytes 3416064 | tf_op jit(solution)/shard_map/bthe,bshe->bhts/dot_general | solution.py:44
  75.4 0.8 convolution_bitcast_fusion.3
  76.3 1.4 multiply_reduce_fusion
  77.6 1.5 copy.150
  79.2 1.3 fusion.11
  80.5 2.5 %psum.21 = f32[2,1024]{1,0:T(2,128)S(1)} all-reduce(f32[2,1024]{1,0:T(2,128)S(1)} %pad_maximum_fusion.9), channel_id=1, replica_groups=mesh['seg_hi'=2,'seg_mid'=2,'seg_lo'=4,'exp_y'=4,'exp_x'=4,'exp_core'=2]..., use_global_device_ids=true, to_apply=%region_19.20 | all-reduce | flops 2048 | bytes 16384 | tf_op jit(solution)/shard_map/psum | solution.py:92
  83.0 7.6 %psum.22 = f32[2,1024]{1,0:T(2,128)S(1)} all-reduce(f32[2,1024]{1,0:T(2,128)S(1)} %psum.21), channel_id=1, replica_groups=mesh['seg_hi'=2,'seg_mid'=2,'seg_lo'=4,'exp_y'=4,'exp_x'=4,'exp_core'=2]..., use_global_device_ids=true, to_apply=%region_20.21 | all-reduce | flops 2048 | bytes 16384 | tf_op jit(solution)/shard_map/psum | solution.py:92
  90.6 10.9 %psum.23 = f32[2,1024]{1,0:T(2,128)S(1)} all-reduce(f32[2,1024]{1,0:T(2,128)S(1)} %psum.22), channel_id=1, replica_groups=mesh['seg_hi'=2,'seg_mid'=2,'seg_lo'=4,'exp_y'=4,'exp_x'=4,'exp_core'=2]..., use_global_device_ids=true, to_apply=%region_21.22 | all-reduce | flops 2048 | bytes 16384 | tf_op jit(solution)/shard_map/psum | solution.py:92
  101.5 2.4 %subtract_convert_fusion = (bf16[1024,256]{1,0:T(8,128)(2,1)}, bf16[1024,256]{1,0:T(8,128)(2,1)}) fusion(bf16[1024,256]{1,0:T(8,128)(2,1)} %param.11, f32[128,8,2,128]{3,2,1,0:T(2,128)S(1)} %bitcast.126, f32[1024]{0:T(1024)S(1)} %bitcast.143, f32[1024]{0:T(1024)S(1)} %bitcast.144, f32[256]{0:T(256)S(1)} %copy-done.17), kind=kLoop, calls=%fused_computation.26 | loop fusion | flops 3145728 | bytes 2630656 | tf_op jit(solution)/shard_map/convert_element_type | solution.py:100
  103.9 2.0 %reshape.602 = bf16[2,512,2,128]{3,2,1,0:T(2,128)(2,1)} reshape(bf16[1024,256]{1,0:T(8,128)(2,1)} %get-tuple-element.28) | data formatting | bytes 1048576 | tf_op jit(solution)/shard_map/reshape | solution.py:101
  105.9 1.3 copy.166
  108.2 15.4 %all_gather.40 = f32[4,2,128,128]{3,2,1,0:T(8,128)} all-gather(f32[1,2,128,128]{3,2,1,0:T(8,128)S(1)} %slice_add_fusion), channel_id=1, replica_groups=mesh['seg_hi'=2,'seg_mid'=2,'seg_lo'=4,'exp_y'=4,'exp_x'=4,'exp_core'=2]..., dimensions={0}, use_global_device_ids=true | all-gather | bytes 655360 | tf_op jit(solution)/shard_map/all_gather | solution.py:114
  123.7 1.3 copy.161
  125.0 1.3 exp.97
  126.3 1.3 copy.162
  127.6 1.2 multiply_reduce_fusion.2
  128.8 12.7 %all-gather.3 = f32[4,128,128]{2,1,0:T(8,128)S(1)} all-gather(f32[2,128,128]{2,1,0:T(8,128)S(1)} %get-tuple-element.7), channel_id=5, replica_groups=mesh['seg_hi'=2,'seg_mid'=2,'seg_lo'=4,'exp_y'=4,'exp_x'=4,'exp_core'=2]..., dimensions={0}, use_global_device_ids=true | all-gather | bytes 393216 | tf_op jit(solution)/shard_map/all_gather | solution.py:114
  143.1 17.6 %all-gather.4 = f32[4,128,128]{2,1,0:T(8,128)S(1)} all-gather(f32[2,128,128]{2,1,0:T(8,128)S(1)} %get-tuple-element.13), channel_id=6, replica_groups=mesh['seg_hi'=2,'seg_mid'=2,'seg_lo'=4,'exp_y'=4,'exp_x'=4,'exp_core'=2]..., dimensions={0}, use_global_device_ids=true | all-gather | bytes 393216 | tf_op jit(solution)/shard_map/all_gather | solution.py:114
  160.9 0.9 convolution_bitcast_fusion
  162.8 0.9 copy.213
  163.7 1.4 multiply_convert_fusion
  165.1 0.9 convolution_bitcast_fusion.1
  167.0 0.9 copy.214
  167.9 0.8 convolution_bitcast_fusion.2
  169.4 0.9 copy.215
  (108 shorter events, 13.4 us)
Async XLA Ops:
  3.2 0.6 copy-start.10
  3.8 3.6 %copy-start.12 = (f32[2,1024]{1,0:T(2,128)S(1)}, f32[2,1024]{1,0:T(2,128)}, u32[]{:S(2)}) copy-start(f32[2,1024]{1,0:T(2,128)} %param.9) | copy-start | bytes 24580
  5.0 68.1 %copy-start.2 = (bf16[2,512,2,128]{3,2,1,0:T(2,128)(2,1)}, bf16[2,512,2,128]{3,2,1,0:T(2,128)(2,1)S(1)}, u32[]{:S(2)}) copy-start(bf16[2,512,2,128]{3,2,1,0:T(2,128)(2,1)S(1)} %reshape.596) | copy-start | bytes 1572868
  6.4 21.0 %copy-start.4 = (bf16[2,512,2,128]{3,2,1,0:T(2,128)(2,1)}, bf16[2,512,2,128]{3,2,1,0:T(2,128)(2,1)S(1)}, u32[]{:S(2)}) copy-start(bf16[2,512,2,128]{3,2,1,0:T(2,128)(2,1)S(1)} %reshape.600) | copy-start | bytes 1572868
  7.3 0.6 copy-start.13
  7.3 65.0 %copy-start.15 = (f32[2]{0:T(128)}, f32[2]{0:T(128)S(1)}, u32[]{:S(2)}) copy-start(f32[2]{0:T(128)S(1)} %get-tuple-element.37) | copy-start | bytes 28
  27.1 45.4 %copy-start.7 = (bf16[1024,256]{1,0:T(8,128)(2,1)S(1)}, bf16[1024,256]{1,0:T(8,128)(2,1)}, u32[]{:S(2)}) copy-start(bf16[1024,256]{1,0:T(8,128)(2,1)} %param.6) | copy-start | bytes 1572868
  73.0 3.3 %copy-start = (bf16[2,512,2,128]{1,3,2,0:T(8,128)(2,1)}, bf16[2,512,2,128]{1,3,2,0:T(8,128)(2,1)S(1)}, u32[]{:S(2)}) copy-start(bf16[2,512,2,128]{1,3,2,0:T(8,128)(2,1)S(1)} %copy.159) | copy-start | bytes 1572868
  73.1 2.3 %copy-start.8 = (pred[512,512]{1,0:T(8,128)(4,1)}, pred[512,512]{1,0:T(8,128)(4,1)S(1)}, u32[]{:S(2)}) copy-start(pred[512,512]{1,0:T(8,128)(4,1)S(1)} %iota_compare_fusion) | copy-start | bytes 786436
  73.1 2.3 %copy-start.5 = (bf16[2,512,2,128]{3,2,1,0:T(2,128)(2,1)S(1)}, bf16[2,512,2,128]{3,2,1,0:T(2,128)(2,1)}, u32[]{:S(2)}) copy-start(bf16[2,512,2,128]{3,2,1,0:T(2,128)(2,1)} %copy-done.4) | copy-start | bytes 1572868
  76.3 2.9 %copy-start.17 = (f32[256]{0:T(256)S(1)}, f32[256]{0:T(256)}, u32[]{:S(2)}) copy-start(f32[256]{0:T(256)} %param.10) | copy-start | bytes 3076
  103.9 3.3 %copy-start.1 = (bf16[2,512,2,128]{1,3,2,0:T(8,128)(2,1)S(1)}, bf16[2,512,2,128]{1,3,2,0:T(8,128)(2,1)}, u32[]{:S(2)}) copy-start(bf16[2,512,2,128]{1,3,2,0:T(8,128)(2,1)} %copy-done) | copy-start | bytes 1572868
  127.6 33.1 %copy-start.16 = (f32[2,2]{1,0:T(2,128)S(1)}, f32[2,2]{1,0:T(2,128)}, u32[]{:S(2)}) copy-start(f32[2,2]{1,0:T(2,128)} %exponential_select_fusion.1) | copy-start | bytes 52
  127.6 33.1 %copy-start.14 = (f32[2]{0:T(128)S(1)}, f32[2]{0:T(128)}, u32[]{:S(2)}) copy-start(f32[2]{0:T(128)} %copy-done.13) | copy-start | bytes 28
  160.8 1.0 copy-start.3
  161.9 1.8 %copy-start.6 = (bf16[2,512,2,128]{3,2,1,0:T(2,128)(2,1)S(1)}, bf16[2,512,2,128]{3,2,1,0:T(2,128)(2,1)}, u32[]{:S(2)}) copy-start(bf16[2,512,2,128]{3,2,1,0:T(2,128)(2,1)} %copy-done.4) | copy-start | bytes 1572868
  161.9 1.8 %copy-start.9 = (pred[512,512]{1,0:T(8,128)(4,1)S(1)}, pred[512,512]{1,0:T(8,128)(4,1)}, u32[]{:S(2)}) copy-start(pred[512,512]{1,0:T(8,128)(4,1)} %copy-done.8) | copy-start | bytes 786436
  161.9 1.8 %copy-start.11 = (f32[2,2,512]{2,1,0:T(2,128)S(1)}, f32[2,2,512]{2,1,0:T(2,128)}, u32[]{:S(2)}) copy-start(f32[2,2,512]{2,1,0:T(2,128)} %copy-done.10) | copy-start | bytes 24580

commit v7 on v3

--- a/solution.py
+++ b/solution.py
@@ -32,21 +32,27 @@
     local_heads = log_decay.shape[0]
     head_width = width // local_heads
     count = rows // BLK
-    shape = (count, BLK, local_heads, head_width)
-    qblocks = queries.reshape(shape)
-    kblocks = keys.reshape(shape)
-    vblocks = values.reshape(shape)
+    view = (count, BLK, width)
     lblocks = log_decay.reshape(local_heads, count, BLK).transpose(1, 0, 2)
     cumulative, totals, mask = decay_parts(lblocks)
-    grow = jnp.exp(cumulative).transpose(0, 2, 1)[..., None]
-    shrink = jnp.exp(totals[:, None, :] - cumulative.transpose(0, 2, 1))[..., None]
-    scores = (
-        jnp.einsum("bthe,bshe->bhts", qblocks, kblocks, preferred_element_type=jnp.float32) * mask
-    ).astype(jnp.bfloat16)
-    inner = jnp.einsum("bhts,bshf->bthf", scores, vblocks, preferred_element_type=jnp.float32)
-    key_weighted = (kblocks * shrink).astype(jnp.bfloat16)
-    block_state = jnp.einsum(
-        "bshe,bshf->bhef", key_weighted, vblocks, preferred_element_type=jnp.float32
+    qv, kv, vv, uv = (a.reshape(view) for a in (queries, keys, values, d_out))
+    cols = [slice(head * head_width, (head + 1) * head_width) for head in range(local_heads)]
+    qh = [qv[:, :, c] for c in cols]
+    kh = [kv[:, :, c] for c in cols]
+    vh = [vv[:, :, c] for c in cols]
+    grow = [jnp.exp(cumulative[:, head, :])[..., None] for head in range(local_heads)]
+    shrink = [jnp.exp(totals[:, head, None] - cumulative[:, head, :])[..., None] for head in range(local_heads)]
+    scores = [
+        (jnp.einsum("bte,bse->bts", qh[h], kh[h], preferred_element_type=jnp.float32) * mask[:, h]).astype(jnp.bfloat16)
+        for h in range(local_heads)
+    ]
+    inner = [jnp.einsum("bts,bsf->btf", scores[h], vh[h], preferred_element_type=jnp.float32) for h in range(local_heads)]
+    block_state = jnp.stack(
+        [
+            jnp.einsum("bse,bsf->bef", (kh[h] * shrink[h]).astype(jnp.bfloat16), vh[h], preferred_element_type=jnp.float32)
+            for h in range(local_heads)
+        ],
+        axis=1,
     )
     block_fade = jnp.exp(totals)
     seg_state = block_state[0]
@@ -81,10 +87,13 @@
         held_list.append(running.astype(jnp.bfloat16))
         running = block_fade[block][:, None, None] * running + block_state[block]
     held = jnp.stack(held_list)
-    attended = inner + grow * jnp.einsum(
-        "bthe,bhef->bthf", qblocks, held, preferred_element_type=jnp.float32
-    )
-    attended = attended.reshape(rows, width)
+    attended = jnp.concatenate(
+        [
+            inner[h] + grow[h] * jnp.einsum("bte,bef->btf", qh[h], held[:, h], preferred_element_type=jnp.float32)
+            for h in range(local_heads)
+        ],
+        axis=-1,
+    ).reshape(rows, width)
     upstream = d_out.astype(jnp.float32)
     partial = jnp.stack(
         (jnp.sum(attended * attended, axis=-1), jnp.sum(gain * upstream * attended, axis=-1))
@@ -100,10 +109,14 @@
         gain * upstream * inv_rms
         - attended * inv_rms * inv_rms * inv_rms * cross[:, None] / features
     ).astype(jnp.bfloat16)
-    grad_blocks = grad_attended.reshape(shape)
-    query_weighted = (qblocks * grow).astype(jnp.bfloat16)
-    back_terms = jnp.einsum(
-        "bthe,bthf->bhef", query_weighted, grad_blocks, preferred_element_type=jnp.float32
+    gv = grad_attended.reshape(view)
+    gh = [gv[:, :, c] for c in cols]
+    back_terms = jnp.stack(
+        [
+            jnp.einsum("bte,btf->bef", (qh[h] * grow[h]).astype(jnp.bfloat16), gh[h], preferred_element_type=jnp.float32)
+            for h in range(local_heads)
+        ],
+        axis=1,
     )
     seg_back = back_terms[count - 1]
     for block in range(count - 2, -1, -1):
@@ -125,28 +138,25 @@
         exit_list[block] = running.astype(jnp.bfloat16)
         running = back_terms[block] + block_fade[block][:, None, None] * running
     exits = jnp.stack(exit_list)
-    grad_scores = (
-        jnp.einsum("bthf,bshf->bhts", grad_blocks, vblocks, preferred_element_type=jnp.float32)
-        * mask
-    ).astype(jnp.bfloat16)
-    grad_q = jnp.einsum("bhts,bshe->bthe", grad_scores, kblocks, preferred_element_type=jnp.float32)
-    grad_q = grad_q + grow * jnp.einsum(
-        "bthf,bhef->bthe", grad_blocks, held, preferred_element_type=jnp.float32
-    )
-    grad_k = jnp.einsum("bhts,bthe->bshe", grad_scores, qblocks, preferred_element_type=jnp.float32)
-    grad_k = grad_k + shrink * jnp.einsum(
-        "bshf,bhef->bshe", vblocks, exits, preferred_element_type=jnp.float32
-    )
-    grad_v = jnp.einsum("bhts,bthf->bshf", scores, grad_blocks, preferred_element_type=jnp.float32)
-    grad_v = grad_v + shrink * jnp.einsum(
-        "bshe,bhef->bshf", kblocks, exits, preferred_element_type=jnp.float32
-    )
-    return (
-        out,
-        grad_q.reshape(rows, width).astype(jnp.bfloat16),
-        grad_k.reshape(rows, width).astype(jnp.bfloat16),
-        grad_v.reshape(rows, width).astype(jnp.bfloat16),
-    )
+    grad_q, grad_k, grad_v = [], [], []
+    for h in range(local_heads):
+        grad_scores = (
+            jnp.einsum("btf,bsf->bts", gh[h], vh[h], preferred_element_type=jnp.float32) * mask[:, h]
+        ).astype(jnp.bfloat16)
+        gq = jnp.einsum("bts,bse->bte", grad_scores, kh[h], preferred_element_type=jnp.float32)
+        gq = gq + grow[h] * jnp.einsum("btf,bef->bte", gh[h], held[:, h], preferred_element_type=jnp.float32)
+        gk = jnp.einsum("bts,bte->bse", grad_scores, qh[h], preferred_element_type=jnp.float32)
+        gk = gk + shrink[h] * jnp.einsum("bsf,bef->bse", vh[h], exits[:, h], preferred_element_type=jnp.float32)
+        gvv = jnp.einsum("bts,btf->bsf", scores[h], gh[h], preferred_element_type=jnp.float32)
+        gvv = gvv + shrink[h] * jnp.einsum("bse,bef->bsf", kh[h], exits[:, h], preferred_element_type=jnp.float32)
+        grad_q.append(gq.astype(jnp.bfloat16))
+        grad_k.append(gk.astype(jnp.bfloat16))
+        grad_v.append(gvv.astype(jnp.bfloat16))
+
+    def whole(parts):
+        return jnp.concatenate(parts, axis=-1).reshape(rows, width)
+
+    return out, whole(grad_q), whole(grad_k), whole(grad_v)
 
 
 def solution(mesh):

time: 155 us -> 150 us (0.968)
  local copies, waits for them, and re-layouts: 17.2 us -> 7.9 us
  matrix products: 9.9 us -> 16.6 us
  blocking collectives: 113 us -> 110 us
    dot_general x12 -> x24, matrix products: 9.9 us -> 16.6 us  [the longest x2 2.99 us: body(): jnp.einsum('bte,btf->bef', (qh[h] * grow[h]).astype(jnp.bfloat16), gh[h],...]
    reshape x8 -> x2, local copies, waits for them, and re-layouts: 6.42 us -> 0.03 us  [the longest x2 3.32 us: body(): grad_blocks = grad_attended.reshape(shape)]
    concatenate x0 -> x3, local copies, waits for them, and re-layouts: none -> 4.59 us  [the longest x2 3.04 us: whole(): return jnp.concatenate(parts, axis=-1).reshape(rows, width)]
    all_gather x1, blocking collectives: 25.2 us -> 22.7 us  [body(): fourth = lax.all_gather(group_back, 'seg_hi')]
    unnamed x46 -> x31, local copies, waits for them, and re-layouts: 3.6 us -> 1.24 us
    select_n x4, local copies, waits for them, and re-layouts: 2.19 us -> 0.38 us  [fade_weights(): return jnp.where(valid[:, None], jnp.exp(summed), 0.0)]
    concatenate x0 -> x3, other arithmetic: none -> 1.72 us  [whole(): return jnp.concatenate(parts, axis=-1).reshape(rows, width)]
where the time goes in v7:
time: 150 us; the launch traced here: 148 us
  blocking collectives  110 us (73%)
  matrix products  16.6 us (11%)
  other arithmetic  12.4 us (8%)
  local copies, waits for them, and re-layouts  7.9 us (5%)
    all_gather x1, blocking collectives, body(): lax.all_gather(jnp.concatenate((group_state, group_rows), axis=1), 'seg_hi')  33 us
    all_gather x1, blocking collectives, body(): fourth = lax.all_gather(group_back, 'seg_hi')  22.7 us
    psum x3, blocking collectives, body(): totals_exp = lax.psum(totals_exp, axis)  20.9 us
    all_gather x1, blocking collectives, body(): lax.all_gather(jnp.concatenate((seg_state, log_rows), axis=1), 'seg_lo')  17.3 us
    all_gather x1, blocking collectives, body(): third = lax.all_gather(seg_back, 'seg_lo')  16.1 us
    concatenate x2, local copies, waits for them, and re-layouts, whole(): return jnp.concatenate(parts, axis=-1).reshape(rows, width)  3.04 us

profile of v7, /device:TPU:6, one launch (start us, length us, event | category | flops | bytes accessed | tf_op | source)
XLA Modules:
  0.0 148.1 jit_solution(1449949283178806382)
XLA Ops:
  0.6 0.8 reshape.455
  1.4 1.2 reduce-window.6
  3.7 1.5 convolution_bitcast_fusion.2
  5.2 1.5 convolution_bitcast_fusion.3
  6.8 0.8 reduce_sum.162
  7.7 17.3 %all-gather = f32[8,136,128]{2,1,0:T(8,128)S(1)} all-gather(f32[2,136,128]{2,1,0:T(8,128)S(1)} %pad_maximum_fusion.4), channel_id=2, replica_groups=mesh['seg_hi'=4,'seg_lo'=4,'exp_y'=4,'exp_x'=4,'exp_core'=2] {'seg_lo'}, dimensions={0}, use_global_device_ids=true | all-gather | bytes 696320 | tf_op jit(solution)/shard_map/all_gather | solution.py:67
  26.0 33.0 %all-gather.1 = f32[8,136,128]{2,1,0:T(8,128)S(1)} all-gather(f32[2,136,128]{2,1,0:T(8,128)S(1)} %pad_maximum_fusion.5), channel_id=3, replica_groups=mesh['seg_hi'=4,'seg_lo'=4,'exp_y'=4,'exp_x'=4,'exp_core'=2] {'seg_hi'}, dimensions={0}, use_global_device_ids=true | all-gather | bytes 696320 | tf_op jit(solution)/shard_map/all_gather | solution.py:76
  60.0 0.8 exponential_select_fusion
  60.9 0.4 multiply_convert_fusion.3
  61.3 0.5 convolution_add_fusion.7
  62.1 0.4 multiply_convert_fusion.2
  62.8 0.5 convolution_add_fusion.6
  63.3 1.1 multiply_reduce_fusion
  64.4 1.6 %copy.148 = f32[2,512,256]{2,1,0:T(8,128)S(1)} copy(f32[2,512,256]{1,2,0:T(8,128)} %get-tuple-element.21) | data formatting | bytes 2097152 | tf_op jit(solution)/shard_map/concatenate | solution.py:90
  66.0 1.4 fusion.12
  67.4 2.5 %psum.21 = f32[2,1024]{1,0:T(2,128)S(1)} all-reduce(f32[2,1024]{1,0:T(2,128)S(1)} %pad_maximum_fusion.10), channel_id=1, replica_groups=mesh['seg_hi'=4,'seg_lo'=4,'exp_y'=4,'exp_x'=4,'exp_core'=2] {'exp_core'}, use_global_device_ids=true, to_apply=%region_13.14 | all-reduce | flops 2048 | bytes 16384 | tf_op jit(solution)/shard_map/psum | solution.py:103
  69.9 7.6 %psum.22 = f32[2,1024]{1,0:T(2,128)S(1)} all-reduce(f32[2,1024]{1,0:T(2,128)S(1)} %psum.21), channel_id=1, replica_groups=mesh['seg_hi'=4,'seg_lo'=4,'exp_y'=4,'exp_x'=4,'exp_core'=2] {'exp_x'}, use_global_device_ids=true, to_apply=%region_14.15 | all-reduce | flops 2048 | bytes 16384 | tf_op jit(solution)/shard_map/psum | solution.py:103
  77.5 10.9 %psum.23 = f32[2,1024]{1,0:T(2,128)S(1)} all-reduce(f32[2,1024]{1,0:T(2,128)S(1)} %psum.22), channel_id=1, replica_groups=mesh['seg_hi'=4,'seg_lo'=4,'exp_y'=4,'exp_x'=4,'exp_core'=2] {'exp_y'}, use_global_device_ids=true, to_apply=%region_15.16 | all-reduce | flops 2048 | bytes 16384 | tf_op jit(solution)/shard_map/psum | solution.py:103
  88.4 2.3 %subtract_convert_fusion = (bf16[1024,256]{1,0:T(8,128)(2,1)S(1)}, bf16[1024,256]{1,0:T(8,128)(2,1)}) fusion(bf16[1024,256]{1,0:T(8,128)(2,1)} %param.11, f32[2,512,256]{2,1,0:T(8,128)S(1)} %copy.148, f32[1024]{0:T(1024)S(1)} %bitcast.174, f32[1024]{0:T(1024)S(1)} %bitcast.175, f32[256]{0:T(256)S(1)} %copy-done.13), kind=kLoop, calls=%fused_computation.43 | loop fusion | flops 3145728 | bytes 2630656 | tf_op jit(solution)/shard_map/convert_element_type | solution.py:111
  90.6 1.6 %convolution_bitcast_fusion = f32[2,1,128,128]{3,2,1,0:T(8,128)S(1)} fusion(f32[2,512]{1,0:T(2,128)S(1)} %get-tuple-element.27, bf16[2,512,256]{2,1,0:T(8,128)(2,1)S(1)} %bitcast.132, bf16[2,512,256]{2,1,0:T(8,128)(2,1)} %bitcast.148), kind=kOutput, calls=%fused_computation.35 | convolution fusion | flops 33947648 | bytes 659456 | tf_op jit(solution)/shard_map/bte,btf->bef/dot_general | solution.py:116
  92.2 1.4 convolution_bitcast_fusion.1
  93.7 0.6 copy-done.12
  94.4 16.1 %all_gather.26 = f32[4,2,128,128]{3,2,1,0:T(8,128)S(1)} all-gather(f32[1,2,128,128]{3,2,1,0:T(8,128)S(1)} %fusion.52), channel_id=1, replica_groups=mesh['seg_hi'=4,'seg_lo'=4,'exp_y'=4,'exp_x'=4,'exp_core'=2] {'seg_lo'}, dimensions={0}, use_global_device_ids=true | all-gather | bytes 655360 | tf_op jit(solution)/shard_map/all_gather | solution.py:124
  110.8 22.7 %all-gather.2 = f32[8,128,128]{2,1,0:T(8,128)S(1)} all-gather(f32[2,128,128]{2,1,0:T(8,128)S(1)} %get-tuple-element.6), channel_id=4, replica_groups=mesh['seg_hi'=4,'seg_lo'=4,'exp_y'=4,'exp_x'=4,'exp_core'=2] {'seg_hi'}, dimensions={0}, use_global_device_ids=true | all-gather | bytes 655360 | tf_op jit(solution)/shard_map/all_gather | solution.py:129
  133.8 1.0 fusion.57
  134.8 1.3 fusion.1
  136.4 1.2 fusion
  138.1 1.0 copy.169
  139.3 2.2 %multiply_convert_fusion.1 = bf16[2,512,512]{2,1,0:T(8,128)(2,1)S(1)} fusion(f32[2,2,512,512]{3,2,0,1:T(8,128)} %copy-done, bf16[2,512,256]{2,1,0:T(8,128)(2,1)S(1)} %bitcast.136, bf16[2,512,256]{2,1,0:T(8,128)(2,1)S(1)} %bitcast.145), kind=kOutput, calls=%fused_computation.4 | convolution fusion | flops 135266304 | bytes 3670016 | tf_op jit(solution)/shard_map/btf,bsf->bts/dot_general | solution.py:144
  143.0 0.8 pad_maximum_fusion.2
  143.8 2.0 %copy.164 = bf16[2,512,256]{2,1,0:T(8,128)(2,1)} copy(bf16[2,512,256]{1,2,0:T(8,128)(2,1)} %pad_maximum_fusion.2) | data formatting | bytes 1048576 | tf_op jit(solution)/shard_map/concatenate | solution.py:157
  147.3 0.9 pad_maximum_fusion.1
  (95 shorter events, 8.1 us)
Async XLA Ops:
  0.6 59.0 %copy-start.6 = (bf16[1024,256]{1,0:T(8,128)(2,1)S(1)}, bf16[1024,256]{1,0:T(8,128)(2,1)}, u32[]{:S(2)}) copy-start(bf16[1024,256]{1,0:T(8,128)(2,1)} %param.6) | copy-start | bytes 1572868
  25.9 35.0 %copy-start.9 = (bf16[1024,256]{1,0:T(8,128)(2,1)S(1)}, bf16[1024,256]{1,0:T(8,128)(2,1)}, u32[]{:S(2)}) copy-start(bf16[1024,256]{1,0:T(8,128)(2,1)} %param.7) | copy-start | bytes 1572868
  59.9 1.4 copy-start.4
  60.9 1.9 %copy-start = (f32[2,2,512,512]{3,2,0,1:T(8,128)}, f32[2,2,512,512]{3,2,0,1:T(8,128)S(1)}, u32[]{:S(2)}) copy-start(f32[2,2,512,512]{3,2,0,1:T(8,128)S(1)} %exponential_select_fusion) | copy-start | bytes 12582916
  62.8 3.2 %copy-start.13 = (f32[256]{0:T(256)S(1)}, f32[256]{0:T(256)}, u32[]{:S(2)}) copy-start(f32[256]{0:T(256)} %param.10) | copy-start | bytes 3076
  90.6 1.6 %copy-start.2 = (bf16[1024,256]{1,0:T(8,128)(2,1)}, bf16[1024,256]{1,0:T(8,128)(2,1)S(1)}, u32[]{:S(2)}) copy-start(bf16[1024,256]{1,0:T(8,128)(2,1)S(1)} %get-tuple-element.18) | copy-start | bytes 1572868
  92.2 1.5 copy-start.11
  93.7 0.7 copy-start.12
  94.3 41.8 %copy-start.3 = (bf16[1024,256]{1,0:T(8,128)(2,1)S(1)}, bf16[1024,256]{1,0:T(8,128)(2,1)}, u32[]{:S(2)}) copy-start(bf16[1024,256]{1,0:T(8,128)(2,1)} %copy-done.2) | copy-start | bytes 1572868
  134.8 4.3 %copy-start.5 = (bf16[1024,256]{1,0:T(8,128)(2,1)S(1)}, bf16[1024,256]{1,0:T(8,128)(2,1)}, u32[]{:S(2)}) copy-start(bf16[1024,256]{1,0:T(8,128)(2,1)} %param.8) | copy-start | bytes 1572868
  138.0 3.5 %copy-start.7 = (bf16[1024,256]{1,0:T(8,128)(2,1)S(1)}, bf16[1024,256]{1,0:T(8,128)(2,1)}, u32[]{:S(2)}) copy-start(bf16[1024,256]{1,0:T(8,128)(2,1)} %param.6) | copy-start | bytes 1572868
  139.1 3.0 %copy-start.1 = (f32[2,2,512,512]{3,2,0,1:T(8,128)S(1)}, f32[2,2,512,512]{3,2,0,1:T(8,128)}, u32[]{:S(2)}) copy-start(f32[2,2,512,512]{3,2,0,1:T(8,128)} %copy-done) | copy-start | bytes 12582916
  141.5 1.1 copy-start.8
  142.7 3.5 %copy-start.10 = (bf16[1024,256]{1,0:T(8,128)(2,1)S(1)}, bf16[1024,256]{1,0:T(8,128)(2,1)}, u32[]{:S(2)}) copy-start(bf16[1024,256]{1,0:T(8,128)(2,1)} %param.7) | copy-start | bytes 1572868

commit v8 on v7

--- a/solution.py
+++ b/solution.py
@@ -72,15 +72,17 @@
     to_end = fade_weights(low_places[:, None] < low_places[None, :], low_places >= 0, low_logs, True)
     group_state = jnp.sum(to_end[:, :, None, None] * low_states, axis=0)
     group_log = jnp.sum(low_logs, axis=0)
+    share = head_width // lax.axis_size("seg_lo")
     group_rows = jnp.broadcast_to(group_log[:, None, None], (local_heads, 8, head_width))
-    second = lax.all_gather(jnp.concatenate((group_state, group_rows), axis=1), "seg_hi")
-    high_states = second[:, :, :head_width, :]
-    high_logs = second[:, :, head_width, 0]
+    quarter = lax.dynamic_slice_in_dim(group_state, low * share, share, axis=1)
+    second = lax.all_gather(jnp.concatenate((quarter, group_rows), axis=1), "seg_hi")
+    high_states = second[:, :, :share, :]
+    high_logs = second[:, :, share, 0]
     before_here = jnp.sum(jnp.where((low_places < low)[:, None], low_logs, 0.0), axis=0)
-    outside = fade_weights(
-        high_places[:, None] < high_places[None, :], high_places < high, high_logs, high_places[None, :] < high, before_here
-    )
-    entering = within + jnp.sum(outside[:, :, None, None] * high_states, axis=0)
+    outside = fade_weights(high_places[:, None] < high_places[None, :], high_places < high, high_logs, high_places[None, :] < high)
+    carried = jnp.sum(outside[:, :, None, None] * high_states, axis=0)
+    carried = lax.all_gather(carried, "seg_lo", axis=1, tiled=True)
+    entering = within + jnp.exp(before_here)[:, None, None] * carried
     held_list = []
     running = entering
     for block in range(count):
@@ -126,12 +128,12 @@
     within_back = jnp.sum(inside_back[:, :, None, None] * third, axis=0)
     to_start = fade_weights(low_places[:, None] > low_places[None, :], low_places >= 0, low_logs, True)
     group_back = jnp.sum(to_start[:, :, None, None] * third, axis=0)
-    fourth = lax.all_gather(group_back, "seg_hi")
+    fourth = lax.all_gather(lax.dynamic_slice_in_dim(group_back, low * share, share, axis=1), "seg_hi")
     after_here = jnp.sum(jnp.where((low_places > low)[:, None], low_logs, 0.0), axis=0)
-    outside_back = fade_weights(
-        high_places[:, None] > high_places[None, :], high_places > high, high_logs, high_places[None, :] > high, after_here
-    )
-    leaving = within_back + jnp.sum(outside_back[:, :, None, None] * fourth, axis=0)
+    outside_back = fade_weights(high_places[:, None] > high_places[None, :], high_places > high, high_logs, high_places[None, :] > high)
+    carried_back = jnp.sum(outside_back[:, :, None, None] * fourth, axis=0)
+    carried_back = lax.all_gather(carried_back, "seg_lo", axis=1, tiled=True)
+    leaving = within_back + jnp.exp(after_here)[:, None, None] * carried_back
     exit_list = [None] * count
     running = leaving
     for block in range(count - 1, -1, -1):

time: 150 us -> 175 us (1.17)
  blocking collectives: 110 us -> 124 us
  other arithmetic: 12.4 us -> 17.1 us
  local copies, waits for them, and re-layouts: 7.9 us -> 12.6 us
    all_gather x2 -> x4, blocking collectives: 55.7 us -> 70.7 us  [the longest x1 25.6 us: body(): lax.all_gather(jnp.concatenate((quarter, group_rows), axis=1), 'seg_hi')]
    exp x4, local copies, waits for them, and re-layouts: 0.2 us -> 2.68 us  [fade_weights(): return jnp.where(valid[:, None], jnp.exp(summed), 0.0)]
where the time goes in v8:
time: 175 us; the launch traced here: 172 us
  blocking collectives  124 us (71%)
  matrix products  17.5 us (10%)
  other arithmetic  17.1 us (10%)
  local copies, waits for them, and re-layouts  12.6 us (7%)
    all_gather x1, blocking collectives, body(): lax.all_gather(jnp.concatenate((quarter, group_rows), axis=1), 'seg_hi')  25.6 us
    psum x3, blocking collectives, body(): totals_exp = lax.psum(totals_exp, axis)  20.9 us
    all_gather x1, blocking collectives, body(): lax.all_gather(lax.dynamic_slice_in_dim(group_back, low * share, share, a...  18.4 us
    all_gather x1, blocking collectives, body(): lax.all_gather(jnp.concatenate((seg_state, log_rows), axis=1), 'seg_lo')  17.4 us
    all_gather x1, blocking collectives, body(): third = lax.all_gather(seg_back, 'seg_lo')  15.1 us
    all_gather x1, blocking collectives, body(): carried = lax.all_gather(carried, 'seg_lo', axis=1, tiled=True)  13.3 us
    all_gather x1, blocking collectives, body(): carried_back = lax.all_gather(carried_back, 'seg_lo', axis=1, tiled=True)  13.3 us

profile of v8, /device:TPU:6, one launch (start us, length us, event | category | flops | bytes accessed | tf_op | source)
XLA Modules:
  0.0 172.4 jit_solution(16697244477428135988)
XLA Ops:
  1.4 1.2 reduce-window.6
  3.7 1.5 convolution_bitcast_fusion.2
  5.2 1.5 convolution_bitcast_fusion.3
  8.2 17.4 %all-gather = f32[8,136,128]{2,1,0:T(8,128)S(1)} all-gather(f32[2,136,128]{2,1,0:T(8,128)S(1)} %pad_maximum_fusion.4), channel_id=2, replica_groups=mesh['seg_hi'=4,'seg_lo'=4,'exp_y'=4,'exp_x'=4,'exp_core'=2] {'seg_lo'}, dimensions={0}, use_global_device_ids=true | all-gather | bytes 696320 | tf_op jit(solution)/shard_map/all_gather | solution.py:67
  26.6 1.2 select_reduce_fusion.6
  28.2 25.6 %all-gather.1 = f32[8,40,128]{2,1,0:T(8,128)S(1)} all-gather(f32[2,40,128]{2,1,0:T(8,128)S(1)} %pad_maximum_fusion.9), channel_id=3, replica_groups=mesh['seg_hi'=4,'seg_lo'=4,'exp_y'=4,'exp_x'=4,'exp_core'=2] {'seg_hi'}, dimensions={0}, use_global_device_ids=true | all-gather | bytes 204800 | tf_op jit(solution)/shard_map/all_gather | solution.py:78
  55.4 13.3 %all_gather.32 = f32[2,128,128]{2,1,0:T(8,128)S(1)} all-gather(f32[2,32,128]{2,1,0:T(8,128)S(1)} %fusion.53), channel_id=1, replica_groups=mesh['seg_hi'=4,'seg_lo'=4,'exp_y'=4,'exp_x'=4,'exp_core'=2] {'seg_lo'}, dimensions={1}, use_global_device_ids=true | all-gather | bytes 163840 | tf_op jit(solution)/shard_map/all_gather | solution.py:84
  72.5 1.1 multiply_reduce_fusion
  73.6 1.6 copy.148
  75.2 1.4 fusion.12
  76.6 2.5 %psum.21 = f32[2,1024]{1,0:T(2,128)S(1)} all-reduce(f32[2,1024]{1,0:T(2,128)S(1)} %pad_maximum_fusion.10), channel_id=1, replica_groups=mesh['seg_hi'=4,'seg_lo'=4,'exp_y'=4,'exp_x'=4,'exp_core'=2] {'exp_core'}, use_global_device_ids=true, to_apply=%region_13.14 | all-reduce | flops 2048 | bytes 16384 | tf_op jit(solution)/shard_map/psum | solution.py:105
  79.1 7.6 %psum.22 = f32[2,1024]{1,0:T(2,128)S(1)} all-reduce(f32[2,1024]{1,0:T(2,128)S(1)} %psum.21), channel_id=1, replica_groups=mesh['seg_hi'=4,'seg_lo'=4,'exp_y'=4,'exp_x'=4,'exp_core'=2] {'exp_x'}, use_global_device_ids=true, to_apply=%region_14.15 | all-reduce | flops 2048 | bytes 16384 | tf_op jit(solution)/shard_map/psum | solution.py:105
  86.7 10.8 %psum.23 = f32[2,1024]{1,0:T(2,128)S(1)} all-reduce(f32[2,1024]{1,0:T(2,128)S(1)} %psum.22), channel_id=1, replica_groups=mesh['seg_hi'=4,'seg_lo'=4,'exp_y'=4,'exp_x'=4,'exp_core'=2] {'exp_y'}, use_global_device_ids=true, to_apply=%region_15.16 | all-reduce | flops 2048 | bytes 16384 | tf_op jit(solution)/shard_map/psum | solution.py:105
  97.5 2.3 %subtract_convert_fusion = (bf16[1024,256]{1,0:T(8,128)(2,1)S(1)}, bf16[1024,256]{1,0:T(8,128)(2,1)}) fusion(bf16[1024,256]{1,0:T(8,128)(2,1)} %param.11, f32[2,512,256]{2,1,0:T(8,128)S(1)} %copy.148, f32[1024]{0:T(1024)S(1)} %bitcast.175, f32[1024]{0:T(1024)S(1)} %bitcast.176, f32[256]{0:T(256)S(1)} %copy-done.14), kind=kLoop, calls=%fused_computation.43 | loop fusion | flops 3145728 | bytes 2630656 | tf_op jit(solution)/shard_map/convert_element_type | solution.py:113
  99.8 1.6 convolution_bitcast_fusion
  101.3 1.4 convolution_bitcast_fusion.1
  103.5 15.1 %all_gather.33 = f32[4,2,128,128]{3,2,1,0:T(8,128)S(1)} all-gather(f32[1,2,128,128]{3,2,1,0:T(8,128)S(1)} %fusion.52), channel_id=1, replica_groups=mesh['seg_hi'=4,'seg_lo'=4,'exp_y'=4,'exp_x'=4,'exp_core'=2] {'seg_lo'}, dimensions={0}, use_global_device_ids=true | all-gather | bytes 655360 | tf_op jit(solution)/shard_map/all_gather | solution.py:126
  118.6 1.3 copy.159
  119.9 1.2 exp.103
  121.2 1.3 copy.161
  122.5 1.5 multiply_reduce_fusion.1
  124.0 18.4 %all-gather.2 = f32[8,32,128]{2,1,0:T(8,128)S(1)} all-gather(f32[2,32,128]{2,1,0:T(8,128)S(1)} %constant_dynamic-slice_fusion), channel_id=4, replica_groups=mesh['seg_hi'=4,'seg_lo'=4,'exp_y'=4,'exp_x'=4,'exp_core'=2] {'seg_hi'}, dimensions={0}, use_global_device_ids=true | all-gather | bytes 163840 | tf_op jit(solution)/shard_map/all_gather | solution.py:131
  143.2 13.3 %all_gather.36 = f32[2,128,128]{2,1,0:T(8,128)S(1)} all-gather(f32[2,32,128]{2,1,0:T(8,128)S(1)} %multiply_reduce_fusion.5), channel_id=1, replica_groups=mesh['seg_hi'=4,'seg_lo'=4,'exp_y'=4,'exp_x'=4,'exp_core'=2] {'seg_lo'}, dimensions={1}, use_global_device_ids=true | all-gather | bytes 163840 | tf_op jit(solution)/shard_map/all_gather | solution.py:135
  157.2 1.0 fusion.58
  158.2 1.3 fusion.1
  159.5 1.3 fusion.10
  160.8 1.2 fusion
  162.4 1.0 copy.169
  163.6 2.2 %multiply_convert_fusion.1 = bf16[2,512,512]{2,1,0:T(8,128)(2,1)S(1)} fusion(f32[2,2,512,512]{3,2,0,1:T(8,128)} %copy-done, bf16[2,512,256]{2,1,0:T(8,128)(2,1)S(1)} %bitcast.137, bf16[2,512,256]{2,1,0:T(8,128)(2,1)S(1)} %bitcast.146), kind=kOutput, calls=%fused_computation.4 | convolution fusion | flops 135266304 | bytes 3670016 | tf_op jit(solution)/shard_map/btf,bsf->bts/dot_general | solution.py:146
  167.3 0.8 pad_maximum_fusion.2
  168.2 2.0 %copy.164 = bf16[2,512,256]{2,1,0:T(8,128)(2,1)} copy(bf16[2,512,256]{1,2,0:T(8,128)(2,1)} %pad_maximum_fusion.2) | data formatting | bytes 1048576 | tf_op jit(solution)/shard_map/concatenate | solution.py:159
  171.6 0.9 pad_maximum_fusion.1
  (103 shorter events, 15.5 us)
Async XLA Ops:
  0.6 68.2 %copy-start.6 = (bf16[1024,256]{1,0:T(8,128)(2,1)S(1)}, bf16[1024,256]{1,0:T(8,128)(2,1)}, u32[]{:S(2)}) copy-start(bf16[1024,256]{1,0:T(8,128)(2,1)} %param.6) | copy-start | bytes 1572868
  6.7 0.6 copy-start.12
  6.7 63.3 %copy-start.13 = (f32[2]{0:T(128)}, f32[2]{0:T(128)S(1)}, u32[]{:S(2)}) copy-start(f32[2]{0:T(128)S(1)} %get-tuple-element.35) | copy-start | bytes 28
  8.2 61.8 %copy-start.9 = (bf16[1024,256]{1,0:T(8,128)(2,1)S(1)}, bf16[1024,256]{1,0:T(8,128)(2,1)}, u32[]{:S(2)}) copy-start(bf16[1024,256]{1,0:T(8,128)(2,1)} %param.7) | copy-start | bytes 1572868
  54.0 0.5 copy-start.15
  69.1 1.4 copy-start.4
  70.1 1.9 %copy-start = (f32[2,2,512,512]{3,2,0,1:T(8,128)}, f32[2,2,512,512]{3,2,0,1:T(8,128)S(1)}, u32[]{:S(2)}) copy-start(f32[2,2,512,512]{3,2,0,1:T(8,128)S(1)} %exponential_select_fusion) | copy-start | bytes 12582916
  72.0 3.2 %copy-start.14 = (f32[256]{0:T(256)S(1)}, f32[256]{0:T(256)}, u32[]{:S(2)}) copy-start(f32[256]{0:T(256)} %param.10) | copy-start | bytes 3076
  99.8 1.6 copy-start.2
  102.7 53.8 %copy-start.11 = (f32[2,1,128,128]{3,2,1,0:T(8,128)}, f32[2,1,128,128]{3,2,1,0:T(8,128)S(1)}, u32[]{:S(2)}) copy-start(f32[2,1,128,128]{3,2,1,0:T(8,128)S(1)} %convolution_bitcast_fusion.1) | copy-start | bytes 393220
  102.8 59.2 %copy-start.3 = (bf16[1024,256]{1,0:T(8,128)(2,1)S(1)}, bf16[1024,256]{1,0:T(8,128)(2,1)}, u32[]{:S(2)}) copy-start(bf16[1024,256]{1,0:T(8,128)(2,1)} %copy-done.2) | copy-start | bytes 1572868
  158.2 5.2 %copy-start.5 = (bf16[1024,256]{1,0:T(8,128)(2,1)S(1)}, bf16[1024,256]{1,0:T(8,128)(2,1)}, u32[]{:S(2)}) copy-start(bf16[1024,256]{1,0:T(8,128)(2,1)} %param.8) | copy-start | bytes 1572868
  162.4 3.5 %copy-start.7 = (bf16[1024,256]{1,0:T(8,128)(2,1)S(1)}, bf16[1024,256]{1,0:T(8,128)(2,1)}, u32[]{:S(2)}) copy-start(bf16[1024,256]{1,0:T(8,128)(2,1)} %param.6) | copy-start | bytes 1572868
  163.4 3.0 %copy-start.1 = (f32[2,2,512,512]{3,2,0,1:T(8,128)S(1)}, f32[2,2,512,512]{3,2,0,1:T(8,128)}, u32[]{:S(2)}) copy-start(f32[2,2,512,512]{3,2,0,1:T(8,128)} %copy-done) | copy-start | bytes 12582916
  165.8 1.1 copy-start.8
  167.0 3.5 %copy-start.10 = (bf16[1024,256]{1,0:T(8,128)(2,1)S(1)}, bf16[1024,256]{1,0:T(8,128)(2,1)}, u32[]{:S(2)}) copy-start(bf16[1024,256]{1,0:T(8,128)(2,1)} %param.7) | copy-start | bytes 1572868

commit v9 on v7

--- a/solution.py
+++ b/solution.py
@@ -98,9 +98,10 @@
     partial = jnp.stack(
         (jnp.sum(attended * attended, axis=-1), jnp.sum(gain * upstream * attended, axis=-1))
     )
-    totals_exp = partial
-    for axis in EXP_PARTS[::-1]:
-        totals_exp = lax.psum(totals_exp, axis)
+    seg_index = lax.axis_index(SEG_PARTS)
+    slots = jnp.zeros((lax.axis_size(SEG_PARTS),) + partial.shape, partial.dtype)
+    slots = lax.dynamic_update_index_in_dim(slots, partial, seg_index, axis=0)
+    totals_exp = lax.dynamic_index_in_dim(lax.psum(slots, SEG_PARTS + EXP_PARTS), seg_index, axis=0, keepdims=False)
     squares, cross = totals_exp[0], totals_exp[1]
     features = width * lax.axis_size(EXP_PARTS)
     inv_rms = lax.rsqrt(squares / features + EPS)[:, None]

time: 150 us -> 607 us (4.05)
  waiting for transfers between devices: 0 us -> 442 us
  blocking collectives: 110 us -> 92.2 us
  between operations: 1.14 us -> 14.6 us
  local copies, waits for them, and re-layouts: 7.9 us -> 16.4 us
  other arithmetic: 12.4 us -> 20.8 us
    psum x0 -> x1, waiting for transfers between devices: none -> 442 us  [body(): lax.psum(slots, SEG_PARTS + EXP_PARTS)]
    psum x3 -> x0, blocking collectives: 20.9 us -> none  [body(): totals_exp = lax.psum(totals_exp, axis)]
  transfers between devices with their start and end apart: 0 -> 1, of which waited for: 0 -> 1; matrix products, arithmetic and copies ran while one was open for 0% -> 0% of each run, Pallas kernels for 0% -> 0%
where the time goes in v9:
time: 607 us; the launch traced here: 606 us
  waiting for transfers between devices  442 us (73%)
  blocking collectives  92.2 us (15%)
  other arithmetic  20.8 us (3%)
  matrix products  20.3 us (3%)
  local copies, waits for them, and re-layouts  16.4 us (3%)
  between operations  14.6 us (2%)
    psum x1, waiting for transfers between devices, body(): lax.psum(slots, SEG_PARTS + EXP_PARTS)  442 us
    all_gather x1, blocking collectives, body(): lax.all_gather(jnp.concatenate((group_state, group_rows), axis=1), 'seg_hi')  32.7 us
    all_gather x1, blocking collectives, body(): fourth = lax.all_gather(group_back, 'seg_hi')  25.6 us
    all_gather x1, blocking collectives, body(): lax.all_gather(jnp.concatenate((seg_state, log_rows), axis=1), 'seg_lo')  17.7 us
    all_gather x1, blocking collectives, body(): third = lax.all_gather(seg_back, 'seg_lo')  16.2 us
  transfers between devices with their start and end apart: 1, of which 1 were waited for; matrix products, arithmetic and copies ran while one was open for 0% of the time, Pallas kernels for 0%

profile of v9, /device:TPU:6, one launch (start us, length us, event | category | flops | bytes accessed | tf_op | source)
XLA Modules:
  0.0 606.2 jit_solution(10908012915882906268)
XLA Ops:
  8.1 1.2 reduce-window.6
  12.2 1.4 copy-done
  14.5 1.4 convolution_bitcast_fusion.2
  15.9 1.4 convolution_bitcast_fusion.3
  18.6 17.7 %all-gather = f32[8,136,128]{2,1,0:T(8,128)} all-gather(f32[2,136,128]{2,1,0:T(8,128)S(1)} %pad_maximum_fusion.4), channel_id=2, replica_groups=mesh['seg_hi'=4,'seg_lo'=4,'exp_y'=4,'exp_x'=4,'exp_core'=2] {'seg_lo'}, dimensions={0}, use_global_device_ids=true | all-gather | bytes 696320 | tf_op jit(solution)/shard_map/all_gather | solution.py:67
  36.3 1.4 slice_reduce_fusion.3
  38.5 1.3 select_reduce_fusion.6
  41.2 1.2 multiply_reduce_fusion.4
  43.2 32.7 %all-gather.1 = f32[8,136,128]{2,1,0:T(8,128)S(1)} all-gather(f32[2,136,128]{2,1,0:T(8,128)S(1)} %pad_maximum_fusion.5), channel_id=3, replica_groups=mesh['seg_hi'=4,'seg_lo'=4,'exp_y'=4,'exp_x'=4,'exp_core'=2] {'seg_hi'}, dimensions={0}, use_global_device_ids=true | all-gather | bytes 696320 | tf_op jit(solution)/shard_map/all_gather | solution.py:76
  77.3 1.3 copy.143
  79.1 1.3 select_reduce_fusion.1
  80.5 1.3 exponential_select_fusion.3
  81.8 1.3 copy.144
  83.1 1.2 fusion.13
  86.8 1.1 multiply_reduce_fusion
  88.0 1.6 copy.148
  89.6 1.4 fusion.12
  92.1 441.9 %all-reduce.2.cloned.1.call-done = f32[16,2,1024]{2,1,0:T(2,128)} async-done(((f32[16,2,1024]{2,1,0:T(2,128)}), f32[16,2,1024]{2,1,0:T(2,128)}) %all-reduce.2.cloned.1.call-update) | async-done | bytes 131088 | tf_op jit(solution)/shard_map/psum | solution.py:104
  534.8 2.3 subtract_convert_fusion
  537.1 1.5 convolution_bitcast_fusion
  538.7 1.4 convolution_bitcast_fusion.1
  540.2 16.2 %all_gather.26 = f32[4,2,128,128]{3,2,1,0:T(8,128)S(1)} all-gather(f32[1,2,128,128]{3,2,1,0:T(8,128)S(1)} %fusion.52), channel_id=1, replica_groups=mesh['seg_hi'=4,'seg_lo'=4,'exp_y'=4,'exp_x'=4,'exp_core'=2] {'seg_lo'}, dimensions={0}, use_global_device_ids=true | all-gather | bytes 655360 | tf_op jit(solution)/shard_map/all_gather | solution.py:125
  556.5 25.6 %all-gather.2 = f32[8,128,128]{2,1,0:T(8,128)S(1)} all-gather(f32[2,128,128]{2,1,0:T(8,128)S(1)} %get-tuple-element.6), channel_id=4, replica_groups=mesh['seg_hi'=4,'seg_lo'=4,'exp_y'=4,'exp_x'=4,'exp_core'=2] {'seg_hi'}, dimensions={0}, use_global_device_ids=true | all-gather | bytes 655360 | tf_op jit(solution)/shard_map/all_gather | solution.py:130
  582.9 1.0 fusion.3
  584.3 1.0 fusion.2
  585.4 1.4 multiply_convert_fusion
  586.8 1.1 convolution_multiply_fusion.5
  587.9 1.0 convolution_multiply_fusion.4
  590.7 1.5 fusion.8
  592.2 1.5 fusion.9
  594.5 2.0 copy.164
  596.5 1.5 fusion.6
  (116 shorter events, 20.3 us)
Async XLA Ops:
  7.2 4.6 copy-start.6
  7.2 4.6 copy-start.5
  7.2 526.8 %all-reduce.2.cloned.1.call-start = ((), (), s32[]{:S(2)}) async-start(), calls=%async_computation | async-start | bytes 262144 | tf_op jit(solution)/shard_map/psum | solution.py:104
  10.8 2.8 copy-start.7
  11.7 1.9 copy-start
  11.7 2.8 copy-start.3
  17.3 67.0 %copy-start.13 = (f32[2,1,128,128]{3,2,0,1:T(8,128)}, f32[2,1,128,128]{3,2,0,1:T(8,128)S(1)}, u32[]{:S(2)}) copy-start(f32[2,1,128,128]{3,2,0,1:T(8,128)S(1)} %convolution_bitcast_fusion.3) | copy-start | bytes 393220
  17.9 0.5 copy-start.14
  75.9 0.8 copy-start.10
  78.6 0.5 copy-start.22
  85.8 3.7 copy-start.20
  86.3 5.4 copy-start.19
  86.3 5.4 copy-start.21
  86.3 5.4 copy-start.23
  86.3 5.5 copy-start.17
  86.3 5.5 copy-start.18
  88.0 452.1 %copy-start.16 = (f32[2]{0:T(128)S(1)}, f32[2]{0:T(128)}, u32[]{:S(2)}) copy-start(f32[2]{0:T(128)} %get-tuple-element.31) | copy-start | bytes 28
  90.9 491.2 %copy-start.15 = (f32[2]{0:T(128)S(1)}, f32[2]{0:T(128)}, u32[]{:S(2)}) copy-start(f32[2]{0:T(128)} %copy-done.14) | copy-start | bytes 28
  91.0 0.7 copy-start.12
  534.8 47.5 %copy-start.8 = (bf16[1024,256]{1,0:T(8,128)(2,1)S(1)}, bf16[1024,256]{1,0:T(8,128)(2,1)}, u32[]{:S(2)}) copy-start(bf16[1024,256]{1,0:T(8,128)(2,1)} %param.7) | copy-start | bytes 1572868
  537.1 45.7 %copy-start.4 = (bf16[1024,256]{1,0:T(8,128)(2,1)S(1)}, bf16[1024,256]{1,0:T(8,128)(2,1)}, u32[]{:S(2)}) copy-start(bf16[1024,256]{1,0:T(8,128)(2,1)} %param.8) | copy-start | bytes 1572868
  537.1 46.8 %copy-start.1 = (f32[2,2,512,512]{3,2,0,1:T(8,128)S(1)}, f32[2,2,512,512]{3,2,0,1:T(8,128)}, u32[]{:S(2)}) copy-start(f32[2,2,512,512]{3,2,0,1:T(8,128)} %copy-done) | copy-start | bytes 12582916
  589.2 3.0 copy-start.2
  589.6 6.9 %copy-start.9 = (bf16[1024,256]{1,0:T(8,128)(2,1)S(1)}, bf16[1024,256]{1,0:T(8,128)(2,1)}, u32[]{:S(2)}) copy-start(bf16[1024,256]{1,0:T(8,128)(2,1)} %param.7) | copy-start | bytes 1572868
  590.7 7.4 %copy-start.11 = (f32[2,512,128]{2,1,0:T(8,128)S(1)}, f32[2,512,128]{2,1,0:T(8,128)}, u32[]{:S(2)}) copy-start(f32[2,512,128]{2,1,0:T(8,128)} %convolution_multiply_fusion.4) | copy-start | bytes 1572868
Sparse Core Ops, SparseCore 0:
  91.8 442.1 all-reduce.1

commit v10 on v7

--- a/solution.py
+++ b/solution.py
@@ -87,30 +87,31 @@
         held_list.append(running.astype(jnp.bfloat16))
         running = block_fade[block][:, None, None] * running + block_state[block]
     held = jnp.stack(held_list)
-    attended = jnp.concatenate(
-        [
-            inner[h] + grow[h] * jnp.einsum("bte,bef->btf", qh[h], held[:, h], preferred_element_type=jnp.float32)
-            for h in range(local_heads)
-        ],
-        axis=-1,
-    ).reshape(rows, width)
-    upstream = d_out.astype(jnp.float32)
-    partial = jnp.stack(
-        (jnp.sum(attended * attended, axis=-1), jnp.sum(gain * upstream * attended, axis=-1))
-    )
+    gains = [gain[c] for c in cols]
+    ups = [uv[:, :, c].astype(jnp.float32) for c in cols]
+    attended = [
+        inner[h] + grow[h] * jnp.einsum("bte,bef->btf", qh[h], held[:, h], preferred_element_type=jnp.float32)
+        for h in range(local_heads)
+    ]
+    squares_local = sum(jnp.sum(attended[h] * attended[h], axis=-1) for h in range(local_heads))
+    cross_local = sum(jnp.sum(gains[h] * ups[h] * attended[h], axis=-1) for h in range(local_heads))
+    partial = jnp.stack((squares_local.reshape(rows), cross_local.reshape(rows)))
     totals_exp = partial
     for axis in EXP_PARTS[::-1]:
         totals_exp = lax.psum(totals_exp, axis)
-    squares, cross = totals_exp[0], totals_exp[1]
+    squares, cross = totals_exp[0].reshape(count, BLK), totals_exp[1].reshape(count, BLK)
     features = width * lax.axis_size(EXP_PARTS)
-    inv_rms = lax.rsqrt(squares / features + EPS)[:, None]
-    out = (attended * inv_rms * gain).astype(jnp.bfloat16)
-    grad_attended = (
-        gain * upstream * inv_rms
-        - attended * inv_rms * inv_rms * inv_rms * cross[:, None] / features
-    ).astype(jnp.bfloat16)
-    gv = grad_attended.reshape(view)
-    gh = [gv[:, :, c] for c in cols]
+    inv_rms = lax.rsqrt(squares / features + EPS)[..., None]
+    out = jnp.concatenate(
+        [(attended[h] * inv_rms * gains[h]).astype(jnp.bfloat16) for h in range(local_heads)], axis=-1
+    ).reshape(rows, width)
+    gh = [
+        (
+            gains[h] * ups[h] * inv_rms
+            - attended[h] * inv_rms * inv_rms * inv_rms * cross[..., None] / features
+        ).astype(jnp.bfloat16)
+        for h in range(local_heads)
+    ]
     back_terms = jnp.stack(
         [
             jnp.einsum("bte,btf->bef", (qh[h] * grow[h]).astype(jnp.bfloat16), gh[h], preferred_element_type=jnp.float32)

time: 150 us -> 160 us (1.067)
  matrix products: 16.6 us -> 21.8 us
  blocking collectives: 110 us -> 112 us
  local copies, waits for them, and re-layouts: 7.9 us -> 9.59 us
    dot_general x2, matrix products: 0.97 us -> 3.75 us  [body(): jnp.einsum('bts,bsf->btf', scores[h], vh[h], preferred_element_type=jnp.f...]
    reduce_sum x2 -> x0, other arithmetic: 2.51 us -> none  [the longest x1 1.37 us: body(): jnp.sum(gain * upstream * attended, axis=-1)]
    unnamed x31 -> x48, local copies, waits for them, and re-layouts: 1.24 us -> 3.7 us
    dot_general x2, matrix products: 2.99 us -> 0.89 us  [body(): jnp.einsum('bte,btf->bef', (qh[h] * grow[h]).astype(jnp.bfloat16), gh[h],...]
    reduce_sum x1, other arithmetic: 0.14 us -> 1.86 us  [body(): group_back = jnp.sum(to_start[:, :, None, None] * third, axis=0)]
    dot_general x2, matrix products: 0.9 us -> 2.57 us  [body(): jnp.einsum('bte,bse->bts', qh[h], kh[h], preferred_element_type=jnp.float32)]
where the time goes in v10:
time: 160 us; the launch traced here: 158 us
  blocking collectives  112 us (70%)
  matrix products  21.8 us (14%)
  other arithmetic  13.2 us (8%)
  local copies, waits for them, and re-layouts  9.59 us (6%)
    all_gather x1, blocking collectives, body(): lax.all_gather(jnp.concatenate((group_state, group_rows), axis=1), 'seg_hi')  33 us
    all_gather x1, blocking collectives, body(): fourth = lax.all_gather(group_back, 'seg_hi')  24.1 us
    psum x3, blocking collectives, body(): totals_exp = lax.psum(totals_exp, axis)  20.9 us
    all_gather x1, blocking collectives, body(): lax.all_gather(jnp.concatenate((seg_state, log_rows), axis=1), 'seg_lo')  17.3 us
    all_gather x1, blocking collectives, body(): third = lax.all_gather(seg_back, 'seg_lo')  16.8 us
    dot_general x2, matrix products, body(): jnp.einsum('bts,bsf->btf', scores[h], vh[h], preferred_element_type=jnp.f...  3.75 us
    unnamed x48, local copies, waits for them, and re-layouts  3.7 us

profile of v10, /device:TPU:6, one launch (start us, length us, event | category | flops | bytes accessed | tf_op | source)
XLA Modules:
  0.0 158.0 jit_solution(6024161005709003291)
XLA Ops:
  1.4 1.2 reduce-window.6
  3.7 1.5 convolution_bitcast_fusion.2
  5.2 1.5 convolution_bitcast_fusion.3
  6.8 0.8 reduce_sum.180
  7.7 17.3 %all-gather = f32[8,136,128]{2,1,0:T(8,128)S(1)} all-gather(f32[2,136,128]{2,1,0:T(8,128)S(1)} %pad_maximum_fusion.4), channel_id=2, replica_groups=mesh['seg_hi'=4,'seg_lo'=4,'exp_y'=4,'exp_x'=4,'exp_core'=2] {'seg_lo'}, dimensions={0}, use_global_device_ids=true | all-gather | bytes 696320 | tf_op jit(solution)/shard_map/all_gather | solution.py:67
  26.0 33.0 %all-gather.1 = f32[8,136,128]{2,1,0:T(8,128)S(1)} all-gather(f32[2,136,128]{2,1,0:T(8,128)S(1)} %pad_maximum_fusion.5), channel_id=3, replica_groups=mesh['seg_hi'=4,'seg_lo'=4,'exp_y'=4,'exp_x'=4,'exp_core'=2] {'seg_hi'}, dimensions={0}, use_global_device_ids=true | all-gather | bytes 696320 | tf_op jit(solution)/shard_map/all_gather | solution.py:76
  60.1 0.8 exponential_select_fusion
  60.9 1.9 %copy-done = f32[2,2,512,512]{3,2,0,1:T(8,128)} copy-done((f32[2,2,512,512]{3,2,0,1:T(8,128)}, f32[2,2,512,512]{3,2,0,1:T(8,128)S(1)}, u32[]{:S(2)}) %copy-start) | copy-done | bytes 4194328
  64.3 1.3 multiply_reduce_fusion.5
  65.6 1.1 fusion.5
  66.6 2.1 %multiply_convert_fusion.3 = bf16[2,512,512]{2,1,0:T(8,128)(2,1)S(1)} fusion(f32[2,2,512,512]{3,2,0,1:T(8,128)} %copy-done, bf16[2,512,256]{2,1,0:T(8,128)(2,1)} %bitcast.152, bf16[2,512,256]{2,1,0:T(8,128)(2,1)S(1)} %bitcast.145), kind=kOutput, calls=%fused_computation.6 | convolution fusion | flops 135266304 | bytes 3670016 | tf_op jit(solution)/shard_map/bte,bse->bts/dot_general | solution.py:46
  68.8 1.1 copy.223
  69.9 2.4 %multiply_reduce_fusion.6 = (f32[2,512]{1,0:T(2,128)S(1)}, f32[2,512]{1,0:T(2,128)S(1)}, f32[2,512,128]{1,2,0:T(8,128)}) fusion(bf16[2,512,128]{1,2,0:T(8,128)(2,1)S(1)} %copy.223, f32[128]{0:T(128)S(1)} %get-tuple-element.39, f32[2,512,128]{1,2,0:T(8,128)} %fusion.5, bf16[2,512,512]{2,1,0:T(8,128)(2,1)S(1)} %multiply_convert_fusion.3, ...), kind=kOutput, calls=%fused_computation.60 | convolution fusion | flops 135133184 | bytes 2630144 | tf_op jit(solution)/shard_map/bts,bsf->btf/dot_general | solution.py:49
  72.4 2.5 %psum.21 = f32[2,1024]{1,0:T(2,128)S(1)} all-reduce(f32[2,1024]{1,0:T(2,128)S(1)} %pad_maximum_fusion.10), channel_id=1, replica_groups=mesh['seg_hi'=4,'seg_lo'=4,'exp_y'=4,'exp_x'=4,'exp_core'=2] {'exp_core'}, use_global_device_ids=true, to_apply=%region_15.16 | all-reduce | flops 2048 | bytes 16384 | tf_op jit(solution)/shard_map/psum | solution.py:101
  74.9 7.6 %psum.22 = f32[2,1024]{1,0:T(2,128)S(1)} all-reduce(f32[2,1024]{1,0:T(2,128)S(1)} %psum.21), channel_id=1, replica_groups=mesh['seg_hi'=4,'seg_lo'=4,'exp_y'=4,'exp_x'=4,'exp_core'=2] {'exp_x'}, use_global_device_ids=true, to_apply=%region_16.17 | all-reduce | flops 2048 | bytes 16384 | tf_op jit(solution)/shard_map/psum | solution.py:101
  82.5 10.9 %psum.23 = f32[2,1024]{1,0:T(2,128)S(1)} all-reduce(f32[2,1024]{1,0:T(2,128)S(1)} %psum.22), channel_id=1, replica_groups=mesh['seg_hi'=4,'seg_lo'=4,'exp_y'=4,'exp_x'=4,'exp_core'=2] {'exp_y'}, use_global_device_ids=true, to_apply=%region_17.18 | all-reduce | flops 2048 | bytes 16384 | tf_op jit(solution)/shard_map/psum | solution.py:101
  93.4 2.5 %subtract_convert_fusion.1 = (bf16[2,512,128]{1,2,0:T(8,128)(2,1)S(1)}, bf16[2,512,128]{1,2,0:T(8,128)(2,1)}, bf16[2,512,128]{1,2,0:T(8,128)(2,1)}, bf16[2,512,128]{1,2,0:T(8,128)(2,1)S(1)}) fusion(bf16[2,512,128]{1,2,0:T(8,128)(2,1)} %copy-done.10, f32[2,512,128]{1,2,0:T(8,128)} %get-tuple-element.44, f32[2,512]{1,0:T(2,128)S(1)} %mul.377, ...), kind=kLoop, calls=%fused_computation.52 | loop fusion | flops 3145728 | bytes 2630656 | tf_op jit(solution)/shard_map/convert_element_type | solution.py:112
  97.2 16.8 %all_gather.26 = f32[4,2,128,128]{3,2,1,0:T(8,128)} all-gather(f32[1,2,128,128]{3,2,1,0:T(8,128)S(1)} %fusion.43), channel_id=1, replica_groups=mesh['seg_hi'=4,'seg_lo'=4,'exp_y'=4,'exp_x'=4,'exp_core'=2] {'seg_lo'}, dimensions={0}, use_global_device_ids=true | all-gather | bytes 655360 | tf_op jit(solution)/shard_map/all_gather | solution.py:125
  114.2 1.9 %multiply_reduce_fusion.1 = (f32[2,128,128]{2,1,0:T(8,128)S(1)}, f32[2,128,128]{2,1,0:T(8,128)}) fusion(f32[4,2,128,128]{3,2,1,0:T(8,128)} %all_gather.26, f32[4,2]{1,0:T(4,128)S(1)} %copy.185, f32[4,2]{1,0:T(4,128)S(1)} %copy.183), kind=kLoop, calls=%fused_computation.47 | loop fusion | flops 458752 | bytes 786496 | tf_op jit(solution)/shard_map/reduce_sum | solution.py:129
  116.1 24.1 %all-gather.2 = f32[8,128,128]{2,1,0:T(8,128)} all-gather(f32[2,128,128]{2,1,0:T(8,128)S(1)} %get-tuple-element.6), channel_id=4, replica_groups=mesh['seg_hi'=4,'seg_lo'=4,'exp_y'=4,'exp_x'=4,'exp_core'=2] {'seg_hi'}, dimensions={0}, use_global_device_ids=true | all-gather | bytes 655360 | tf_op jit(solution)/shard_map/all_gather | solution.py:130
  140.3 1.2 multiply_reduce_fusion
  141.5 1.0 fusion.48
  142.6 0.9 bitcast_convert_fusion
  143.5 1.2 fusion.1
  144.8 1.3 fusion.10
  146.7 1.0 copy.191
  147.7 1.1 fusion.3
  148.9 2.2 %multiply_convert_fusion.1 = bf16[2,512,512]{2,1,0:T(8,128)(2,1)S(1)} fusion(f32[2,2,512,512]{3,2,0,1:T(8,128)} %copy-done, bf16[2,512,128]{1,2,0:T(8,128)(2,1)S(1)} %copy-done.8, bf16[2,512,256]{2,1,0:T(8,128)(2,1)S(1)} %bitcast.139), kind=kOutput, calls=%fused_computation.4 | convolution fusion | flops 135266304 | bytes 3670016 | tf_op jit(solution)/shard_map/btf,bsf->bts/dot_general | solution.py:145
  152.6 1.0 copy.188
  153.6 1.3 convolution_multiply_fusion.5
  156.1 0.9 pad_maximum_fusion.1
  157.0 1.0 copy.166
  (117 shorter events, 10.3 us)
Async XLA Ops:
  0.6 59.0 %copy-start.3 = (bf16[1024,256]{1,0:T(8,128)(2,1)S(1)}, bf16[1024,256]{1,0:T(8,128)(2,1)}, u32[]{:S(2)}) copy-start(bf16[1024,256]{1,0:T(8,128)(2,1)} %param.6) | copy-start | bytes 1572868
  25.9 36.9 %copy-start.4 = (bf16[1024,256]{1,0:T(8,128)(2,1)S(1)}, bf16[1024,256]{1,0:T(8,128)(2,1)}, u32[]{:S(2)}) copy-start(bf16[1024,256]{1,0:T(8,128)(2,1)} %param.7) | copy-start | bytes 1572868
  59.6 6.0 %copy-start.11 = (bf16[1,2,128,128]{3,2,1,0:T(8,128)(2,1)}, bf16[1,2,128,128]{3,2,1,0:T(8,128)(2,1)S(1)}, u32[]{:S(2)}) copy-start(bf16[1,2,128,128]{3,2,1,0:T(8,128)(2,1)S(1)} %fusion.46) | copy-start | bytes 196612
  59.9 3.3 %copy-start.17 = (bf16[1024,256]{1,0:T(8,128)(2,1)S(1)}, bf16[1024,256]{1,0:T(8,128)(2,1)}, u32[]{:S(2)}) copy-start(bf16[1024,256]{1,0:T(8,128)(2,1)} %param.11) | copy-start | bytes 1572868
  60.0 4.2 %copy-start.20 = (f32[256]{0:T(256)S(1)}, f32[256]{0:T(256)}, u32[]{:S(2)}) copy-start(f32[256]{0:T(256)} %param.10) | copy-start | bytes 3076
  60.1 4.2 %copy-start.2 = (bf16[1024,256]{1,0:T(8,128)(2,1)S(1)}, bf16[1024,256]{1,0:T(8,128)(2,1)}, u32[]{:S(2)}) copy-start(bf16[1024,256]{1,0:T(8,128)(2,1)} %param.8) | copy-start | bytes 1572868
  60.9 1.9 %copy-start = (f32[2,2,512,512]{3,2,0,1:T(8,128)}, f32[2,2,512,512]{3,2,0,1:T(8,128)S(1)}, u32[]{:S(2)}) copy-start(f32[2,2,512,512]{3,2,0,1:T(8,128)S(1)} %exponential_select_fusion) | copy-start | bytes 12582916
  64.2 1.3 copy-start.9
  69.9 23.5 %copy-start.10 = (bf16[2,512,128]{1,2,0:T(8,128)(2,1)}, bf16[2,512,128]{1,2,0:T(8,128)(2,1)S(1)}, u32[]{:S(2)}) copy-start(bf16[2,512,128]{1,2,0:T(8,128)(2,1)S(1)} %copy.223) | copy-start | bytes 786436
  95.9 0.7 copy-start.7
  96.4 17.6 %copy-start.18 = (f32[2,1,128,128]{3,2,1,0:T(8,128)}, f32[2,1,128,128]{3,2,1,0:T(8,128)S(1)}, u32[]{:S(2)}) copy-start(f32[2,1,128,128]{3,2,1,0:T(8,128)S(1)} %convolution_bitcast_fusion) | copy-start | bytes 393220
  97.1 16.9 %copy-start.19 = (f32[2,1,128,128]{3,2,1,0:T(8,128)}, f32[2,1,128,128]{3,2,1,0:T(8,128)S(1)}, u32[]{:S(2)}) copy-start(f32[2,1,128,128]{3,2,1,0:T(8,128)S(1)} %convolution_bitcast_fusion.1) | copy-start | bytes 393220
  140.3 5.7 %copy-start.5 = (bf16[1024,256]{1,0:T(8,128)(2,1)S(1)}, bf16[1024,256]{1,0:T(8,128)(2,1)}, u32[]{:S(2)}) copy-start(bf16[1024,256]{1,0:T(8,128)(2,1)} %param.7) | copy-start | bytes 1572868
  142.6 4.1 %copy-start.13 = (bf16[1,2,128,128]{3,2,1,0:T(8,128)(2,1)}, bf16[1,2,128,128]{3,2,1,0:T(8,128)(2,1)S(1)}, u32[]{:S(2)}) copy-start(bf16[1,2,128,128]{3,2,1,0:T(8,128)(2,1)S(1)} %fusion.48) | copy-start | bytes 196612
  146.0 2.8 %copy-start.8 = (bf16[2,512,128]{1,2,0:T(8,128)(2,1)S(1)}, bf16[2,512,128]{1,2,0:T(8,128)(2,1)}, u32[]{:S(2)}) copy-start(bf16[2,512,128]{1,2,0:T(8,128)(2,1)} %copy-done.7) | copy-start | bytes 786436
  146.7 4.7 %copy-start.14 = (bf16[1,2,128,128]{3,2,1,0:T(8,128)(2,1)S(1)}, bf16[1,2,128,128]{3,2,1,0:T(8,128)(2,1)}, u32[]{:S(2)}) copy-start(bf16[1,2,128,128]{3,2,1,0:T(8,128)(2,1)} %copy-done.13) | copy-start | bytes 196612
  147.7 4.0 %copy-start.1 = (f32[2,2,512,512]{3,2,0,1:T(8,128)S(1)}, f32[2,2,512,512]{3,2,0,1:T(8,128)}, u32[]{:S(2)}) copy-start(f32[2,2,512,512]{3,2,0,1:T(8,128)} %copy-done) | copy-start | bytes 12582916
  151.7 1.9 %copy-start.12 = (bf16[1,2,128,128]{3,2,1,0:T(8,128)(2,1)S(1)}, bf16[1,2,128,128]{3,2,1,0:T(8,128)(2,1)}, u32[]{:S(2)}) copy-start(bf16[1,2,128,128]{3,2,1,0:T(8,128)(2,1)} %copy-done.11) | copy-start | bytes 196612
  152.2 2.7 %copy-start.6 = (bf16[1024,256]{1,0:T(8,128)(2,1)S(1)}, bf16[1024,256]{1,0:T(8,128)(2,1)}, u32[]{:S(2)}) copy-start(bf16[1024,256]{1,0:T(8,128)(2,1)} %param.7) | copy-start | bytes 1572868
  153.6 3.4 %copy-start.15 = (bf16[2,512,128]{1,2,0:T(8,128)(2,1)S(1)}, bf16[2,512,128]{1,2,0:T(8,128)(2,1)}, u32[]{:S(2)}) copy-start(bf16[2,512,128]{1,2,0:T(8,128)(2,1)} %get-tuple-element.27) | copy-start | bytes 786436
  153.6 3.4 %copy-start.16 = (bf16[2,512,128]{1,2,0:T(8,128)(2,1)S(1)}, bf16[2,512,128]{1,2,0:T(8,128)(2,1)}, u32[]{:S(2)}) copy-start(bf16[2,512,128]{1,2,0:T(8,128)(2,1)} %get-tuple-element.32) | copy-start | bytes 786436
